TPU v7x, 128 devices: a whole 4x4x4 slice. The times are simulated.
128 devices in a mesh: req: 8 (over y, core), exp: 16 (over z, x).
Axes of the slice: x: 4, y: 4, z: 4, core: 2. Of those that a mesh axis runs over, the one named last changes fastest.
Arguments:
- queries: bfloat16 [16, 512, 2048], P('req', None, 'exp'), may hold values from -40 to 40
- new_entries: bfloat16 [16, 2, 512, 2048], P('req', None, None, 'exp'), may hold values from -40 to 40
- cache_entries: bfloat16 [16, 2, 4096, 2048], P('req', None, None, 'exp'), may hold values from -6 to 6
- cache_lengths: int32 [16], P('req'), may hold values from 1 to 4096, 32768 in all
- out_proj: bfloat16 [2048, 2048], P('exp'), may hold values from -0.125 to 0.125
- residual: bfloat16 [8192, 2048], P(('req', 'exp')), may hold values from -40 to 40
- norm_gain: float32 [2048], replicated, may hold values from 0.1 to 1.9
- routes: int32 [8192, 8], P(('req', 'exp')), may hold values from 0 to 63, all different within a row; in each aligned block of 64 rows (0 to 63, 64 to 127, ...) at most 10 rows name the same one
- gate_weights: float32 [8192, 8], P(('req', 'exp')), may hold values from 0.1 to 0.6
- expert_in: bfloat16 [2, 2048, 65536], P(None, None, ('req', 'exp')), may hold values from -0.125 to 0.125
- expert_down: bfloat16 [65536, 2048], P(('req', 'exp')), may hold values from -0.1875 to 0.1875
Outputs:
- attended: bfloat16 [8192, 2048], P(('req', 'exp'))
- expert_out: bfloat16 [8192, 2048], P(('req', 'exp'))
Inputs may be any that keep to these rules, and one draw needn't show every extreme that they name: `cache_lengths`: the lengths add up to 32768 and one is exactly 4096. `routes`: each row names 8 different experts; within the rows of one device (aligned blocks of 64 rows) no expert is named more than 10 times, a bound that some block reaches.
All inputs are finite; a program needn't handle non-finite values. No bound on the sum of `cache_lengths` on one device may be relied on, other than what follows from the above.
Results may differ from a plain program's by a relative error of at most 0.0085.
Values may be sent and summed in bfloat16 or wider, within the bound.
No kernel may reach another device: no remote copies, remote signals or barrier semaphores. Data moves between devices by JAX's collectives and lax.ppermute only.
A program may use at most 128 MiB of HBM per device.

v0:
```python
import jax
import jax.numpy as jnp
from jax import lax
from jax.sharding import PartitionSpec as P

HD = 128
EXPERTS = 64
FF = 1024
TOP = 8


def local(
    queries,
    new_entries,
    cache_entries,
    cache_lengths,
    out_proj,
    residual,
    norm_gain,
    routes,
    gate_weights,
    expert_in,
    expert_down,
):
    req_local, new_len, width_local = queries.shape
    heads_local = width_local // HD
    cache_len = cache_entries.shape[2]
    tok_local = residual.shape[0]
    model_width = residual.shape[1]

    def attend_request(packed):
        query_rows, new_rows, cache_rows, length = packed
        query_heads = query_rows.reshape(new_len, heads_local, HD)
        cache_keys = cache_rows[0].reshape(cache_len, heads_local, HD)
        cache_vals = cache_rows[1].reshape(cache_len, heads_local, HD)
        new_keys = new_rows[0].reshape(new_len, heads_local, HD)
        new_vals = new_rows[1].reshape(new_len, heads_local, HD)
        scale = HD ** (-0.5)
        cache_scores = (
            jnp.einsum("thd,jhd->htj", query_heads, cache_keys, preferred_element_type=jnp.float32)
            * scale
        )
        new_scores = (
            jnp.einsum("thd,jhd->htj", query_heads, new_keys, preferred_element_type=jnp.float32)
            * scale
        )
        cache_valid = jnp.arange(cache_len, dtype=jnp.int32) < length
        causal = (
            jnp.arange(new_len, dtype=jnp.int32)[None, :]
            <= jnp.arange(new_len, dtype=jnp.int32)[:, None]
        )
        scores = jnp.concatenate(
            [
                jnp.where(cache_valid[None, None, :], cache_scores, -1e30),
                jnp.where(causal[None, :, :], new_scores, -1e30),
            ],
            axis=-1,
        )
        peak = jnp.max(scores, axis=-1, keepdims=True)
        weights = jnp.exp(scores - peak)
        denoms = jnp.sum(weights, axis=-1)
        weights_bf = weights.astype(jnp.bfloat16)
        all_vals = jnp.concatenate([cache_vals, new_vals], axis=0)
        mixed = jnp.einsum("htj,jhd->thd", weights_bf, all_vals, preferred_element_type=jnp.float32)
        mixed = mixed / jnp.transpose(denoms)[:, :, None]
        return mixed.astype(jnp.bfloat16).reshape(new_len, width_local)

    attention = lax.map(attend_request, (queries, new_entries, cache_entries, cache_lengths))
    attention = attention.reshape(req_local * new_len, width_local)
    projected = lax.psum_scatter(
        jnp.dot(attention, out_proj, preferred_element_type=jnp.float32),
        "exp",
        scatter_dimension=0,
        tiled=True,
    )
    hidden = residual.astype(jnp.float32) + projected
    attended = hidden.astype(jnp.bfloat16)
    mean_square = jnp.mean(hidden * hidden, axis=-1, keepdims=True)
    normed = (hidden * lax.rsqrt(mean_square + 1e-05) * norm_gain).astype(jnp.bfloat16)
    req_count = lax.axis_size("req")
    exp_count = lax.axis_size("exp")
    devices = req_count * exp_count
    half_units = FF // 2
    pieces = expert_in.shape[2] // half_units
    capacity = max(2, tok_local * TOP * 5 // (EXPERTS * 4))
    flat_routes = routes.reshape(-1)
    onehot = (flat_routes[:, None] == jnp.arange(EXPERTS, dtype=jnp.int32)[None, :]).astype(
        jnp.int32
    )
    slot_index = jnp.sum(jnp.cumsum(onehot, axis=0) * onehot, axis=1) - 1
    positions = flat_routes * capacity + slot_index
    slot_rows = (
        jnp.zeros((EXPERTS * capacity, model_width), jnp.bfloat16)
        .at[positions]
        .set(jnp.repeat(normed, TOP, axis=0))
    )
    outgoing = jnp.repeat(slot_rows.reshape(EXPERTS, capacity, model_width), 2, axis=0)
    outgoing = outgoing.reshape(devices, pieces, capacity, model_width)
    arrived = lax.all_to_all(outgoing, ("req", "exp"), split_axis=0, concat_axis=0, tiled=True)
    sources = arrived.shape[0]
    items = arrived.shape[2]
    rows = arrived[:, 0].reshape(sources * items, model_width)
    gate_part = jnp.dot(rows, expert_in[0, :, 0:half_units], preferred_element_type=jnp.float32)
    up_part = jnp.dot(rows, expert_in[1, :, 0:half_units], preferred_element_type=jnp.float32)
    inner = (jax.nn.silu(gate_part) * up_part).astype(jnp.bfloat16)
    half_out = jnp.dot(inner, expert_down, preferred_element_type=jnp.float32).astype(jnp.bfloat16)
    outputs = [half_out.reshape(sources, items, model_width)]
    returned = lax.all_to_all(
        jnp.stack(outputs, axis=1), ("req", "exp"), split_axis=0, concat_axis=0, tiled=True
    )
    halves = returned.reshape(EXPERTS, 2, capacity, model_width)
    summed = (halves[:, 0].astype(jnp.float32) + halves[:, 1].astype(jnp.float32)).reshape(
        EXPERTS * capacity, model_width
    )
    picked = summed[positions] * gate_weights.reshape(-1)[:, None]
    expert_out = jnp.sum(picked.reshape(tok_local, TOP, model_width), axis=1).astype(jnp.bfloat16)
    return (attended, expert_out)


def solution(mesh):
    return jax.shard_map(
        local,
        mesh=mesh,
        in_specs=(
            P("req", None, "exp"),
            P("req", None, None, "exp"),
            P("req", None, None, "exp"),
            P("req"),
            P("exp", None),
            P(("req", "exp"), None),
            P(),
            P(("req", "exp"), None),
            P(("req", "exp"), None),
            P(None, None, ("req", "exp")),
            P(("req", "exp"), None),
        ),
        out_specs=(P(("req", "exp"), None), P(("req", "exp"), None)),
        check_vma=False,
    )
```

profile of v0, /device:TPU:37, one launch (start us, length us, event | category | flops | bytes accessed | tf_op | source)
XLA Modules:
  0.0 451.6 jit_solution(18325572295595590617)
XLA Ops:
  7.2 38.5 %while.10 = (s32[]{:T(128)}, bf16[2,512,128]{2,1,0:T(8,128)(2,1)S(1)}, bf16[2,2,4096,128]{3,2,1,0:T(8,128)(2,1)}, bf16[2,2,512,128]{3,2,1,0:T(8,128)(2,1)}, s32[...) while((s32[]{:T(128)}, bf16[2,512,128]{2,1,0:T(8,128)(2,1)S(1)}, ...), condition=%wide.region_4.5_spmd, body=%wide.region_0.4_spmd.sunk | while | flops 1231948800 | bytes 67530928 | solution.py:68
  10.6 5.9 %fusion.63 = (f32[512]{0:T(512)S(1)}, f32[512,4096]{1,0:T(8,128)}) fusion(bf16[2,2,4096,128]{3,2,1,0:T(8,128)(2,1)} %get-tuple-element.118, s32[]{:T(128)S(6)} %copy.48, bf16[2,512,128]{2,1,0:T(8,128)(2,1)} %get-tuple-element.121, pred[4096]{0:T(1024)(128)(4,1)S(1)} %iota_compare_fusion.5), kind=kOutput, calls=%fused_computation.70.clone.1 | convolution fusion | flops 543161856 | bytes 9575424 | tf_op jit(solution)/shard_map/while/body/eval_jaxpr/thd,jhd->htj/dot_general | solution.py:40
  18.8 4.5 %fusion.64 = f32[512]{0:T(512)S(1)} fusion(f32[1,512,512]{2,1,0:T(8,128)S(1)} %bitcast.147, f32[1,512,4096]{2,1,0:T(8,128)} %bitcast.143, f32[512]{0:T(512)S(1)} %reduce_max.27), kind=kLoop, calls=%fused_computation.7.clone.1 | loop fusion | flops 7077376 | bytes 9441280 | tf_op jit(solution)/shard_map/while/body/eval_jaxpr/reduce_sum | solution.py:61
  24.6 1.8 fusion.65
  29.8 5.9 %fusion.63 = (f32[512]{0:T(512)S(1)}, f32[512,4096]{1,0:T(8,128)}) fusion(bf16[2,2,4096,128]{3,2,1,0:T(8,128)(2,1)} %get-tuple-element.118, s32[]{:T(128)S(6)} %copy.48, bf16[2,512,128]{2,1,0:T(8,128)(2,1)} %get-tuple-element.121, pred[4096]{0:T(1024)(128)(4,1)S(1)} %iota_compare_fusion.5), kind=kOutput, calls=%fused_computation.70.clone.1 | convolution fusion | flops 543161856 | bytes 9575424 | tf_op jit(solution)/shard_map/while/body/eval_jaxpr/thd,jhd->htj/dot_general | solution.py:40
  37.9 4.5 %fusion.64 = f32[512]{0:T(512)S(1)} fusion(f32[1,512,512]{2,1,0:T(8,128)S(1)} %bitcast.147, f32[1,512,4096]{2,1,0:T(8,128)} %bitcast.143, f32[512]{0:T(512)S(1)} %reduce_max.27), kind=kLoop, calls=%fused_computation.7.clone.1 | loop fusion | flops 7077376 | bytes 9441280 | tf_op jit(solution)/shard_map/while/body/eval_jaxpr/reduce_sum | solution.py:61
  43.7 1.8 fusion.65
  45.7 5.5 %fusion.50 = f32[1024,2048]{1,0:T(8,128)} fusion(bf16[1024,128]{1,0:T(8,128)(2,1)S(1)} %bitcast.149, bf16[128,2048]{1,0:T(8,128)(2,1)} %param.17), kind=kOutput, calls=%fused_computation.72 | convolution fusion | flops 536870912 | bytes 9175040 | tf_op jit(solution)/shard_map/dot_general | solution.py:71
  54.0 82.0 %reduce-scatter.2.cloned.1.call-done = f32[64,2048]{1,0:T(8,128)} async-done(((f32[1024,2048]{1,0:T(8,128)}), f32[64,2048]{1,0:T(8,128)}) %reduce-scatter.2.cloned.1.call-update) | async-done | bytes 524304 | tf_op jit(solution)/shard_map/reduce_scatter | solution.py:70
  137.3 1.8 multiply_convert_fusion
  139.1 5.4 %scatter_custom_fusion = bf16[640,2048]{1,0:T(8,128)(2,1)} fusion(s32[512]{0:T(512)S(1)} %bitcast.150, bf16[]{:T(256)} %constant.20.clone.1, bf16[64,2048]{1,0:T(8,128)(2,1)S(1)} %get-tuple-element.51), kind=kCustom, calls=%fused_computation.46 | custom fusion | bytes 2883586 | tf_op jit(solution)/shard_map/scatter | solution.py:95
  144.4 5.4 %reshape.304 = bf16[64,10,2048]{2,1,0:T(8,128)(2,1)} reshape(bf16[640,2048]{1,0:T(8,128)(2,1)} %scatter_custom_fusion) | data formatting | bytes 5242880 | tf_op jit(solution)/shard_map/reshape | solution.py:97
  149.8 6.8 %broadcast_in_dim.45 = bf16[64,2,10,2048]{3,2,1,0:T(8,128)(2,1)} broadcast(bf16[64,10,2048]{2,1,0:T(8,128)(2,1)} %reshape.304), dimensions={0,2,3} | broadcast | bytes 7864320 | tf_op jit(solution)/shard_map/broadcast_in_dim | solution.py:97
  156.6 106.3 %all_to_all.10 = bf16[128,1,10,2048]{3,2,1,0:T(8,128)(2,1)} all-to-all(bf16[128,1,10,2048]{3,2,1,0:T(8,128)(2,1)} %bitcast.146), channel_id=1, replica_groups=mesh['req'=8,'exp'=16] {'req','exp'}, dimensions={0} | all-to-all | bytes 10485760 | tf_op jit(solution)/shard_map/all_to_all | solution.py:99
  262.8 9.8 %reshape_squeeze.3 = bf16[1280,2048]{1,0:T(8,128)(2,1)} reshape(bf16[128,1,10,2048]{3,2,1,0:T(8,128)(2,1)} %all_to_all.10) | data formatting | bytes 10485760 | tf_op jit(solution)/shard_map/reshape;squeeze | solution.py:102
  272.7 7.5 %fusion.33 = f32[1280,512]{1,0:T(8,128)} fusion(bf16[1280,2048]{1,0:T(8,128)(2,1)} %reshape_squeeze.3, bf16[2,2048,512]{2,1,0:T(8,128)(2,1)} %param.22), kind=kOutput, calls=%fused_computation.44 | convolution fusion | flops 2684354560 | bytes 9961472 | tf_op jit(solution)/shard_map/dot_general | solution.py:103
  280.2 10.3 %convolution_convert_fusion = bf16[1280,2048]{1,0:T(8,128)(2,1)} fusion(bf16[512,2048]{1,0:T(8,128)(2,1)S(1)} %copy-done, bf16[1280,2048]{1,0:T(8,128)(2,1)} %reshape_squeeze.3, f32[1280,512]{1,0:T(8,128)} %fusion.33, bf16[2,2048,512]{2,1,0:T(8,128)(2,1)} %param.22), kind=kOutput, calls=%fused_computation.36 | convolution fusion | flops 5375262720 | bytes 17301504 | tf_op jit(solution)/shard_map/dot_general | solution.py:106
  290.6 9.5 %stack_reshape.3 = bf16[128,1,10,2048]{3,2,0,1:T(8,128)(2,1)} reshape(bf16[1280,2048]{1,0:T(8,128)(2,1)} %convolution_convert_fusion) | data formatting | bytes 10485760 | tf_op jit(solution)/shard_map/stack;reshape | solution.py:109
  300.1 7.1 %all-to-all-start.1 = ((bf16[128,1,10,2048]{3,2,1,0:T(8,128)(2,1)}), bf16[128,1,10,2048]{3,2,1,0:T(8,128)(2,1)}, u32[]{:S(2)}, u32[]{:S(2)}) async-start(bf16[128,1,10,2048]{3,2,1,0:T(8,128)(2,1)} %bitcast.145), calls=%async_computation.2 | async-start | bytes 16777216 | tf_op jit(solution)/shard_map/all_to_all | solution.py:108
  307.3 109.1 %all-to-all-done.1 = bf16[128,1,10,2048]{3,2,1,0:T(8,128)(2,1)} async-done(((bf16[128,1,10,2048]{3,2,1,0:T(8,128)(2,1)}), bf16[128,1,10,2048]{3,2,1,0:T(8,128)(2,1)}, u32[]{:S(2)}, u32[]{:S(2)}) %all-to-all-start.1) | async-done | bytes 5242912 | tf_op jit(solution)/shard_map/all_to_all | solution.py:108
  416.4 8.6 %convert_add_fusion = f32[64,1,10,2048]{3,2,0,1:T(8,128)} fusion(bf16[64,2,10,2048]{3,2,1,0:T(8,128)(2,1)} %bitcast.24), kind=kLoop, calls=%fused_computation.35 | loop fusion | flops 3932160 | bytes 10485760 | tf_op jit(solution)/shard_map/add | solution.py:112
  425.0 7.3 %add.67 = f32[640,2048]{1,0:T(8,128)} reshape(f32[64,1,10,2048]{3,2,0,1:T(8,128)} %convert_add_fusion) | data formatting | bytes 10485760 | tf_op jit(solution)/shard_map/add | solution.py:112
  432.4 8.0 %gather_fusion = f32[512,2048]{1,0:T(8,128)} fusion(f32[640,2048]{1,0:T(8,128)} %add.67, s32[1024]{0:T(1024)S(1)} %pad_clamp_fusion), kind=kCustom, calls=%fused_computation | custom fusion | bytes 8390656 | tf_op jit(solution)/shard_map/gather | solution.py:115
  440.4 4.4 fusion.30
  (51 shorter events, 18.1 us)
Async XLA Ops:
  7.2 273.1 %copy-start = (bf16[512,2048]{1,0:T(8,128)(2,1)S(1)}, bf16[512,2048]{1,0:T(8,128)(2,1)}, u32[]{:S(2)}) copy-start(bf16[512,2048]{1,0:T(8,128)(2,1)} %param.23) | copy-start | bytes 6291460
  7.2 128.8 %reduce-scatter.2.cloned.1.call-start = ((), (), s32[]{:S(2)}) async-start(), calls=%async_computation.3 | async-start | bytes 8912896 | tf_op jit(solution)/shard_map/reduce_scatter | solution.py:70
  18.7 5.8 %copy-start.1 = (f32[512,4096]{1,0:T(8,128)S(1)}, f32[512,4096]{1,0:T(8,128)}, u32[]{:S(2)}) copy-start(f32[512,4096]{1,0:T(8,128)} %get-tuple-element.95) | copy-start | bytes 25165828 | tf_op jit(solution)/shard_map/while
  37.9 5.8 %copy-start.1 = (f32[512,4096]{1,0:T(8,128)S(1)}, f32[512,4096]{1,0:T(8,128)}, u32[]{:S(2)}) copy-start(f32[512,4096]{1,0:T(8,128)} %get-tuple-element.95) | copy-start | bytes 25165828 | tf_op jit(solution)/shard_map/while
  51.2 0.7 copy-start.3
  51.2 84.8 %copy-start.2 = (bf16[64,2048]{1,0:T(8,128)(2,1)S(1)}, bf16[64,2048]{1,0:T(8,128)(2,1)}, u32[]{:S(2)}) copy-start(bf16[64,2048]{1,0:T(8,128)(2,1)} %param.18) | copy-start | bytes 786436
  51.2 86.0 %copy-start.4 = (f32[2048]{0:T(1024)S(1)}, f32[2048]{0:T(1024)}, u32[]{:S(2)}) copy-start(f32[2048]{0:T(1024)} %param.19) | copy-start | bytes 24580
  300.1 7.1 %copy-start.5 = (f32[64,8]{0,1:T(8,128)S(1)}, f32[64,8]{0,1:T(8,128)}, u32[]{:S(2)}) copy-start(f32[64,8]{0,1:T(8,128)} %param.21) | copy-start | bytes 6148
  300.1 116.3 %all-to-all-start.1 = ((bf16[128,1,10,2048]{3,2,1,0:T(8,128)(2,1)}), bf16[128,1,10,2048]{3,2,1,0:T(8,128)(2,1)}, u32[]{:S(2)}, u32[]{:S(2)}) async-start(bf16[128,1,10,2048]{3,2,1,0:T(8,128)(2,1)} %bitcast.145), calls=%async_computation.2 | async-start | bytes 16777216 | tf_op jit(solution)/shard_map/all_to_all | solution.py:108
Sparse Core Ops, SparseCore 0:
  51.3 84.6 reduce-scatter.1
where the time goes:
time: 453 us; the launch traced here: 452 us
  waiting for transfers between devices  191 us (42%)
  blocking collectives  106 us (23%)
  local copies, waits for them, and re-layouts  63.5 us (14%)
  matrix products  41.5 us (9%)
  other arithmetic  27.7 us (6%)
  between operations  14.1 us (3%)
  starting transfers between devices  7.13 us (2%)
    all_to_all x1, waiting for transfers between devices, local(): lax.all_to_all(jnp.stack(outputs, axis=1), ('req', 'exp'), split_axis=0,...  109 us
    all_to_all x1, blocking collectives, local(): lax.all_to_all(outgoing, ('req', 'exp'), split_axis=0, concat_axis=0, til...  106 us
    reduce_scatter x1, waiting for transfers between devices, local(): lax.psum_scatter(jnp.dot(attention, out_proj, preferred_element_type=jnp....  82 us
    dot_general x2, matrix products, attend_request(): jnp.einsum('thd,jhd->htj', query_heads, cache_keys, preferred_element_typ...  11.8 us
    dot_general x1, matrix products, local(): jnp.dot(inner, expert_down, preferred_element_type=jnp.float32)  10.3 us
    another operation x1, local copies, waits for them, and re-layouts, local(): rows = arrived[:, 0].reshape(sources * items, model_width)  9.85 us
    another operation x1, local copies, waits for them, and re-layouts, local(): jnp.stack(outputs, axis=1)  9.55 us
  transfers between devices with their start and end apart: 2, of which 2 were waited for; matrix products, arithmetic and copies ran while one was open for 0% of the time, Pallas kernels for 0%

commit v1 on v0

--- a/solution.py
+++ b/solution.py
@@ -68,12 +68,12 @@
     attention = lax.map(attend_request, (queries, new_entries, cache_entries, cache_lengths))
     attention = attention.reshape(req_local * new_len, width_local)
     projected = lax.psum_scatter(
-        jnp.dot(attention, out_proj, preferred_element_type=jnp.float32),
+        jnp.dot(attention, out_proj, preferred_element_type=jnp.float32).astype(jnp.bfloat16),
         "exp",
         scatter_dimension=0,
         tiled=True,
     )
-    hidden = residual.astype(jnp.float32) + projected
+    hidden = residual.astype(jnp.float32) + projected.astype(jnp.float32)
     attended = hidden.astype(jnp.bfloat16)
     mean_square = jnp.mean(hidden * hidden, axis=-1, keepdims=True)
     normed = (hidden * lax.rsqrt(mean_square + 1e-05) * norm_gain).astype(jnp.bfloat16)

time: 453 us -> 444 us (0.980)
  waiting for transfers between devices: 191 us -> 184 us
    reduce_scatter x1, waiting for transfers between devices: 82 us -> 75.1 us  [local(): lax.psum_scatter(jnp.dot(attention, out_proj, preferred_element_type=jnp....]
where the time goes in v1:
time: 444 us; the launch traced here: 443 us
  waiting for transfers between devices  184 us (41%)
  blocking collectives  106 us (24%)
  local copies, waits for them, and re-layouts  62.8 us (14%)
  matrix products  40.3 us (9%)
  other arithmetic  27.6 us (6%)
  between operations  14.1 us (3%)
  starting transfers between devices  7.13 us (2%)
    all_to_all x1, waiting for transfers between devices, local(): lax.all_to_all(jnp.stack(outputs, axis=1), ('req', 'exp'), split_axis=0,...  109 us
    all_to_all x1, blocking collectives, local(): lax.all_to_all(outgoing, ('req', 'exp'), split_axis=0, concat_axis=0, til...  106 us
    reduce_scatter x1, waiting for transfers between devices, local(): lax.psum_scatter(jnp.dot(attention, out_proj, preferred_element_type=jnp....  75.1 us
    dot_general x2, matrix products, attend_request(): jnp.einsum('thd,jhd->htj', query_heads, cache_keys, preferred_element_typ...  11.8 us
    dot_general x1, matrix products, local(): jnp.dot(inner, expert_down, preferred_element_type=jnp.float32)  10.3 us
    another operation x1, local copies, waits for them, and re-layouts, local(): rows = arrived[:, 0].reshape(sources * items, model_width)  9.85 us
    another operation x1, local copies, waits for them, and re-layouts, local(): jnp.stack(outputs, axis=1)  9.55 us
    reduce_sum x2, other arithmetic, attend_request(): denoms = jnp.sum(weights, axis=-1)  9.03 us
  transfers between devices with their start and end apart: 2, of which 2 were waited for; matrix products, arithmetic and copies ran while one was open for 0% of the time, Pallas kernels for 0%

profile of v1, /device:TPU:37, one launch (start us, length us, event | category | flops | bytes accessed | tf_op | source)
XLA Modules:
  0.0 442.5 jit_solution(12398747678377036752)
XLA Ops:
  7.2 38.5 %while.10 = (s32[]{:T(128)}, bf16[2,512,128]{2,1,0:T(8,128)(2,1)S(1)}, bf16[2,2,4096,128]{3,2,1,0:T(8,128)(2,1)}, bf16[2,2,512,128]{3,2,1,0:T(8,128)(2,1)}, s32[...) while((s32[]{:T(128)}, bf16[2,512,128]{2,1,0:T(8,128)(2,1)S(1)}, ...), condition=%wide.region_4.5_spmd, body=%wide.region_0.4_spmd.sunk | while | flops 1231948800 | bytes 67530928 | solution.py:68
  10.6 5.9 %fusion.62 = (f32[512]{0:T(512)S(1)}, f32[512,4096]{1,0:T(8,128)}) fusion(bf16[2,2,4096,128]{3,2,1,0:T(8,128)(2,1)} %get-tuple-element.118, s32[]{:T(128)S(6)} %copy.48, bf16[2,512,128]{2,1,0:T(8,128)(2,1)} %get-tuple-element.121, pred[4096]{0:T(1024)(128)(4,1)S(1)} %iota_compare_fusion.5), kind=kOutput, calls=%fused_computation.71.clone.1 | convolution fusion | flops 543161856 | bytes 9575424 | tf_op jit(solution)/shard_map/while/body/eval_jaxpr/thd,jhd->htj/dot_general | solution.py:40
  18.8 4.5 %fusion.63 = f32[512]{0:T(512)S(1)} fusion(f32[1,512,512]{2,1,0:T(8,128)S(1)} %bitcast.147, f32[1,512,4096]{2,1,0:T(8,128)} %bitcast.143, f32[512]{0:T(512)S(1)} %reduce_max.27), kind=kLoop, calls=%fused_computation.7.clone.1 | loop fusion | flops 7077376 | bytes 9441280 | tf_op jit(solution)/shard_map/while/body/eval_jaxpr/reduce_sum | solution.py:61
  24.6 1.8 fusion.64
  29.8 5.9 %fusion.62 = (f32[512]{0:T(512)S(1)}, f32[512,4096]{1,0:T(8,128)}) fusion(bf16[2,2,4096,128]{3,2,1,0:T(8,128)(2,1)} %get-tuple-element.118, s32[]{:T(128)S(6)} %copy.48, bf16[2,512,128]{2,1,0:T(8,128)(2,1)} %get-tuple-element.121, pred[4096]{0:T(1024)(128)(4,1)S(1)} %iota_compare_fusion.5), kind=kOutput, calls=%fused_computation.71.clone.1 | convolution fusion | flops 543161856 | bytes 9575424 | tf_op jit(solution)/shard_map/while/body/eval_jaxpr/thd,jhd->htj/dot_general | solution.py:40
  37.9 4.5 %fusion.63 = f32[512]{0:T(512)S(1)} fusion(f32[1,512,512]{2,1,0:T(8,128)S(1)} %bitcast.147, f32[1,512,4096]{2,1,0:T(8,128)} %bitcast.143, f32[512]{0:T(512)S(1)} %reduce_max.27), kind=kLoop, calls=%fused_computation.7.clone.1 | loop fusion | flops 7077376 | bytes 9441280 | tf_op jit(solution)/shard_map/while/body/eval_jaxpr/reduce_sum | solution.py:61
  43.7 1.8 fusion.64
  45.7 4.2 convolution_convert_fusion.1
  52.1 75.1 %reduce-scatter.2.cloned.1.call-done = bf16[64,2048]{1,0:T(8,128)(2,1)} async-done(((bf16[1024,2048]{1,0:T(8,128)(2,1)}), bf16[64,2048]{1,0:T(8,128)(2,1)}) %reduce-scatter.2.cloned.1.call-update) | async-done | bytes 262160 | tf_op jit(solution)/shard_map/reduce_scatter | solution.py:70
  128.3 1.7 multiply_convert_fusion
  130.1 5.4 %scatter_custom_fusion = bf16[640,2048]{1,0:T(8,128)(2,1)} fusion(s32[512]{0:T(512)S(1)} %bitcast.150, bf16[]{:T(256)} %constant.20.clone.1, bf16[64,2048]{1,0:T(8,128)(2,1)S(1)} %get-tuple-element.51), kind=kCustom, calls=%fused_computation.47 | custom fusion | bytes 2883586 | tf_op jit(solution)/shard_map/scatter | solution.py:95
  135.5 5.4 %reshape.304 = bf16[64,10,2048]{2,1,0:T(8,128)(2,1)} reshape(bf16[640,2048]{1,0:T(8,128)(2,1)} %scatter_custom_fusion) | data formatting | bytes 5242880 | tf_op jit(solution)/shard_map/reshape | solution.py:97
  140.8 6.8 %broadcast_in_dim.45 = bf16[64,2,10,2048]{3,2,1,0:T(8,128)(2,1)} broadcast(bf16[64,10,2048]{2,1,0:T(8,128)(2,1)} %reshape.304), dimensions={0,2,3} | broadcast | bytes 7864320 | tf_op jit(solution)/shard_map/broadcast_in_dim | solution.py:97
  147.6 106.2 %all_to_all.10 = bf16[128,1,10,2048]{3,2,1,0:T(8,128)(2,1)} all-to-all(bf16[128,1,10,2048]{3,2,1,0:T(8,128)(2,1)} %bitcast.146), channel_id=1, replica_groups=mesh['req'=8,'exp'=16] {'req','exp'}, dimensions={0} | all-to-all | bytes 10485760 | tf_op jit(solution)/shard_map/all_to_all | solution.py:99
  253.8 9.8 %reshape_squeeze.3 = bf16[1280,2048]{1,0:T(8,128)(2,1)} reshape(bf16[128,1,10,2048]{3,2,1,0:T(8,128)(2,1)} %all_to_all.10) | data formatting | bytes 10485760 | tf_op jit(solution)/shard_map/reshape;squeeze | solution.py:102
  263.7 7.5 %fusion.33 = f32[1280,512]{1,0:T(8,128)} fusion(bf16[1280,2048]{1,0:T(8,128)(2,1)} %reshape_squeeze.3, bf16[2,2048,512]{2,1,0:T(8,128)(2,1)} %param.22), kind=kOutput, calls=%fused_computation.45 | convolution fusion | flops 2684354560 | bytes 9961472 | tf_op jit(solution)/shard_map/dot_general | solution.py:103
  271.2 10.3 %convolution_convert_fusion = bf16[1280,2048]{1,0:T(8,128)(2,1)} fusion(bf16[512,2048]{1,0:T(8,128)(2,1)S(1)} %copy-done, bf16[1280,2048]{1,0:T(8,128)(2,1)} %reshape_squeeze.3, f32[1280,512]{1,0:T(8,128)} %fusion.33, bf16[2,2048,512]{2,1,0:T(8,128)(2,1)} %param.22), kind=kOutput, calls=%fused_computation.36 | convolution fusion | flops 5375262720 | bytes 17301504 | tf_op jit(solution)/shard_map/dot_general | solution.py:106
  281.5 9.5 %stack_reshape.3 = bf16[128,1,10,2048]{3,2,0,1:T(8,128)(2,1)} reshape(bf16[1280,2048]{1,0:T(8,128)(2,1)} %convolution_convert_fusion) | data formatting | bytes 10485760 | tf_op jit(solution)/shard_map/stack;reshape | solution.py:109
  291.1 7.1 %all-to-all-start.1 = ((bf16[128,1,10,2048]{3,2,1,0:T(8,128)(2,1)}), bf16[128,1,10,2048]{3,2,1,0:T(8,128)(2,1)}, u32[]{:S(2)}, u32[]{:S(2)}) async-start(bf16[128,1,10,2048]{3,2,1,0:T(8,128)(2,1)} %bitcast.145), calls=%async_computation.2 | async-start | bytes 16777216 | tf_op jit(solution)/shard_map/all_to_all | solution.py:108
  298.3 109.1 %all-to-all-done.1 = bf16[128,1,10,2048]{3,2,1,0:T(8,128)(2,1)} async-done(((bf16[128,1,10,2048]{3,2,1,0:T(8,128)(2,1)}), bf16[128,1,10,2048]{3,2,1,0:T(8,128)(2,1)}, u32[]{:S(2)}, u32[]{:S(2)}) %all-to-all-start.1) | async-done | bytes 5242912 | tf_op jit(solution)/shard_map/all_to_all | solution.py:108
  407.4 8.6 %convert_add_fusion = f32[64,1,10,2048]{3,2,0,1:T(8,128)} fusion(bf16[64,2,10,2048]{3,2,1,0:T(8,128)(2,1)} %bitcast.24), kind=kLoop, calls=%fused_computation.35 | loop fusion | flops 3932160 | bytes 10485760 | tf_op jit(solution)/shard_map/add | solution.py:112
  416.0 7.3 %add.67 = f32[640,2048]{1,0:T(8,128)} reshape(f32[64,1,10,2048]{3,2,0,1:T(8,128)} %convert_add_fusion) | data formatting | bytes 10485760 | tf_op jit(solution)/shard_map/add | solution.py:112
  423.4 8.0 %gather_fusion = f32[512,2048]{1,0:T(8,128)} fusion(f32[640,2048]{1,0:T(8,128)} %add.67, s32[1024]{0:T(1024)S(1)} %pad_clamp_fusion), kind=kCustom, calls=%fused_computation | custom fusion | bytes 8390656 | tf_op jit(solution)/shard_map/gather | solution.py:115
  431.3 4.4 fusion.30
  (51 shorter events, 17.4 us)
Async XLA Ops:
  7.2 264.0 %copy-start = (bf16[512,2048]{1,0:T(8,128)(2,1)S(1)}, bf16[512,2048]{1,0:T(8,128)(2,1)}, u32[]{:S(2)}) copy-start(bf16[512,2048]{1,0:T(8,128)(2,1)} %param.23) | copy-start | bytes 6291460
  7.2 120.0 %reduce-scatter.2.cloned.1.call-start = ((), (), s32[]{:S(2)}) async-start(), calls=%async_computation.3 | async-start | bytes 4456448 | tf_op jit(solution)/shard_map/reduce_scatter | solution.py:70
  18.7 5.8 %copy-start.1 = (f32[512,4096]{1,0:T(8,128)S(1)}, f32[512,4096]{1,0:T(8,128)}, u32[]{:S(2)}) copy-start(f32[512,4096]{1,0:T(8,128)} %get-tuple-element.95) | copy-start | bytes 25165828 | tf_op jit(solution)/shard_map/while
  37.9 5.8 %copy-start.1 = (f32[512,4096]{1,0:T(8,128)S(1)}, f32[512,4096]{1,0:T(8,128)}, u32[]{:S(2)}) copy-start(f32[512,4096]{1,0:T(8,128)} %get-tuple-element.95) | copy-start | bytes 25165828 | tf_op jit(solution)/shard_map/while
  45.7 4.3 copy-start.3
  49.9 77.3 %copy-start.2 = (bf16[64,2048]{1,0:T(8,128)(2,1)S(1)}, bf16[64,2048]{1,0:T(8,128)(2,1)}, u32[]{:S(2)}) copy-start(bf16[64,2048]{1,0:T(8,128)(2,1)} %param.18) | copy-start | bytes 786436
  49.9 78.4 %copy-start.4 = (f32[2048]{0:T(1024)S(1)}, f32[2048]{0:T(1024)}, u32[]{:S(2)}) copy-start(f32[2048]{0:T(1024)} %param.19) | copy-start | bytes 24580
  291.1 7.1 %copy-start.5 = (f32[64,8]{0,1:T(8,128)S(1)}, f32[64,8]{0,1:T(8,128)}, u32[]{:S(2)}) copy-start(f32[64,8]{0,1:T(8,128)} %param.21) | copy-start | bytes 6148
  291.1 116.3 %all-to-all-start.1 = ((bf16[128,1,10,2048]{3,2,1,0:T(8,128)(2,1)}), bf16[128,1,10,2048]{3,2,1,0:T(8,128)(2,1)}, u32[]{:S(2)}, u32[]{:S(2)}) async-start(bf16[128,1,10,2048]{3,2,1,0:T(8,128)(2,1)} %bitcast.145), calls=%async_computation.2 | async-start | bytes 16777216 | tf_op jit(solution)/shard_map/all_to_all | solution.py:108
Sparse Core Ops, SparseCore 0:
  50.1 77.0 reduce-scatter.1

commit v2 on v0

--- a/solution.py
+++ b/solution.py
@@ -67,12 +67,9 @@
 
     attention = lax.map(attend_request, (queries, new_entries, cache_entries, cache_lengths))
     attention = attention.reshape(req_local * new_len, width_local)
-    projected = lax.psum_scatter(
-        jnp.dot(attention, out_proj, preferred_element_type=jnp.float32),
-        "exp",
-        scatter_dimension=0,
-        tiled=True,
-    )
+    gathered = lax.all_to_all(attention, "exp", 0, 1, tiled=True)
+    full_proj = lax.all_gather(out_proj, "exp", axis=0, tiled=True)
+    projected = jnp.dot(gathered, full_proj, preferred_element_type=jnp.float32)
     hidden = residual.astype(jnp.float32) + projected
     attended = hidden.astype(jnp.bfloat16)
     mean_square = jnp.mean(hidden * hidden, axis=-1, keepdims=True)

time: 453 us -> 403 us (0.89)
  waiting for transfers between devices: 191 us -> 143 us
  other arithmetic: 27.7 us -> 19.6 us
  starting transfers between devices: 7.13 us -> 14.4 us
    reduce_scatter x1 -> x0, waiting for transfers between devices: 82 us -> none  [local(): lax.psum_scatter(jnp.dot(attention, out_proj, preferred_element_type=jnp....]
    all_gather x0 -> x1, waiting for transfers between devices: none -> 28.3 us  [local(): full_proj = lax.all_gather(out_proj, 'exp', axis=0, tiled=True)]
    dot_general x2, matrix products: 3.55 us -> 11.7 us  [attend_request(): jnp.einsum('htj,jhd->thd', weights_bf, all_vals, preferred_element_type=j...]
    all_to_all x0 -> x1, starting transfers between devices: none -> 7.28 us  [local(): gathered = lax.all_to_all(attention, 'exp', 0, 1, tiled=True)]
    dot_general x2, matrix products: 11.8 us -> 5.62 us  [attend_request(): jnp.einsum('thd,jhd->htj', query_heads, cache_keys, preferred_element_typ...]
    reduce_sum x2, other arithmetic: 9.03 us -> 3.3 us  [attend_request(): denoms = jnp.sum(weights, axis=-1)]
    all_to_all x0 -> x1, waiting for transfers between devices: none -> 5.02 us  [local(): gathered = lax.all_to_all(attention, 'exp', 0, 1, tiled=True)]
  transfers between devices with their start and end apart: 2 -> 3, of which waited for: 2 -> 3; matrix products, arithmetic and copies ran while one was open for 0% -> 8% of each run, Pallas kernels for 0% -> 0%
where the time goes in v2:
time: 403 us; the launch traced here: 401 us
  waiting for transfers between devices  143 us (35%)
  blocking collectives  105 us (26%)
  local copies, waits for them, and re-layouts  61.7 us (15%)
  matrix products  43.2 us (11%)
  other arithmetic  19.6 us (5%)
  starting transfers between devices  14.4 us (4%)
  between operations  14.1 us (3%)
    all_to_all x1, waiting for transfers between devices, local(): lax.all_to_all(jnp.stack(outputs, axis=1), ('req', 'exp'), split_axis=0,...  109 us
    all_to_all x1, blocking collectives, local(): lax.all_to_all(outgoing, ('req', 'exp'), split_axis=0, concat_axis=0, til...  105 us
    all_gather x1, waiting for transfers between devices, local(): full_proj = lax.all_gather(out_proj, 'exp', axis=0, tiled=True)  28.3 us
    dot_general x2, matrix products, attend_request(): jnp.einsum('htj,jhd->thd', weights_bf, all_vals, preferred_element_type=j...  11.7 us
    dot_general x1, matrix products, local(): jnp.dot(inner, expert_down, preferred_element_type=jnp.float32)  10.3 us
    another operation x1, local copies, waits for them, and re-layouts, local(): rows = arrived[:, 0].reshape(sources * items, model_width)  9.85 us
    another operation x1, local copies, waits for them, and re-layouts, local(): jnp.stack(outputs, axis=1)  9.55 us
    add x1, other arithmetic, local(): halves[:, 0].astype(jnp.float32) + halves[:, 1].astype(jnp.float32)  8.61 us
  transfers between devices with their start and end apart: 3, of which 3 were waited for; matrix products, arithmetic and copies ran while one was open for 8% of the time, Pallas kernels for 0%

profile of v2, /device:TPU:37, one launch (start us, length us, event | category | flops | bytes accessed | tf_op | source)
XLA Modules:
  0.0 401.2 jit_solution(13641321687438725492)
XLA Ops:
  7.9 33.6 %while.10 = (s32[]{:T(128)}, bf16[2,512,128]{2,1,0:T(8,128)(2,1)}, bf16[2,2,4096,128]{3,2,1,0:T(8,128)(2,1)}, bf16[2,2,512,128]{3,2,1,0:T(8,128)(2,1)}, s32[2]{0...) while((s32[]{:T(128)}, bf16[2,512,128]{2,1,0:T(8,128)(2,1)}, ...), condition=%wide.region_4.5_spmd, body=%wide.region_0.4_spmd.sunk | while | flops 1231948800 | bytes 70676728 | solution.py:68
  9.8 2.8 fusion.63
  14.0 1.7 fusion.64
  18.0 5.9 %fusion.65 = bf16[1,512,128]{1,2,0:T(8,128)(2,1)S(1)} fusion(f32[1,512,1,1,1,1,512]{6,1,5,4,3,2,0:T(8,128)S(1)} %bitcast.157, f32[1,512,1,1,1,1,4096]{6,1,5,4,3,2,0:T(8,128)} %bitcast.153, f32[512]{0:T(512)S(1)} %reduce_max.27, bf16[512,1,128]{2,0,1:T(8,128)(2,1)S(1)} %dynamic-slice_bitcast_fusion.8, ...), kind=kOutput, calls=%fused_computation.19.clone.1 | convolution fusion | flops 613548032 | bytes 10752000 | tf_op jit(solution)/shard_map/while/body/eval_jaxpr/htj,jhd->thd/dot_general | solution.py:64
  26.6 2.8 fusion.63
  34.8 5.9 %fusion.65 = bf16[1,512,128]{1,2,0:T(8,128)(2,1)S(1)} fusion(f32[1,512,1,1,1,1,512]{6,1,5,4,3,2,0:T(8,128)S(1)} %bitcast.157, f32[1,512,1,1,1,1,4096]{6,1,5,4,3,2,0:T(8,128)} %bitcast.153, f32[512]{0:T(512)S(1)} %reduce_max.27, bf16[512,1,128]{2,0,1:T(8,128)(2,1)S(1)} %dynamic-slice_bitcast_fusion.8, ...), kind=kOutput, calls=%fused_computation.19.clone.1 | convolution fusion | flops 613548032 | bytes 10752000 | tf_op jit(solution)/shard_map/while/body/eval_jaxpr/htj,jhd->thd/dot_general | solution.py:64
  41.6 7.3 %all-to-all-start = ((bf16[16,64,128]{2,1,0:T(8,128)(2,1)}), bf16[16,64,128]{2,1,0:T(8,128)(2,1)S(1)}, u32[]{:S(2)}, u32[]{:S(2)}) async-start(bf16[16,64,128]{2,1,0:T(8,128)(2,1)} %bitcast.158), calls=%async_computation | async-start | bytes 524288 | tf_op jit(solution)/shard_map/all_to_all | solution.py:70
  51.0 5.0 %all-to-all-done = bf16[16,64,128]{2,1,0:T(8,128)(2,1)S(1)} async-done(((bf16[16,64,128]{2,1,0:T(8,128)(2,1)}), bf16[16,64,128]{2,1,0:T(8,128)(2,1)S(1)}, u32[]{:S(2)}, u32[]{:S(2)}) %all-to-all-start) | async-done | bytes 262176 | tf_op jit(solution)/shard_map/all_to_all | solution.py:70
  56.0 28.3 %all-gather.2.cloned.1.call-done = bf16[2048,2048]{1,0:T(8,128)(2,1)} async-done(((bf16[128,2048]{1,0:T(8,128)(2,1)}), bf16[2048,2048]{1,0:T(8,128)(2,1)}) %all-gather.2.cloned.1.call-update) | async-done | bytes 8388624 | tf_op jit(solution)/shard_map/all_gather | solution.py:71
  84.3 5.1 %multiply_reduce_fusion = (f32[64]{0:T(128)S(1)}, f32[64,2048]{1,0:T(8,128)S(1)}) fusion(bf16[2048,2048]{1,0:T(8,128)(2,1)} %all-gather.2.cloned.1.call-done, bf16[64,2048]{1,0:T(8,128)(2,1)} %param.18, bf16[16,64,128]{2,1,0:T(8,128)(2,1)S(1)} %all-to-all-done), kind=kOutput, calls=%fused_computation.54 | convolution fusion | flops 537395136 | bytes 9437440 | tf_op jit(solution)/shard_map/dot_general | solution.py:72
  90.2 5.4 %scatter_custom_fusion = bf16[640,2048]{1,0:T(8,128)(2,1)} fusion(s32[512]{0:T(512)S(1)} %bitcast.159, bf16[]{:T(256)} %constant.20.clone.1, bf16[64,2048]{1,0:T(8,128)(2,1)S(1)} %get-tuple-element.51), kind=kCustom, calls=%fused_computation.47 | custom fusion | bytes 2883586 | tf_op jit(solution)/shard_map/scatter | solution.py:92
  95.6 5.4 %reshape.305 = bf16[64,10,2048]{2,1,0:T(8,128)(2,1)} reshape(bf16[640,2048]{1,0:T(8,128)(2,1)} %scatter_custom_fusion) | data formatting | bytes 5242880 | tf_op jit(solution)/shard_map/reshape | solution.py:94
  101.0 6.8 %broadcast_in_dim.45 = bf16[64,2,10,2048]{3,2,1,0:T(8,128)(2,1)} broadcast(bf16[64,10,2048]{2,1,0:T(8,128)(2,1)} %reshape.305), dimensions={0,2,3} | broadcast | bytes 7864320 | tf_op jit(solution)/shard_map/broadcast_in_dim | solution.py:94
  107.7 104.8 %all_to_all.29 = bf16[128,1,10,2048]{3,2,1,0:T(8,128)(2,1)} all-to-all(bf16[128,1,10,2048]{3,2,1,0:T(8,128)(2,1)} %bitcast.155), channel_id=1, replica_groups=mesh['req'=8,'exp'=16] {'req','exp'}, dimensions={0} | all-to-all | bytes 10485760 | tf_op jit(solution)/shard_map/all_to_all | solution.py:96
  212.5 9.8 %reshape_squeeze.3 = bf16[1280,2048]{1,0:T(8,128)(2,1)} reshape(bf16[128,1,10,2048]{3,2,1,0:T(8,128)(2,1)} %all_to_all.29) | data formatting | bytes 10485760 | tf_op jit(solution)/shard_map/reshape;squeeze | solution.py:99
  222.3 7.6 %fusion.33 = f32[1280,512]{1,0:T(8,128)} fusion(bf16[1280,2048]{1,0:T(8,128)(2,1)} %reshape_squeeze.3, bf16[2,2048,512]{2,1,0:T(8,128)(2,1)} %param.22), kind=kOutput, calls=%fused_computation.45 | convolution fusion | flops 2684354560 | bytes 9961472 | tf_op jit(solution)/shard_map/dot_general | solution.py:100
  229.9 10.3 %convolution_convert_fusion = bf16[1280,2048]{1,0:T(8,128)(2,1)} fusion(bf16[512,2048]{1,0:T(8,128)(2,1)S(1)} %copy-done, bf16[1280,2048]{1,0:T(8,128)(2,1)} %reshape_squeeze.3, f32[1280,512]{1,0:T(8,128)} %fusion.33, bf16[2,2048,512]{2,1,0:T(8,128)(2,1)} %param.22), kind=kOutput, calls=%fused_computation.36 | convolution fusion | flops 5375262720 | bytes 17301504 | tf_op jit(solution)/shard_map/dot_general | solution.py:103
  240.2 9.5 %stack_reshape.3 = bf16[128,1,10,2048]{3,2,0,1:T(8,128)(2,1)} reshape(bf16[1280,2048]{1,0:T(8,128)(2,1)} %convolution_convert_fusion) | data formatting | bytes 10485760 | tf_op jit(solution)/shard_map/stack;reshape | solution.py:106
  249.7 7.1 %all-to-all-start.2 = ((bf16[128,1,10,2048]{3,2,1,0:T(8,128)(2,1)}), bf16[128,1,10,2048]{3,2,1,0:T(8,128)(2,1)}, u32[]{:S(2)}, u32[]{:S(2)}) async-start(bf16[128,1,10,2048]{3,2,1,0:T(8,128)(2,1)} %bitcast.154), calls=%async_computation.2 | async-start | bytes 16777216 | tf_op jit(solution)/shard_map/all_to_all | solution.py:105
  256.9 109.1 %all-to-all-done.2 = bf16[128,1,10,2048]{3,2,1,0:T(8,128)(2,1)} async-done(((bf16[128,1,10,2048]{3,2,1,0:T(8,128)(2,1)}), bf16[128,1,10,2048]{3,2,1,0:T(8,128)(2,1)}, u32[]{:S(2)}, u32[]{:S(2)}) %all-to-all-start.2) | async-done | bytes 5242912 | tf_op jit(solution)/shard_map/all_to_all | solution.py:105
  366.1 8.6 %convert_add_fusion = f32[64,1,10,2048]{3,2,0,1:T(8,128)} fusion(bf16[64,2,10,2048]{3,2,1,0:T(8,128)(2,1)} %bitcast.25), kind=kLoop, calls=%fused_computation.35 | loop fusion | flops 3932160 | bytes 10485760 | tf_op jit(solution)/shard_map/add | solution.py:109
  374.7 7.3 %add.65 = f32[640,2048]{1,0:T(8,128)} reshape(f32[64,1,10,2048]{3,2,0,1:T(8,128)} %convert_add_fusion) | data formatting | bytes 10485760 | tf_op jit(solution)/shard_map/add | solution.py:109
  382.0 8.0 %gather_fusion = f32[512,2048]{1,0:T(8,128)} fusion(f32[640,2048]{1,0:T(8,128)} %add.65, s32[1024]{0:T(1024)S(1)} %pad_clamp_fusion), kind=kCustom, calls=%fused_computation | custom fusion | bytes 8390656 | tf_op jit(solution)/shard_map/gather | solution.py:112
  390.0 4.4 %fusion.30 = bf16[64,2048]{1,0:T(8,128)(2,1)} fusion(f32[512,2048]{1,0:T(8,128)} %gather_fusion, f32[64,8]{1,0:T(8,128)S(1)} %copy.37), kind=kLoop, calls=%fused_computation.40 | loop fusion | flops 1966080 | bytes 4458496 | tf_op jit(solution)/shard_map/reduce_sum | solution.py:113
  (62 shorter events, 18.1 us)
Async XLA Ops:
  7.2 222.7 %copy-start = (bf16[512,2048]{1,0:T(8,128)(2,1)S(1)}, bf16[512,2048]{1,0:T(8,128)(2,1)}, u32[]{:S(2)}) copy-start(bf16[512,2048]{1,0:T(8,128)(2,1)} %param.23) | copy-start | bytes 6291460
  7.2 77.1 %all-gather.2.cloned.1.call-start = ((), (), s32[]{:S(2)}) async-start(), calls=%async_computation.3 | async-start | bytes 8912896 | tf_op jit(solution)/shard_map/all_gather | solution.py:71
  7.9 40.9 %copy-start.5 = (s32[64,8]{0,1:T(8,128)S(1)}, s32[64,8]{0,1:T(8,128)}, u32[]{:S(2)}) copy-start(s32[64,8]{0,1:T(8,128)} %param.20) | copy-start | bytes 6148
  9.7 2.8 copy-start.2
  12.6 3.2 copy-start.1
  18.0 6.0 %copy-start.3 = (bf16[2,512,128]{2,1,0:T(8,128)(2,1)S(1)}, bf16[2,512,128]{2,1,0:T(8,128)(2,1)}, u32[]{:S(2)}) copy-start(bf16[2,512,128]{2,1,0:T(8,128)(2,1)} %get-tuple-element.110) | copy-start | bytes 786436 | tf_op jit(solution)/shard_map/while
  24.0 0.7 copy-start.4
  26.5 2.8 copy-start.2
  29.4 3.2 copy-start.1
  34.8 6.0 %copy-start.3 = (bf16[2,512,128]{2,1,0:T(8,128)(2,1)S(1)}, bf16[2,512,128]{2,1,0:T(8,128)(2,1)}, u32[]{:S(2)}) copy-start(bf16[2,512,128]{2,1,0:T(8,128)(2,1)} %get-tuple-element.110) | copy-start | bytes 786436 | tf_op jit(solution)/shard_map/while
  40.9 0.7 copy-start.4
  41.6 14.4 %all-to-all-start = ((bf16[16,64,128]{2,1,0:T(8,128)(2,1)}), bf16[16,64,128]{2,1,0:T(8,128)(2,1)S(1)}, u32[]{:S(2)}, u32[]{:S(2)}) async-start(bf16[16,64,128]{2,1,0:T(8,128)(2,1)} %bitcast.158), calls=%async_computation | async-start | bytes 524288 | tf_op jit(solution)/shard_map/all_to_all | solution.py:70
  50.9 38.5 %copy-start.6 = (f32[2048]{0:T(1024)S(1)}, f32[2048]{0:T(1024)}, u32[]{:S(2)}) copy-start(f32[2048]{0:T(1024)} %param.19) | copy-start | bytes 24580
  249.7 7.1 %copy-start.7 = (f32[64,8]{0,1:T(8,128)S(1)}, f32[64,8]{0,1:T(8,128)}, u32[]{:S(2)}) copy-start(f32[64,8]{0,1:T(8,128)} %param.21) | copy-start | bytes 6148
  249.7 116.3 %all-to-all-start.2 = ((bf16[128,1,10,2048]{3,2,1,0:T(8,128)(2,1)}), bf16[128,1,10,2048]{3,2,1,0:T(8,128)(2,1)}, u32[]{:S(2)}, u32[]{:S(2)}) async-start(bf16[128,1,10,2048]{3,2,1,0:T(8,128)(2,1)} %bitcast.154), calls=%async_computation.2 | async-start | bytes 16777216 | tf_op jit(solution)/shard_map/all_to_all | solution.py:105
Sparse Core Ops, SparseCore 0:
  10.1 74.1 all-gather.1

commit v3 on v2

--- a/solution.py
+++ b/solution.py
@@ -80,37 +80,38 @@
     half_units = FF // 2
     pieces = expert_in.shape[2] // half_units
     capacity = max(2, tok_local * TOP * 5 // (EXPERTS * 4))
+    lanes = 128
+    folds = model_width // lanes
     flat_routes = routes.reshape(-1)
     onehot = (flat_routes[:, None] == jnp.arange(EXPERTS, dtype=jnp.int32)[None, :]).astype(
         jnp.int32
     )
     slot_index = jnp.sum(jnp.cumsum(onehot, axis=0) * onehot, axis=1) - 1
     positions = flat_routes * capacity + slot_index
-    slot_rows = (
-        jnp.zeros((EXPERTS * capacity, model_width), jnp.bfloat16)
-        .at[positions]
-        .set(jnp.repeat(normed, TOP, axis=0))
+    token_of = jnp.arange(tok_local * TOP, dtype=jnp.int32) // TOP
+    rows_table = jnp.full((EXPERTS * capacity,), tok_local, jnp.int32).at[positions].set(token_of)
+    normed_fold = jnp.concatenate(
+        [normed.reshape(tok_local, folds, lanes), jnp.zeros((1, folds, lanes), jnp.bfloat16)], axis=0
     )
-    outgoing = jnp.repeat(slot_rows.reshape(EXPERTS, capacity, model_width), 2, axis=0)
-    outgoing = outgoing.reshape(devices, pieces, capacity, model_width)
-    arrived = lax.all_to_all(outgoing, ("req", "exp"), split_axis=0, concat_axis=0, tiled=True)
+    slot_rows = normed_fold[rows_table].reshape(EXPERTS, 1, capacity * folds, lanes)
+    outgoing = jnp.broadcast_to(slot_rows, (EXPERTS, 2, capacity * folds, lanes))
+    outgoing = outgoing.reshape(devices, pieces * capacity * folds, lanes)
+    arrived = lax.all_to_all(outgoing, ("req", "exp"), 0, 0, tiled=True)
     sources = arrived.shape[0]
-    items = arrived.shape[2]
-    rows = arrived[:, 0].reshape(sources * items, model_width)
+    rows = arrived.reshape(sources * capacity, model_width)
     gate_part = jnp.dot(rows, expert_in[0, :, 0:half_units], preferred_element_type=jnp.float32)
     up_part = jnp.dot(rows, expert_in[1, :, 0:half_units], preferred_element_type=jnp.float32)
     inner = (jax.nn.silu(gate_part) * up_part).astype(jnp.bfloat16)
     half_out = jnp.dot(inner, expert_down, preferred_element_type=jnp.float32).astype(jnp.bfloat16)
-    outputs = [half_out.reshape(sources, items, model_width)]
-    returned = lax.all_to_all(
-        jnp.stack(outputs, axis=1), ("req", "exp"), split_axis=0, concat_axis=0, tiled=True
+    back = half_out.reshape(sources, capacity * folds, lanes)
+    returned = lax.all_to_all(back, ("req", "exp"), 0, 0, tiled=True)
+    halves = returned.reshape(EXPERTS, 2, capacity, folds, lanes)
+    summed = (halves[:, 0].astype(jnp.float32) + halves[:, 1].astype(jnp.float32)).reshape(
+        EXPERTS * capacity, folds, lanes
     )
-    halves = returned.reshape(EXPERTS, 2, capacity, model_width)
-    summed = (halves[:, 0].astype(jnp.float32) + halves[:, 1].astype(jnp.float32)).reshape(
-        EXPERTS * capacity, model_width
-    )
-    picked = summed[positions] * gate_weights.reshape(-1)[:, None]
-    expert_out = jnp.sum(picked.reshape(tok_local, TOP, model_width), axis=1).astype(jnp.bfloat16)
+    picked = summed[positions] * gate_weights.reshape(-1)[:, None, None]
+    expert_out = jnp.sum(picked.reshape(tok_local, TOP, folds, lanes), axis=1)
+    expert_out = expert_out.astype(jnp.bfloat16).reshape(tok_local, model_width)
     return (attended, expert_out)
 
 

time: 403 us -> 297 us (0.74)
  waiting for transfers between devices: 143 us -> 92.5 us
  blocking collectives: 105 us -> 70.7 us
  local copies, waits for them, and re-layouts: 61.7 us -> 41.9 us
  other arithmetic: 19.6 us -> 14.9 us
    all_to_all x1, waiting for transfers between devices: 109 us -> 60.9 us  [local(): returned = lax.all_to_all(back, ('req', 'exp'), 0, 0, tiled=True)]
    all_to_all x1, blocking collectives: 105 us -> 70.7 us  [local(): arrived = lax.all_to_all(outgoing, ('req', 'exp'), 0, 0, tiled=True)]
    another operation x3 -> x1, local copies, waits for them, and re-layouts: 19.4 us -> 0.01 us  [the longest x1 9.85 us: local(): rows = arrived[:, 0].reshape(sources * items, model_width)]
    reshape x1 -> x2, local copies, waits for them, and re-layouts: 5.38 us -> 17.8 us  [the longest x1 8.93 us: local(): back = half_out.reshape(sources, capacity * folds, lanes)]
    add x1 -> x0, local copies, waits for them, and re-layouts: 7.35 us -> none  [local(): halves[:, 0].astype(jnp.float32) + halves[:, 1].astype(jnp.float32)]
    broadcast_in_dim x1, local copies, waits for them, and re-layouts: 6.75 us -> 2.61 us  [local(): jnp.broadcast_to(slot_rows, (EXPERTS, 2, capacity * folds, lanes))]
    gather x1 -> x2, local copies, waits for them, and re-layouts: 7.95 us -> 8.73 us  [the longest x1 5.38 us: local(): picked = summed[positions] * gate_weights.reshape(-1)[:, None, None]]
  transfers between devices with their start and end apart: 3 -> 3, of which waited for: 3 -> 3; matrix products, arithmetic and copies ran while one was open for 8% -> 12% of each run, Pallas kernels for 0% -> 0%
where the time goes in v3:
time: 297 us; the launch traced here: 294 us
  waiting for transfers between devices  92.5 us (31%)
  blocking collectives  70.7 us (24%)
  matrix products  43.2 us (15%)
  local copies, waits for them, and re-layouts  41.9 us (14%)
  starting transfers between devices  16 us (5%)
  other arithmetic  14.9 us (5%)
  between operations  14.2 us (5%)
    all_to_all x1, blocking collectives, local(): arrived = lax.all_to_all(outgoing, ('req', 'exp'), 0, 0, tiled=True)  70.7 us
    all_to_all x1, waiting for transfers between devices, local(): returned = lax.all_to_all(back, ('req', 'exp'), 0, 0, tiled=True)  60.9 us
    all_gather x1, waiting for transfers between devices, local(): full_proj = lax.all_gather(out_proj, 'exp', axis=0, tiled=True)  28.3 us
    dot_general x2, matrix products, attend_request(): jnp.einsum('htj,jhd->thd', weights_bf, all_vals, preferred_element_type=j...  11.7 us
    dot_general x1, matrix products, local(): jnp.dot(inner, expert_down, preferred_element_type=jnp.float32)  10.3 us
    reshape x1, local copies, waits for them, and re-layouts, local(): back = half_out.reshape(sources, capacity * folds, lanes)  8.93 us
    reshape x1, local copies, waits for them, and re-layouts, local(): rows = arrived.reshape(sources * capacity, model_width)  8.82 us
    all_to_all x1, starting transfers between devices, local(): returned = lax.all_to_all(back, ('req', 'exp'), 0, 0, tiled=True)  8.7 us
  transfers between devices with their start and end apart: 3, of which 3 were waited for; matrix products, arithmetic and copies ran while one was open for 12% of the time, Pallas kernels for 0%

profile of v3, /device:TPU:37, one launch (start us, length us, event | category | flops | bytes accessed | tf_op | source)
XLA Modules:
  0.0 293.5 jit_solution(13303697736091604535)
XLA Ops:
  7.9 33.6 %while.10 = (s32[]{:T(128)}, bf16[2,512,128]{2,1,0:T(8,128)(2,1)}, bf16[2,2,4096,128]{3,2,1,0:T(8,128)(2,1)}, bf16[2,2,512,128]{3,2,1,0:T(8,128)(2,1)}, s32[2]{0...) while((s32[]{:T(128)}, bf16[2,512,128]{2,1,0:T(8,128)(2,1)}, ...), condition=%wide.region_4.5_spmd, body=%wide.region_0.4_spmd.sunk | while | flops 1231948800 | bytes 70676728 | solution.py:68
  9.8 2.8 fusion.64
  14.0 1.7 fusion.65
  18.0 5.9 %fusion.66 = bf16[1,512,128]{1,2,0:T(8,128)(2,1)S(1)} fusion(f32[1,512,1,1,1,1,512]{6,1,5,4,3,2,0:T(8,128)S(1)} %bitcast.148, f32[1,512,1,1,1,1,4096]{6,1,5,4,3,2,0:T(8,128)} %bitcast.146, f32[512]{0:T(512)S(1)} %reduce_max.27, bf16[512,1,128]{2,0,1:T(8,128)(2,1)S(1)} %dynamic-slice_bitcast_fusion.8, ...), kind=kOutput, calls=%fused_computation.20.clone.1 | convolution fusion | flops 613548032 | bytes 10752000 | tf_op jit(solution)/shard_map/while/body/eval_jaxpr/htj,jhd->thd/dot_general | solution.py:64
  26.6 2.8 fusion.64
  30.9 1.7 fusion.65
  34.8 5.9 %fusion.66 = bf16[1,512,128]{1,2,0:T(8,128)(2,1)S(1)} fusion(f32[1,512,1,1,1,1,512]{6,1,5,4,3,2,0:T(8,128)S(1)} %bitcast.148, f32[1,512,1,1,1,1,4096]{6,1,5,4,3,2,0:T(8,128)} %bitcast.146, f32[512]{0:T(512)S(1)} %reduce_max.27, bf16[512,1,128]{2,0,1:T(8,128)(2,1)S(1)} %dynamic-slice_bitcast_fusion.8, ...), kind=kOutput, calls=%fused_computation.20.clone.1 | convolution fusion | flops 613548032 | bytes 10752000 | tf_op jit(solution)/shard_map/while/body/eval_jaxpr/htj,jhd->thd/dot_general | solution.py:64
  41.6 7.3 %all-to-all-start = ((bf16[16,64,128]{2,1,0:T(8,128)(2,1)}), bf16[16,64,128]{2,1,0:T(8,128)(2,1)S(1)}, u32[]{:S(2)}, u32[]{:S(2)}) async-start(bf16[16,64,128]{2,1,0:T(8,128)(2,1)} %bitcast.155), calls=%async_computation | async-start | bytes 524288 | tf_op jit(solution)/shard_map/all_to_all | solution.py:70
  51.0 2.4 scatter_custom_fusion
  53.4 2.5 all-to-all-done
  56.0 28.3 %all-gather.2.cloned.1.call-done = bf16[2048,2048]{1,0:T(8,128)(2,1)} async-done(((bf16[128,2048]{1,0:T(8,128)(2,1)}), bf16[2048,2048]{1,0:T(8,128)(2,1)}) %all-gather.2.cloned.1.call-update) | async-done | bytes 8388624 | tf_op jit(solution)/shard_map/all_gather | solution.py:71
  84.3 5.1 %multiply_reduce_fusion.1 = (f32[64]{0:T(128)S(1)}, f32[64,2048]{1,0:T(8,128)S(1)}) fusion(bf16[2048,2048]{1,0:T(8,128)(2,1)} %all-gather.2.cloned.1.call-done, bf16[64,2048]{1,0:T(8,128)(2,1)} %param.18, bf16[16,64,128]{2,1,0:T(8,128)(2,1)S(1)} %all-to-all-done), kind=kOutput, calls=%fused_computation.48 | convolution fusion | flops 537395136 | bytes 9437440 | tf_op jit(solution)/shard_map/dot_general | solution.py:72
  90.2 3.3 %gather_fusion = bf16[640,16,128]{2,1,0:T(8,128)(2,1)} fusion(bf16[65,16,128]{2,1,0:T(8,128)(2,1)S(1)} %concatenate.42, s32[1024]{0:T(1024)S(1)} %pad_clamp_fusion.1), kind=kCustom, calls=%fused_computation | custom fusion | bytes 5245440 | tf_op jit(solution)/shard_map/gather | solution.py:96
  93.6 2.6 broadcast_in_dim.51
  96.2 70.7 %all_to_all.29 = bf16[128,160,128]{2,1,0:T(8,128)(2,1)} all-to-all(bf16[128,160,128]{2,1,0:T(8,128)(2,1)S(1)} %bitcast.149), channel_id=1, replica_groups=mesh['req'=8,'exp'=16] {'req','exp'}, dimensions={0} | all-to-all | bytes 10485760 | tf_op jit(solution)/shard_map/all_to_all | solution.py:99
  166.9 8.8 %reshape.314 = bf16[1280,2048]{1,0:T(8,128)(2,1)} reshape(bf16[128,160,128]{2,1,0:T(8,128)(2,1)} %all_to_all.29) | data formatting | bytes 10485760 | tf_op jit(solution)/shard_map/reshape | solution.py:101
  175.7 7.5 %fusion.32 = f32[1280,512]{1,0:T(8,128)} fusion(bf16[1280,2048]{1,0:T(8,128)(2,1)} %reshape.314, bf16[2,2048,512]{2,1,0:T(8,128)(2,1)} %param.22), kind=kOutput, calls=%fused_computation.43 | convolution fusion | flops 2684354560 | bytes 9961472 | tf_op jit(solution)/shard_map/dot_general | solution.py:102
  183.3 10.3 %convolution_convert_fusion = bf16[1280,2048]{1,0:T(8,128)(2,1)} fusion(bf16[512,2048]{1,0:T(8,128)(2,1)S(1)} %copy-done, bf16[1280,2048]{1,0:T(8,128)(2,1)} %reshape.314, f32[1280,512]{1,0:T(8,128)} %fusion.32, bf16[2,2048,512]{2,1,0:T(8,128)(2,1)} %param.22), kind=kOutput, calls=%fused_computation.36 | convolution fusion | flops 5375262720 | bytes 17301504 | tf_op jit(solution)/shard_map/dot_general | solution.py:105
  193.6 8.9 %reshape.315 = bf16[128,160,128]{2,1,0:T(8,128)(2,1)} reshape(bf16[1280,2048]{1,0:T(8,128)(2,1)} %convolution_convert_fusion) | data formatting | bytes 10485760 | tf_op jit(solution)/shard_map/reshape | solution.py:106
  202.5 8.7 %all-to-all-start.2 = ((bf16[128,160,128]{2,1,0:T(8,128)(2,1)}), bf16[128,160,128]{2,1,0:T(8,128)(2,1)}, u32[]{:S(2)}, u32[]{:S(2)}) async-start(bf16[128,160,128]{2,1,0:T(8,128)(2,1)} %reshape.315), calls=%async_computation.2 | async-start | bytes 10485760 | tf_op jit(solution)/shard_map/all_to_all | solution.py:107
  211.3 60.9 %all-to-all-done.2 = bf16[128,160,128]{2,1,0:T(8,128)(2,1)} async-done(((bf16[128,160,128]{2,1,0:T(8,128)(2,1)}), bf16[128,160,128]{2,1,0:T(8,128)(2,1)}, u32[]{:S(2)}, u32[]{:S(2)}) %all-to-all-start.2) | async-done | bytes 5242912 | tf_op jit(solution)/shard_map/all_to_all | solution.py:107
  272.2 5.6 %convert_add_fusion = f32[64,1,10,16,128]{4,3,2,1,0:T(8,128)} fusion(bf16[64,2,10,16,128]{4,3,2,1,0:T(8,128)(2,1)} %bitcast.24), kind=kLoop, calls=%fused_computation.37 | loop fusion | flops 3932160 | bytes 10485760 | tf_op jit(solution)/shard_map/add | solution.py:109
  277.9 5.4 %gather_fusion.1 = f32[512,16,128]{2,1,0:T(8,128)} fusion(f32[640,16,128]{2,1,0:T(8,128)} %bitcast.150, s32[1024]{0:T(1024)S(1)} %pad_clamp_fusion), kind=kCustom, calls=%fused_computation.1 | custom fusion | bytes 8390656 | tf_op jit(solution)/shard_map/gather | solution.py:112
  283.3 2.6 multiply_reduce_fusion
  (67 shorter events, 17.3 us)
Async XLA Ops:
  7.2 176.1 %copy-start = (bf16[512,2048]{1,0:T(8,128)(2,1)S(1)}, bf16[512,2048]{1,0:T(8,128)(2,1)}, u32[]{:S(2)}) copy-start(bf16[512,2048]{1,0:T(8,128)(2,1)} %param.23) | copy-start | bytes 6291460
  7.2 77.1 %all-gather.2.cloned.1.call-start = ((), (), s32[]{:S(2)}) async-start(), calls=%async_computation.3 | async-start | bytes 8912896 | tf_op jit(solution)/shard_map/all_gather | solution.py:71
  7.9 40.9 %copy-start.5 = (s32[64,8]{0,1:T(8,128)S(1)}, s32[64,8]{0,1:T(8,128)}, u32[]{:S(2)}) copy-start(s32[64,8]{0,1:T(8,128)} %param.20) | copy-start | bytes 6148
  9.7 2.8 copy-start.2
  12.6 3.2 %copy-start.1 = (f32[512,4096]{1,0:T(8,128)}, f32[512,4096]{1,0:T(8,128)S(1)}, u32[]{:S(2)}) copy-start(f32[512,4096]{1,0:T(8,128)S(1)} %get-tuple-element.97) | copy-start | bytes 25165828 | tf_op jit(solution)/shard_map/while
  18.0 6.0 %copy-start.3 = (bf16[2,512,128]{2,1,0:T(8,128)(2,1)S(1)}, bf16[2,512,128]{2,1,0:T(8,128)(2,1)}, u32[]{:S(2)}) copy-start(bf16[2,512,128]{2,1,0:T(8,128)(2,1)} %get-tuple-element.110) | copy-start | bytes 786436 | tf_op jit(solution)/shard_map/while
  24.0 0.7 copy-start.4
  26.5 2.8 copy-start.2
  29.4 3.2 %copy-start.1 = (f32[512,4096]{1,0:T(8,128)}, f32[512,4096]{1,0:T(8,128)S(1)}, u32[]{:S(2)}) copy-start(f32[512,4096]{1,0:T(8,128)S(1)} %get-tuple-element.97) | copy-start | bytes 25165828 | tf_op jit(solution)/shard_map/while
  34.8 6.0 %copy-start.3 = (bf16[2,512,128]{2,1,0:T(8,128)(2,1)S(1)}, bf16[2,512,128]{2,1,0:T(8,128)(2,1)}, u32[]{:S(2)}) copy-start(bf16[2,512,128]{2,1,0:T(8,128)(2,1)} %get-tuple-element.110) | copy-start | bytes 786436 | tf_op jit(solution)/shard_map/while
  40.9 0.7 copy-start.4
  41.6 14.4 %all-to-all-start = ((bf16[16,64,128]{2,1,0:T(8,128)(2,1)}), bf16[16,64,128]{2,1,0:T(8,128)(2,1)S(1)}, u32[]{:S(2)}, u32[]{:S(2)}) async-start(bf16[16,64,128]{2,1,0:T(8,128)(2,1)} %bitcast.155), calls=%async_computation | async-start | bytes 524288 | tf_op jit(solution)/shard_map/all_to_all | solution.py:70
  53.4 36.0 %copy-start.6 = (f32[2048]{0:T(1024)S(1)}, f32[2048]{0:T(1024)}, u32[]{:S(2)}) copy-start(f32[2048]{0:T(1024)} %param.19) | copy-start | bytes 24580
  202.5 8.7 %copy-start.7 = (f32[64,8]{0,1:T(8,128)S(1)}, f32[64,8]{0,1:T(8,128)}, u32[]{:S(2)}) copy-start(f32[64,8]{0,1:T(8,128)} %param.21) | copy-start | bytes 6148
  202.5 69.7 %all-to-all-start.2 = ((bf16[128,160,128]{2,1,0:T(8,128)(2,1)}), bf16[128,160,128]{2,1,0:T(8,128)(2,1)}, u32[]{:S(2)}, u32[]{:S(2)}) async-start(bf16[128,160,128]{2,1,0:T(8,128)(2,1)} %reshape.315), calls=%async_computation.2 | async-start | bytes 10485760 | tf_op jit(solution)/shard_map/all_to_all | solution.py:107
Sparse Core Ops, SparseCore 0:
  10.1 74.1 all-gather.1

commit v4 on v3

--- a/solution.py
+++ b/solution.py
@@ -67,15 +67,19 @@
 
     attention = lax.map(attend_request, (queries, new_entries, cache_entries, cache_lengths))
     attention = attention.reshape(req_local * new_len, width_local)
+    req_count = lax.axis_size("req")
+    exp_count = lax.axis_size("exp")
+    share = out_proj.shape[0] // req_count
+    piece = lax.dynamic_slice_in_dim(out_proj, lax.axis_index("req") * share, share, 0)
+    full_proj = lax.all_gather(piece, ("req", "exp"), axis=0, tiled=True)
     gathered = lax.all_to_all(attention, "exp", 0, 1, tiled=True)
-    full_proj = lax.all_gather(out_proj, "exp", axis=0, tiled=True)
+    gathered = gathered.reshape(tok_local, exp_count, req_count, share)
+    gathered = jnp.transpose(gathered, (0, 2, 1, 3)).reshape(tok_local, width_local * exp_count)
     projected = jnp.dot(gathered, full_proj, preferred_element_type=jnp.float32)
     hidden = residual.astype(jnp.float32) + projected
     attended = hidden.astype(jnp.bfloat16)
     mean_square = jnp.mean(hidden * hidden, axis=-1, keepdims=True)
     normed = (hidden * lax.rsqrt(mean_square + 1e-05) * norm_gain).astype(jnp.bfloat16)
-    req_count = lax.axis_size("req")
-    exp_count = lax.axis_size("exp")
     devices = req_count * exp_count
     half_units = FF // 2
     pieces = expert_in.shape[2] // half_units

time: 297 us -> 292 us (0.983)
  waiting for transfers between devices: 92.5 us -> 81.9 us
  other arithmetic: 14.9 us -> 21 us
  local copies, waits for them, and re-layouts: 41.9 us -> 45.9 us
    dot_general x2, matrix products: 11.7 us -> 3.55 us  [attend_request(): jnp.einsum('htj,jhd->thd', weights_bf, all_vals, preferred_element_type=j...]
    all_gather x1, waiting for transfers between devices: 28.3 us -> 20.8 us  [local(): full_proj = lax.all_gather(piece, ('req', 'exp'), axis=0, tiled=True)]
    reduce_sum x2, other arithmetic: 3.3 us -> 9.43 us  [attend_request(): denoms = jnp.sum(weights, axis=-1)]
    dot_general x2, matrix products: 5.62 us -> 11.7 us  [attend_request(): jnp.einsum('thd,jhd->htj', query_heads, cache_keys, preferred_element_typ...]
  transfers between devices with their start and end apart: 3 -> 3, of which waited for: 3 -> 3; matrix products, arithmetic and copies ran while one was open for 12% -> 15% of each run, Pallas kernels for 0% -> 0%
where the time goes in v4:
time: 292 us; the launch traced here: 289 us
  waiting for transfers between devices  81.9 us (28%)
  blocking collectives  68.8 us (24%)
  local copies, waits for them, and re-layouts  45.9 us (16%)
  matrix products  41 us (14%)
  other arithmetic  21 us (7%)
  starting transfers between devices  16 us (5%)
  between operations  14.2 us (5%)
    all_to_all x1, blocking collectives, local(): arrived = lax.all_to_all(outgoing, ('req', 'exp'), 0, 0, tiled=True)  68.8 us
    all_to_all x1, waiting for transfers between devices, local(): returned = lax.all_to_all(back, ('req', 'exp'), 0, 0, tiled=True)  60.9 us
    all_gather x1, waiting for transfers between devices, local(): full_proj = lax.all_gather(piece, ('req', 'exp'), axis=0, tiled=True)  20.8 us
    dot_general x2, matrix products, attend_request(): jnp.einsum('thd,jhd->htj', query_heads, cache_keys, preferred_element_typ...  11.7 us
    dot_general x1, matrix products, local(): jnp.dot(inner, expert_down, preferred_element_type=jnp.float32)  10.3 us
    reduce_sum x2, other arithmetic, attend_request(): denoms = jnp.sum(weights, axis=-1)  9.43 us
    reshape x1, local copies, waits for them, and re-layouts, local(): back = half_out.reshape(sources, capacity * folds, lanes)  8.93 us
    reshape x1, local copies, waits for them, and re-layouts, local(): rows = arrived.reshape(sources * capacity, model_width)  8.82 us
  transfers between devices with their start and end apart: 3, of which 3 were waited for; matrix products, arithmetic and copies ran while one was open for 15% of the time, Pallas kernels for 0%

profile of v4, /device:TPU:37, one launch (start us, length us, event | category | flops | bytes accessed | tf_op | source)
XLA Modules:
  0.0 289.0 jit_solution(317079232553803504)
XLA Ops:
  7.2 1.6 constant_dynamic-slice_fusion
  8.9 39.6 %while.10 = (s32[]{:T(128)}, bf16[2,512,128]{2,1,0:T(8,128)(2,1)}, bf16[2,2,4096,128]{3,2,1,0:T(8,128)(2,1)}, bf16[2,2,512,128]{3,2,1,0:T(8,128)(2,1)}, s32[2]{0...) while((s32[]{:T(128)}, bf16[2,512,128]{2,1,0:T(8,128)(2,1)}, ...), condition=%wide.region_4.5_spmd, body=%wide.region_0.4_spmd.sunk | while | flops 1231948800 | bytes 67530928 | solution.py:68
  12.1 5.9 %fusion.62 = (f32[512]{0:T(512)S(1)}, f32[512,4096]{1,0:T(8,128)}) fusion(bf16[2,2,4096,128]{3,2,1,0:T(8,128)(2,1)} %get-tuple-element.120, s32[]{:T(128)S(6)} %copy.39, bf16[2,512,128]{2,1,0:T(8,128)(2,1)} %get-tuple-element.123, pred[4096]{0:T(1024)(128)(4,1)S(1)} %iota_compare_fusion.5), kind=kOutput, calls=%fused_computation.77.clone.1 | convolution fusion | flops 543161856 | bytes 9575424 | tf_op jit(solution)/shard_map/while/body/eval_jaxpr/thd,jhd->htj/dot_general | solution.py:40
  20.2 4.7 %fusion.63 = f32[512]{0:T(512)S(1)} fusion(f32[1,512,512]{2,1,0:T(8,128)S(1)} %bitcast.143, f32[1,512,4096]{2,1,0:T(8,128)} %bitcast.141, f32[512]{0:T(512)S(1)} %reduce_max.27), kind=kLoop, calls=%fused_computation.8.clone.1 | loop fusion | flops 7077376 | bytes 9441280 | tf_op jit(solution)/shard_map/while/body/eval_jaxpr/reduce_sum | solution.py:61
  26.1 1.8 fusion.64
  31.9 5.9 %fusion.62 = (f32[512]{0:T(512)S(1)}, f32[512,4096]{1,0:T(8,128)}) fusion(bf16[2,2,4096,128]{3,2,1,0:T(8,128)(2,1)} %get-tuple-element.120, s32[]{:T(128)S(6)} %copy.39, bf16[2,512,128]{2,1,0:T(8,128)(2,1)} %get-tuple-element.123, pred[4096]{0:T(1024)(128)(4,1)S(1)} %iota_compare_fusion.5), kind=kOutput, calls=%fused_computation.77.clone.1 | convolution fusion | flops 543161856 | bytes 9575424 | tf_op jit(solution)/shard_map/while/body/eval_jaxpr/thd,jhd->htj/dot_general | solution.py:40
  40.0 4.7 %fusion.63 = f32[512]{0:T(512)S(1)} fusion(f32[1,512,512]{2,1,0:T(8,128)S(1)} %bitcast.143, f32[1,512,4096]{2,1,0:T(8,128)} %bitcast.141, f32[512]{0:T(512)S(1)} %reduce_max.27), kind=kLoop, calls=%fused_computation.8.clone.1 | loop fusion | flops 7077376 | bytes 9441280 | tf_op jit(solution)/shard_map/while/body/eval_jaxpr/reduce_sum | solution.py:61
  45.9 1.8 fusion.64
  48.5 7.3 %all-to-all-start = ((bf16[16,64,128]{2,1,0:T(8,128)(2,1)}), bf16[16,64,128]{2,1,0:T(8,128)(2,1)S(1)}, u32[]{:S(2)}, u32[]{:S(2)}) async-start(bf16[16,64,128]{2,1,0:T(8,128)(2,1)} %bitcast.154), calls=%async_computation | async-start | bytes 524288 | tf_op jit(solution)/shard_map/all_to_all | solution.py:75
  57.8 2.4 scatter_custom_fusion
  60.8 20.8 %all-gather.2.cloned.1.call-done = bf16[2048,2048]{1,0:T(8,128)(2,1)} async-done(((bf16[16,2048]{1,0:T(8,128)(2,1)}), bf16[2048,2048]{1,0:T(8,128)(2,1)}) %all-gather.2.cloned.1.call-update) | async-done | bytes 8388624 | tf_op jit(solution)/shard_map/all_gather | solution.py:74
  81.6 5.1 %multiply_reduce_fusion.1 = (f32[64]{0:T(128)S(1)}, f32[64,2048]{1,0:T(8,128)S(1)}) fusion(bf16[64,2048]{0,1:T(8,128)(2,1)S(1)} %bitcast.148, bf16[2048,2048]{1,0:T(8,128)(2,1)} %all-gather.2.cloned.1.call-done, bf16[64,2048]{1,0:T(8,128)(2,1)S(1)} %copy-done.2), kind=kOutput, calls=%fused_computation.48 | convolution fusion | flops 537395136 | bytes 9437440 | tf_op jit(solution)/shard_map/dot_general | solution.py:78
  87.5 3.3 %gather_fusion = bf16[640,16,128]{2,1,0:T(8,128)(2,1)} fusion(bf16[65,16,128]{2,1,0:T(8,128)(2,1)S(1)} %concatenate.42, s32[1024]{0:T(1024)S(1)} %pad_clamp_fusion.1), kind=kCustom, calls=%fused_computation | custom fusion | bytes 5245440 | tf_op jit(solution)/shard_map/gather | solution.py:100
  90.9 2.6 broadcast_in_dim.51
  93.5 68.8 %all_to_all.26 = bf16[128,160,128]{2,1,0:T(8,128)(2,1)} all-to-all(bf16[128,160,128]{2,1,0:T(8,128)(2,1)S(1)} %bitcast.145), channel_id=1, replica_groups=mesh['req'=8,'exp'=16] {'req','exp'}, dimensions={0} | all-to-all | bytes 10485760 | tf_op jit(solution)/shard_map/all_to_all | solution.py:103
  162.3 8.8 %reshape.323 = bf16[1280,2048]{1,0:T(8,128)(2,1)} reshape(bf16[128,160,128]{2,1,0:T(8,128)(2,1)} %all_to_all.26) | data formatting | bytes 10485760 | tf_op jit(solution)/shard_map/reshape | solution.py:105
  171.2 7.6 %fusion.32 = f32[1280,512]{1,0:T(8,128)} fusion(bf16[1280,2048]{1,0:T(8,128)(2,1)} %reshape.323, bf16[2,2048,512]{2,1,0:T(8,128)(2,1)} %param.22), kind=kOutput, calls=%fused_computation.43 | convolution fusion | flops 2684354560 | bytes 9961472 | tf_op jit(solution)/shard_map/dot_general | solution.py:106
  178.7 10.3 %convolution_convert_fusion = bf16[1280,2048]{1,0:T(8,128)(2,1)} fusion(bf16[512,2048]{1,0:T(8,128)(2,1)S(1)} %copy-done, bf16[1280,2048]{1,0:T(8,128)(2,1)} %reshape.323, f32[1280,512]{1,0:T(8,128)} %fusion.32, bf16[2,2048,512]{2,1,0:T(8,128)(2,1)} %param.22), kind=kOutput, calls=%fused_computation.36 | convolution fusion | flops 5375262720 | bytes 17301504 | tf_op jit(solution)/shard_map/dot_general | solution.py:109
  189.0 8.9 %reshape.324 = bf16[128,160,128]{2,1,0:T(8,128)(2,1)} reshape(bf16[1280,2048]{1,0:T(8,128)(2,1)} %convolution_convert_fusion) | data formatting | bytes 10485760 | tf_op jit(solution)/shard_map/reshape | solution.py:110
  198.0 8.7 %all-to-all-start.2 = ((bf16[128,160,128]{2,1,0:T(8,128)(2,1)}), bf16[128,160,128]{2,1,0:T(8,128)(2,1)}, u32[]{:S(2)}, u32[]{:S(2)}) async-start(bf16[128,160,128]{2,1,0:T(8,128)(2,1)} %reshape.324), calls=%async_computation.2 | async-start | bytes 10485760 | tf_op jit(solution)/shard_map/all_to_all | solution.py:111
  206.8 60.9 %all-to-all-done.2 = bf16[128,160,128]{2,1,0:T(8,128)(2,1)} async-done(((bf16[128,160,128]{2,1,0:T(8,128)(2,1)}), bf16[128,160,128]{2,1,0:T(8,128)(2,1)}, u32[]{:S(2)}, u32[]{:S(2)}) %all-to-all-start.2) | async-done | bytes 5242912 | tf_op jit(solution)/shard_map/all_to_all | solution.py:111
  267.7 5.6 %convert_add_fusion = f32[64,1,10,16,128]{4,3,2,1,0:T(8,128)} fusion(bf16[64,2,10,16,128]{4,3,2,1,0:T(8,128)(2,1)} %bitcast.27), kind=kLoop, calls=%fused_computation.37 | loop fusion | flops 3932160 | bytes 10485760 | tf_op jit(solution)/shard_map/add | solution.py:113
  273.3 5.4 %gather_fusion.1 = f32[512,16,128]{2,1,0:T(8,128)} fusion(f32[640,16,128]{2,1,0:T(8,128)} %bitcast.146, s32[1024]{0:T(1024)S(1)} %pad_clamp_fusion), kind=kCustom, calls=%fused_computation.1 | custom fusion | bytes 8390656 | tf_op jit(solution)/shard_map/gather | solution.py:116
  278.7 2.6 multiply_reduce_fusion
  (60 shorter events, 19.0 us)
Async XLA Ops:
  7.2 171.6 %copy-start = (bf16[512,2048]{1,0:T(8,128)(2,1)S(1)}, bf16[512,2048]{1,0:T(8,128)(2,1)}, u32[]{:S(2)}) copy-start(bf16[512,2048]{1,0:T(8,128)(2,1)} %param.23) | copy-start | bytes 6291460
  7.2 74.4 %all-gather.2.cloned.1.call-start = ((), (), s32[]{:S(2)}) async-start(), calls=%async_computation.3 | async-start | bytes 8454144 | tf_op jit(solution)/shard_map/all_gather | solution.py:74
  8.9 46.9 %copy-start.3 = (s32[64,8]{0,1:T(8,128)S(1)}, s32[64,8]{0,1:T(8,128)}, u32[]{:S(2)}) copy-start(s32[64,8]{0,1:T(8,128)} %param.20) | copy-start | bytes 6148
  8.9 72.7 %copy-start.2 = (bf16[64,2048]{1,0:T(8,128)(2,1)S(1)}, bf16[64,2048]{1,0:T(8,128)(2,1)}, u32[]{:S(2)}) copy-start(bf16[64,2048]{1,0:T(8,128)(2,1)} %param.18) | copy-start | bytes 786436
  20.2 5.9 %copy-start.1 = (f32[512,4096]{1,0:T(8,128)S(1)}, f32[512,4096]{1,0:T(8,128)}, u32[]{:S(2)}) copy-start(f32[512,4096]{1,0:T(8,128)} %get-tuple-element.97) | copy-start | bytes 25165828 | tf_op jit(solution)/shard_map/while
  40.0 5.9 %copy-start.1 = (f32[512,4096]{1,0:T(8,128)S(1)}, f32[512,4096]{1,0:T(8,128)}, u32[]{:S(2)}) copy-start(f32[512,4096]{1,0:T(8,128)} %get-tuple-element.97) | copy-start | bytes 25165828 | tf_op jit(solution)/shard_map/while
  48.5 12.0 %all-to-all-start = ((bf16[16,64,128]{2,1,0:T(8,128)(2,1)}), bf16[16,64,128]{2,1,0:T(8,128)(2,1)S(1)}, u32[]{:S(2)}, u32[]{:S(2)}) async-start(bf16[16,64,128]{2,1,0:T(8,128)(2,1)} %bitcast.154), calls=%async_computation | async-start | bytes 524288 | tf_op jit(solution)/shard_map/all_to_all | solution.py:75
  81.6 5.1 %copy-start.4 = (f32[2048]{0:T(1024)S(1)}, f32[2048]{0:T(1024)}, u32[]{:S(2)}) copy-start(f32[2048]{0:T(1024)} %param.19) | copy-start | bytes 24580
  198.0 8.7 %copy-start.5 = (f32[64,8]{0,1:T(8,128)S(1)}, f32[64,8]{0,1:T(8,128)}, u32[]{:S(2)}) copy-start(f32[64,8]{0,1:T(8,128)} %param.21) | copy-start | bytes 6148
  198.0 69.7 %all-to-all-start.2 = ((bf16[128,160,128]{2,1,0:T(8,128)(2,1)}), bf16[128,160,128]{2,1,0:T(8,128)(2,1)}, u32[]{:S(2)}, u32[]{:S(2)}) async-start(bf16[128,160,128]{2,1,0:T(8,128)(2,1)} %reshape.324), calls=%async_computation.2 | async-start | bytes 10485760 | tf_op jit(solution)/shard_map/all_to_all | solution.py:111
Sparse Core Ops, SparseCore 0:
  11.7 69.8 all-gather.1

commit v5 on v4

--- a/solution.py
+++ b/solution.py
@@ -97,24 +97,43 @@
     normed_fold = jnp.concatenate(
         [normed.reshape(tok_local, folds, lanes), jnp.zeros((1, folds, lanes), jnp.bfloat16)], axis=0
     )
-    slot_rows = normed_fold[rows_table].reshape(EXPERTS, 1, capacity * folds, lanes)
-    outgoing = jnp.broadcast_to(slot_rows, (EXPERTS, 2, capacity * folds, lanes))
-    outgoing = outgoing.reshape(devices, pieces * capacity * folds, lanes)
-    arrived = lax.all_to_all(outgoing, ("req", "exp"), 0, 0, tiled=True)
-    sources = arrived.shape[0]
-    rows = arrived.reshape(sources * capacity, model_width)
-    gate_part = jnp.dot(rows, expert_in[0, :, 0:half_units], preferred_element_type=jnp.float32)
-    up_part = jnp.dot(rows, expert_in[1, :, 0:half_units], preferred_element_type=jnp.float32)
+    slot_rows = normed_fold[rows_table].reshape(EXPERTS, 1, capacity, folds, lanes)
+    chunks = 2
+    fold_chunk = folds // chunks
+    width_chunk = fold_chunk * lanes
+    gate_part = 0.0
+    up_part = 0.0
+    for c in range(chunks):
+        part = slot_rows[:, :, :, c * fold_chunk : (c + 1) * fold_chunk, :]
+        outgoing = jnp.broadcast_to(part, (EXPERTS, 2, capacity, fold_chunk, lanes))
+        outgoing = outgoing.reshape(devices, pieces * capacity * fold_chunk, lanes)
+        arrived = lax.all_to_all(outgoing, ("req", "exp"), 0, 0, tiled=True)
+        sources = arrived.shape[0]
+        rows = arrived.reshape(sources * capacity, width_chunk)
+        cols = slice(c * width_chunk, (c + 1) * width_chunk)
+        gate_part = gate_part + jnp.dot(
+            rows, expert_in[0, cols, 0:half_units], preferred_element_type=jnp.float32
+        )
+        up_part = up_part + jnp.dot(
+            rows, expert_in[1, cols, 0:half_units], preferred_element_type=jnp.float32
+        )
     inner = (jax.nn.silu(gate_part) * up_part).astype(jnp.bfloat16)
-    half_out = jnp.dot(inner, expert_down, preferred_element_type=jnp.float32).astype(jnp.bfloat16)
-    back = half_out.reshape(sources, capacity * folds, lanes)
-    returned = lax.all_to_all(back, ("req", "exp"), 0, 0, tiled=True)
-    halves = returned.reshape(EXPERTS, 2, capacity, folds, lanes)
-    summed = (halves[:, 0].astype(jnp.float32) + halves[:, 1].astype(jnp.float32)).reshape(
-        EXPERTS * capacity, folds, lanes
-    )
-    picked = summed[positions] * gate_weights.reshape(-1)[:, None, None]
-    expert_out = jnp.sum(picked.reshape(tok_local, TOP, folds, lanes), axis=1)
+    gates = gate_weights.reshape(-1)[:, None, None]
+    outs = []
+    for c in range(chunks):
+        cols = slice(c * width_chunk, (c + 1) * width_chunk)
+        half_out = jnp.dot(
+            inner, expert_down[:, cols], preferred_element_type=jnp.float32
+        ).astype(jnp.bfloat16)
+        back = half_out.reshape(sources, capacity * fold_chunk, lanes)
+        returned = lax.all_to_all(back, ("req", "exp"), 0, 0, tiled=True)
+        halves = returned.reshape(EXPERTS, 2, capacity, fold_chunk, lanes)
+        summed = (halves[:, 0].astype(jnp.float32) + halves[:, 1].astype(jnp.float32)).reshape(
+            EXPERTS * capacity, fold_chunk, lanes
+        )
+        picked = summed[positions] * gates
+        outs.append(jnp.sum(picked.reshape(tok_local, TOP, fold_chunk, lanes), axis=1))
+    expert_out = jnp.concatenate(outs, axis=1)
     expert_out = expert_out.astype(jnp.bfloat16).reshape(tok_local, model_width)
     return (attended, expert_out)
 

time: 292 us -> 295 us (1.010)
  blocking collectives: 68.8 us -> 40.7 us
  starting transfers between devices: 16 us -> 28.7 us
  waiting for transfers between devices: 81.9 us -> 93 us
  matrix products: 41 us -> 46.8 us
    all_to_all x1, blocking collectives: 68.8 us -> 40.7 us  [local(): arrived = lax.all_to_all(outgoing, ('req', 'exp'), 0, 0, tiled=True)]
    all_to_all x0 -> x1, waiting for transfers between devices: none -> 18.3 us  [local(): arrived = lax.all_to_all(outgoing, ('req', 'exp'), 0, 0, tiled=True)]
    all_to_all x1 -> x2, waiting for transfers between devices: 60.9 us -> 54 us  [local(): returned = lax.all_to_all(back, ('req', 'exp'), 0, 0, tiled=True)]
    all_to_all x0 -> x1, starting transfers between devices: none -> 6.79 us  [local(): arrived = lax.all_to_all(outgoing, ('req', 'exp'), 0, 0, tiled=True)]
    dot_general x2 -> x6, matrix products: 17.9 us -> 23.7 us  [the longest x2 8.84 us: local(): jnp.dot(rows, expert_in[0, cols, 0:half_units], preferred_element_type=jn...]
    all_to_all x1 -> x2, starting transfers between devices: 8.71 us -> 14.5 us  [local(): returned = lax.all_to_all(back, ('req', 'exp'), 0, 0, tiled=True)]
    reshape x2 -> x4, local copies, waits for them, and re-layouts: 17.8 us -> 16.6 us  [the longest x2 8.29 us: local(): back = half_out.reshape(sources, capacity * fold_chunk, lanes)]
    gather x2 -> x3, local copies, waits for them, and re-layouts: 8.73 us -> 9.56 us  [the longest x2 6.91 us: local(): picked = summed[positions] * gates]
  transfers between devices with their start and end apart: 3 -> 5, of which waited for: 3 -> 5; matrix products, arithmetic and copies ran while one was open for 15% -> 24% of each run, Pallas kernels for 0% -> 0%
where the time goes in v5:
time: 295 us; the launch traced here: 291 us
  waiting for transfers between devices  93 us (32%)
  local copies, waits for them, and re-layouts  46.8 us (16%)
  matrix products  46.8 us (16%)
  blocking collectives  40.7 us (14%)
  starting transfers between devices  28.7 us (10%)
  other arithmetic  20.4 us (7%)
  between operations  14.3 us (5%)
    all_to_all x2, waiting for transfers between devices, local(): returned = lax.all_to_all(back, ('req', 'exp'), 0, 0, tiled=True)  54 us
    all_to_all x1, blocking collectives, local(): arrived = lax.all_to_all(outgoing, ('req', 'exp'), 0, 0, tiled=True)  40.7 us
    all_gather x1, waiting for transfers between devices, local(): full_proj = lax.all_gather(piece, ('req', 'exp'), axis=0, tiled=True)  20.5 us
    all_to_all x1, waiting for transfers between devices, local(): arrived = lax.all_to_all(outgoing, ('req', 'exp'), 0, 0, tiled=True)  18.3 us
    all_to_all x2, starting transfers between devices, local(): returned = lax.all_to_all(back, ('req', 'exp'), 0, 0, tiled=True)  14.5 us
    dot_general x2, matrix products, attend_request(): jnp.einsum('thd,jhd->htj', query_heads, cache_keys, preferred_element_typ...  11.7 us
    reduce_sum x2, other arithmetic, attend_request(): denoms = jnp.sum(weights, axis=-1)  9.43 us
    dot_general x2, matrix products, local(): jnp.dot(rows, expert_in[0, cols, 0:half_units], preferred_element_type=jn...  8.84 us
  transfers between devices with their start and end apart: 5, of which 5 were waited for; matrix products, arithmetic and copies ran while one was open for 24% of the time, Pallas kernels for 0%

profile of v5, /device:TPU:37, one launch (start us, length us, event | category | flops | bytes accessed | tf_op | source)
XLA Modules:
  0.0 290.8 jit_solution(15630088052432284335)
XLA Ops:
  8.9 39.7 %while.10 = (s32[]{:T(128)}, bf16[2,512,128]{2,1,0:T(8,128)(2,1)}, bf16[2,2,4096,128]{3,2,1,0:T(8,128)(2,1)}, bf16[2,2,512,128]{3,2,1,0:T(8,128)(2,1)}, s32[2]{0...) while((s32[]{:T(128)}, bf16[2,512,128]{2,1,0:T(8,128)(2,1)}, ...), condition=%wide.region_4.5_spmd, body=%wide.region_0.4_spmd.sunk | while | flops 1231948800 | bytes 67530928 | solution.py:68
  12.2 5.9 %fusion.70 = (f32[512]{0:T(512)S(1)}, f32[512,4096]{1,0:T(8,128)}) fusion(bf16[2,2,4096,128]{3,2,1,0:T(8,128)(2,1)} %get-tuple-element.124, s32[]{:T(128)S(6)} %copy.39, bf16[2,512,128]{2,1,0:T(8,128)(2,1)} %get-tuple-element.127, pred[4096]{0:T(1024)(128)(4,1)S(1)} %iota_compare_fusion.5), kind=kOutput, calls=%fused_computation.92.clone.1 | convolution fusion | flops 543161856 | bytes 9575424 | tf_op jit(solution)/shard_map/while/body/eval_jaxpr/thd,jhd->htj/dot_general | solution.py:40
  20.3 4.7 %fusion.71 = f32[512]{0:T(512)S(1)} fusion(f32[1,512,512]{2,1,0:T(8,128)S(1)} %bitcast.159, f32[1,512,4096]{2,1,0:T(8,128)} %bitcast.157, f32[512]{0:T(512)S(1)} %reduce_max.27), kind=kLoop, calls=%fused_computation.9.clone.1 | loop fusion | flops 7077376 | bytes 9441280 | tf_op jit(solution)/shard_map/while/body/eval_jaxpr/reduce_sum | solution.py:61
  32.0 5.9 %fusion.70 = (f32[512]{0:T(512)S(1)}, f32[512,4096]{1,0:T(8,128)}) fusion(bf16[2,2,4096,128]{3,2,1,0:T(8,128)(2,1)} %get-tuple-element.124, s32[]{:T(128)S(6)} %copy.39, bf16[2,512,128]{2,1,0:T(8,128)(2,1)} %get-tuple-element.127, pred[4096]{0:T(1024)(128)(4,1)S(1)} %iota_compare_fusion.5), kind=kOutput, calls=%fused_computation.92.clone.1 | convolution fusion | flops 543161856 | bytes 9575424 | tf_op jit(solution)/shard_map/while/body/eval_jaxpr/thd,jhd->htj/dot_general | solution.py:40
  40.1 4.7 %fusion.71 = f32[512]{0:T(512)S(1)} fusion(f32[1,512,512]{2,1,0:T(8,128)S(1)} %bitcast.159, f32[1,512,4096]{2,1,0:T(8,128)} %bitcast.157, f32[512]{0:T(512)S(1)} %reduce_max.27), kind=kLoop, calls=%fused_computation.9.clone.1 | loop fusion | flops 7077376 | bytes 9441280 | tf_op jit(solution)/shard_map/while/body/eval_jaxpr/reduce_sum | solution.py:61
  48.6 7.4 %all-to-all-start = ((bf16[16,64,128]{2,1,0:T(8,128)(2,1)}), bf16[16,64,128]{2,1,0:T(8,128)(2,1)S(1)}, u32[]{:S(2)}, u32[]{:S(2)}) async-start(bf16[16,64,128]{2,1,0:T(8,128)(2,1)} %bitcast.15), calls=%async_computation | async-start | bytes 524288 | tf_op jit(solution)/shard_map/all_to_all | solution.py:75
  61.1 20.5 %all-gather.2.cloned.1.call-done = bf16[2048,2048]{1,0:T(8,128)(2,1)} async-done(((bf16[16,2048]{1,0:T(8,128)(2,1)}), bf16[2048,2048]{1,0:T(8,128)(2,1)}) %all-gather.2.cloned.1.call-update) | async-done | bytes 8388624 | tf_op jit(solution)/shard_map/all_gather | solution.py:74
  81.6 5.1 %multiply_reduce_fusion.2 = (f32[64]{0:T(128)S(1)}, f32[64,2048]{1,0:T(8,128)S(1)}) fusion(bf16[64,2048]{0,1:T(8,128)(2,1)S(1)} %bitcast.167, bf16[2048,2048]{1,0:T(8,128)(2,1)} %all-gather.2.cloned.1.call-done, bf16[64,2048]{1,0:T(8,128)(2,1)S(1)} %copy-done.7), kind=kOutput, calls=%fused_computation.63 | convolution fusion | flops 537395136 | bytes 9437440 | tf_op jit(solution)/shard_map/dot_general | solution.py:78
  91.0 40.7 %all_to_all.36 = bf16[128,80,128]{2,1,0:T(8,128)(2,1)} all-to-all(bf16[128,80,128]{2,1,0:T(8,128)(2,1)S(1)} %bitcast.164), channel_id=1, replica_groups=mesh['req'=8,'exp'=16] {'req','exp'}, dimensions={0} | all-to-all | bytes 5242880 | tf_op jit(solution)/shard_map/all_to_all | solution.py:110
  133.6 6.8 %all-to-all-start.2 = ((bf16[128,80,128]{2,1,0:T(8,128)(2,1)}), bf16[128,80,128]{2,1,0:T(8,128)(2,1)S(1)}, u32[]{:S(2)}, u32[]{:S(2)}) async-start(bf16[128,80,128]{2,1,0:T(8,128)(2,1)} %bitcast.162), calls=%async_computation.2 | async-start | bytes 5242880 | tf_op jit(solution)/shard_map/all_to_all | solution.py:110
  140.4 5.2 %reshape.347 = bf16[1280,1024]{1,0:T(8,128)(2,1)} reshape(bf16[128,80,128]{2,1,0:T(8,128)(2,1)} %all_to_all.36) | data formatting | bytes 5242880 | tf_op jit(solution)/shard_map/reshape | solution.py:112
  145.6 5.2 %fusion.33 = f32[1280,512]{1,0:T(8,128)} fusion(bf16[1280,1024]{1,0:T(8,128)(2,1)} %reshape.347, bf16[2,2048,512]{2,1,0:T(8,128)(2,1)} %param.22), kind=kOutput, calls=%fused_computation.51 | convolution fusion | flops 1342177280 | bytes 6291456 | tf_op jit(solution)/shard_map/dot_general | solution.py:117
  150.8 4.3 %fusion.36 = f32[1280,512]{1,0:T(8,128)} fusion(bf16[1280,1024]{1,0:T(8,128)(2,1)S(1)} %copy-done.6, bf16[2,2048,512]{2,1,0:T(8,128)(2,1)} %param.22), kind=kOutput, calls=%fused_computation.54 | convolution fusion | flops 1342177280 | bytes 6291456 | tf_op jit(solution)/shard_map/dot_general | solution.py:114
  155.0 18.3 %all-to-all-done.2 = bf16[128,80,128]{2,1,0:T(8,128)(2,1)S(1)} async-done(((bf16[128,80,128]{2,1,0:T(8,128)(2,1)}), bf16[128,80,128]{2,1,0:T(8,128)(2,1)S(1)}, u32[]{:S(2)}, u32[]{:S(2)}) %all-to-all-start.2) | async-done | bytes 2621472 | tf_op jit(solution)/shard_map/all_to_all | solution.py:110
  176.5 4.6 %convolution_add_fusion.1 = f32[1280,512]{1,0:T(8,128)S(1)} fusion(f32[1280,512]{1,0:T(8,128)} %fusion.36, bf16[1280,1024]{1,0:T(8,128)(2,1)} %reshape.349, bf16[2,2048,512]{2,1,0:T(8,128)(2,1)} %param.22), kind=kOutput, calls=%fused_computation.41 | convolution fusion | flops 1342832640 | bytes 8912896 | tf_op jit(solution)/shard_map/dot_general | solution.py:114
  181.1 3.5 %fusion.31 = bf16[1280,512]{1,0:T(8,128)(2,1)S(1)} fusion(f32[1280,512]{1,0:T(8,128)S(1)} %copy-done.12, bf16[1280,1024]{1,0:T(8,128)(2,1)S(1)} %copy-done.5, f32[1280,512]{1,0:T(8,128)S(1)} %convolution_add_fusion.1, bf16[2,2048,512]{2,1,0:T(8,128)(2,1)} %param.22), kind=kOutput, calls=%fused_computation.42 | convolution fusion | flops 1346764800 | bytes 10223616 | tf_op jit(solution)/shard_map/dot_general | solution.py:117
  190.3 6.8 %all-to-all-start.3 = ((bf16[128,80,128]{2,1,0:T(8,128)(2,1)}), bf16[128,80,128]{2,1,0:T(8,128)(2,1)S(1)}, u32[]{:S(2)}, u32[]{:S(2)}) async-start(bf16[128,80,128]{2,1,0:T(8,128)(2,1)} %reshape.350), calls=%async_computation.3 | async-start | bytes 5242880 | tf_op jit(solution)/shard_map/all_to_all | solution.py:129
  197.1 4.6 %convolution_convert_fusion = bf16[1280,1024]{1,0:T(8,128)(2,1)} fusion(bf16[1280,512]{1,0:T(8,128)(2,1)} %copy-done.13, bf16[512,2048]{1,0:T(8,128)(2,1)} %param.23), kind=kOutput, calls=%fused_computation.37 | convolution fusion | flops 1343488000 | bytes 4980736 | tf_op jit(solution)/shard_map/dot_general | solution.py:125
  201.7 5.2 %reshape.352 = bf16[128,80,128]{2,1,0:T(8,128)(2,1)} reshape(bf16[1280,1024]{1,0:T(8,128)(2,1)} %convolution_convert_fusion) | data formatting | bytes 5242880 | tf_op jit(solution)/shard_map/reshape | solution.py:128
  206.9 23.2 %all-to-all-done.3 = bf16[128,80,128]{2,1,0:T(8,128)(2,1)S(1)} async-done(((bf16[128,80,128]{2,1,0:T(8,128)(2,1)}), bf16[128,80,128]{2,1,0:T(8,128)(2,1)S(1)}, u32[]{:S(2)}, u32[]{:S(2)}) %all-to-all-start.3) | async-done | bytes 2621472 | tf_op jit(solution)/shard_map/all_to_all | solution.py:129
  230.1 7.7 %all-to-all-start.4 = ((bf16[128,80,128]{2,1,0:T(8,128)(2,1)}), bf16[128,80,128]{2,1,0:T(8,128)(2,1)}, u32[]{:S(2)}, u32[]{:S(2)}) async-start(bf16[128,80,128]{2,1,0:T(8,128)(2,1)} %reshape.352), calls=%async_computation.4 | async-start | bytes 5242880 | tf_op jit(solution)/shard_map/all_to_all | solution.py:129
  239.7 30.8 %all-to-all-done.4 = bf16[128,80,128]{2,1,0:T(8,128)(2,1)} async-done(((bf16[128,80,128]{2,1,0:T(8,128)(2,1)}), bf16[128,80,128]{2,1,0:T(8,128)(2,1)}, u32[]{:S(2)}, u32[]{:S(2)}) %all-to-all-start.4) | async-done | bytes 2621472 | tf_op jit(solution)/shard_map/all_to_all | solution.py:129
  270.5 3.7 %convert_add_fusion = f32[64,1,10,8,128]{4,3,2,1,0:T(8,128)} fusion(bf16[64,2,10,8,128]{4,3,2,1,0:T(8,128)(2,1)} %bitcast.35), kind=kLoop, calls=%fused_computation.43 | loop fusion | flops 1966080 | bytes 5242880 | tf_op jit(solution)/shard_map/add | solution.py:131
  276.9 4.2 %gather_fusion.2 = f32[512,8,128]{2,1,0:T(8,128)} fusion(f32[640,8,128]{2,1,0:T(8,128)} %bitcast.166, s32[1024]{0:T(1024)S(1)} %pad_clamp_fusion), kind=kCustom, calls=%fused_computation.2 | custom fusion | bytes 4196352 | tf_op jit(solution)/shard_map/gather | solution.py:134
  (91 shorter events, 47.5 us)
Async XLA Ops:
  7.2 1.1 copy-start
  7.2 74.4 %all-gather.2.cloned.1.call-start = ((), (), s32[]{:S(2)}) async-start(), calls=%async_computation.5 | async-start | bytes 8454144 | tf_op jit(solution)/shard_map/all_gather | solution.py:74
  8.9 47.1 %copy-start.8 = (s32[64,8]{0,1:T(8,128)S(1)}, s32[64,8]{0,1:T(8,128)}, u32[]{:S(2)}) copy-start(s32[64,8]{0,1:T(8,128)} %param.20) | copy-start | bytes 6148
  20.3 5.9 %copy-start.2 = (f32[512,4096]{1,0:T(8,128)S(1)}, f32[512,4096]{1,0:T(8,128)}, u32[]{:S(2)}) copy-start(f32[512,4096]{1,0:T(8,128)} %get-tuple-element.101) | copy-start | bytes 25165828 | tf_op jit(solution)/shard_map/while
  40.1 5.9 %copy-start.2 = (f32[512,4096]{1,0:T(8,128)S(1)}, f32[512,4096]{1,0:T(8,128)}, u32[]{:S(2)}) copy-start(f32[512,4096]{1,0:T(8,128)} %get-tuple-element.101) | copy-start | bytes 25165828 | tf_op jit(solution)/shard_map/while
  48.6 33.0 %copy-start.7 = (bf16[64,2048]{1,0:T(8,128)(2,1)S(1)}, bf16[64,2048]{1,0:T(8,128)(2,1)}, u32[]{:S(2)}) copy-start(bf16[64,2048]{1,0:T(8,128)(2,1)} %param.18) | copy-start | bytes 786436
  48.6 12.1 %all-to-all-start = ((bf16[16,64,128]{2,1,0:T(8,128)(2,1)}), bf16[16,64,128]{2,1,0:T(8,128)(2,1)S(1)}, u32[]{:S(2)}, u32[]{:S(2)}) async-start(bf16[16,64,128]{2,1,0:T(8,128)(2,1)} %bitcast.15), calls=%async_computation | async-start | bytes 524288 | tf_op jit(solution)/shard_map/all_to_all | solution.py:75
  81.6 5.1 %copy-start.9 = (f32[2048]{0:T(1024)S(1)}, f32[2048]{0:T(1024)}, u32[]{:S(2)}) copy-start(f32[2048]{0:T(1024)} %param.19) | copy-start | bytes 24580
  133.6 39.8 %all-to-all-start.2 = ((bf16[128,80,128]{2,1,0:T(8,128)(2,1)}), bf16[128,80,128]{2,1,0:T(8,128)(2,1)S(1)}, u32[]{:S(2)}, u32[]{:S(2)}) async-start(bf16[128,80,128]{2,1,0:T(8,128)(2,1)} %bitcast.162), calls=%async_computation.2 | async-start | bytes 5242880 | tf_op jit(solution)/shard_map/all_to_all | solution.py:110
  145.6 5.2 %copy-start.6 = (bf16[1280,1024]{1,0:T(8,128)(2,1)S(1)}, bf16[1280,1024]{1,0:T(8,128)(2,1)}, u32[]{:S(2)}) copy-start(bf16[1280,1024]{1,0:T(8,128)(2,1)} %reshape.347) | copy-start | bytes 7864324
  176.5 4.6 %copy-start.5 = (bf16[1280,1024]{1,0:T(8,128)(2,1)S(1)}, bf16[1280,1024]{1,0:T(8,128)(2,1)}, u32[]{:S(2)}) copy-start(bf16[1280,1024]{1,0:T(8,128)(2,1)} %reshape.349) | copy-start | bytes 7864324
  176.5 4.6 %copy-start.12 = (f32[1280,512]{1,0:T(8,128)S(1)}, f32[1280,512]{1,0:T(8,128)}, u32[]{:S(2)}) copy-start(f32[1280,512]{1,0:T(8,128)} %fusion.33) | copy-start | bytes 7864324
  181.1 4.6 %copy-start.11 = (bf16[512,2048]{1,0:T(8,128)(2,1)S(1)}, bf16[512,2048]{1,0:T(8,128)(2,1)}, u32[]{:S(2)}) copy-start(bf16[512,2048]{1,0:T(8,128)(2,1)} %param.23) | copy-start | bytes 6291460
  184.6 1.1 copy-start.13
  190.3 39.8 %all-to-all-start.3 = ((bf16[128,80,128]{2,1,0:T(8,128)(2,1)}), bf16[128,80,128]{2,1,0:T(8,128)(2,1)S(1)}, u32[]{:S(2)}, u32[]{:S(2)}) async-start(bf16[128,80,128]{2,1,0:T(8,128)(2,1)} %reshape.350), calls=%async_computation.3 | async-start | bytes 5242880 | tf_op jit(solution)/shard_map/all_to_all | solution.py:129
  206.9 30.9 %copy-start.10 = (f32[64,8]{0,1:T(8,128)S(1)}, f32[64,8]{0,1:T(8,128)}, u32[]{:S(2)}) copy-start(f32[64,8]{0,1:T(8,128)} %param.21) | copy-start | bytes 6148
  230.1 40.4 %all-to-all-start.4 = ((bf16[128,80,128]{2,1,0:T(8,128)(2,1)}), bf16[128,80,128]{2,1,0:T(8,128)(2,1)}, u32[]{:S(2)}, u32[]{:S(2)}) async-start(bf16[128,80,128]{2,1,0:T(8,128)(2,1)} %reshape.352), calls=%async_computation.4 | async-start | bytes 5242880 | tf_op jit(solution)/shard_map/all_to_all | solution.py:129
  270.5 3.7 %copy-start.3 = (f32[64,1,10,8,128]{4,3,2,1,0:T(8,128)S(1)}, f32[64,1,10,8,128]{4,3,2,1,0:T(8,128)}, u32[]{:S(2)}) copy-start(f32[64,1,10,8,128]{4,3,2,1,0:T(8,128)} %convert_add_fusion.1) | copy-start | bytes 7864324
  276.9 4.2 %copy-start.4 = (f32[512,8,128]{2,1,0:T(8,128)S(1)}, f32[512,8,128]{2,1,0:T(8,128)}, u32[]{:S(2)}) copy-start(f32[512,8,128]{2,1,0:T(8,128)} %gather_fusion.1) | copy-start | bytes 6291460
  276.9 7.1 %copy-start.1 = (bf16[128,2048]{1,0:T(8,128)(2,1)S(1)}, bf16[128,2048]{1,0:T(8,128)(2,1)}, u32[]{:S(2)}) copy-start(bf16[128,2048]{1,0:T(8,128)(2,1)} %param.17) | copy-start | bytes 1572868
Sparse Core Ops, SparseCore 0:
  11.7 69.8 all-gather.1

commit v6 on v3

--- a/solution.py
+++ b/solution.py
@@ -1,7 +1,8 @@
 import jax
 import jax.numpy as jnp
 from jax import lax
-from jax.sharding import PartitionSpec as P
+from jax.sharding import Mesh, PartitionSpec as P
+
 
 HD = 128
 EXPERTS = 64
@@ -9,7 +10,7 @@
 TOP = 8
 
 
-def local(
+def layer(
     queries,
     new_entries,
     cache_entries,
@@ -67,16 +68,33 @@
 
     attention = lax.map(attend_request, (queries, new_entries, cache_entries, cache_lengths))
     attention = attention.reshape(req_local * new_len, width_local)
-    gathered = lax.all_to_all(attention, "exp", 0, 1, tiled=True)
-    full_proj = lax.all_gather(out_proj, "exp", axis=0, tiled=True)
-    projected = jnp.dot(gathered, full_proj, preferred_element_type=jnp.float32)
+    req_count = lax.axis_size("req")
+    z_count = lax.axis_size("z")
+    x_count = lax.axis_size("x")
+    x_here = lax.axis_index("x")
+    shifted = [out_proj]
+    for step in range(1, x_count):
+        pairs = [(i, (i + step) % x_count) for i in range(x_count)]
+        shifted.append(lax.ppermute(out_proj, "x", pairs))
+    stacked = jnp.stack(shifted)
+    order = (x_here - jnp.arange(x_count, dtype=jnp.int32)) % x_count
+    row_proj = stacked[order]
+    row_proj = row_proj.reshape(x_count * width_local, model_width)
+    rows_att = attention.reshape(z_count, x_count, tok_local, width_local)
+    rows_att = jnp.transpose(rows_att, (1, 0, 2, 3))
+    rows_att = lax.all_to_all(rows_att, "x", 0, 0, tiled=True)
+    rows_att = jnp.transpose(rows_att, (1, 2, 0, 3)).reshape(
+        z_count * tok_local, x_count * width_local
+    )
+    partial = jnp.dot(rows_att, row_proj, preferred_element_type=jnp.float32)
+    partial = partial.reshape(z_count, tok_local, model_width)
+    partial = lax.all_to_all(partial, "z", 0, 0, tiled=True)
+    projected = jnp.sum(partial, axis=0)
     hidden = residual.astype(jnp.float32) + projected
     attended = hidden.astype(jnp.bfloat16)
     mean_square = jnp.mean(hidden * hidden, axis=-1, keepdims=True)
     normed = (hidden * lax.rsqrt(mean_square + 1e-05) * norm_gain).astype(jnp.bfloat16)
-    req_count = lax.axis_size("req")
-    exp_count = lax.axis_size("exp")
-    devices = req_count * exp_count
+    devices = req_count * z_count * x_count
     half_units = FF // 2
     pieces = expert_in.shape[2] // half_units
     capacity = max(2, tok_local * TOP * 5 // (EXPERTS * 4))
@@ -96,7 +114,7 @@
     slot_rows = normed_fold[rows_table].reshape(EXPERTS, 1, capacity * folds, lanes)
     outgoing = jnp.broadcast_to(slot_rows, (EXPERTS, 2, capacity * folds, lanes))
     outgoing = outgoing.reshape(devices, pieces * capacity * folds, lanes)
-    arrived = lax.all_to_all(outgoing, ("req", "exp"), 0, 0, tiled=True)
+    arrived = lax.all_to_all(outgoing, ("req", "z", "x"), 0, 0, tiled=True)
     sources = arrived.shape[0]
     rows = arrived.reshape(sources * capacity, model_width)
     gate_part = jnp.dot(rows, expert_in[0, :, 0:half_units], preferred_element_type=jnp.float32)
@@ -104,7 +122,7 @@
     inner = (jax.nn.silu(gate_part) * up_part).astype(jnp.bfloat16)
     half_out = jnp.dot(inner, expert_down, preferred_element_type=jnp.float32).astype(jnp.bfloat16)
     back = half_out.reshape(sources, capacity * folds, lanes)
-    returned = lax.all_to_all(back, ("req", "exp"), 0, 0, tiled=True)
+    returned = lax.all_to_all(back, ("req", "z", "x"), 0, 0, tiled=True)
     halves = returned.reshape(EXPERTS, 2, capacity, folds, lanes)
     summed = (halves[:, 0].astype(jnp.float32) + halves[:, 1].astype(jnp.float32)).reshape(
         EXPERTS * capacity, folds, lanes
@@ -116,22 +134,29 @@
 
 
 def solution(mesh):
+    req_size, exp_size = mesh.devices.shape
+    x_size = 4 if exp_size % 4 == 0 else 1
+    sub_mesh = Mesh(
+        mesh.devices.reshape(req_size, exp_size // x_size, x_size), ("req", "z", "x")
+    )
+    exp = ("z", "x")
+    flat = ("req", "z", "x")
     return jax.shard_map(
-        local,
-        mesh=mesh,
+        layer,
+        mesh=sub_mesh,
         in_specs=(
-            P("req", None, "exp"),
-            P("req", None, None, "exp"),
-            P("req", None, None, "exp"),
+            P("req", None, exp),
+            P("req", None, None, exp),
+            P("req", None, None, exp),
             P("req"),
-            P("exp", None),
-            P(("req", "exp"), None),
+            P(exp, None),
+            P(flat, None),
             P(),
-            P(("req", "exp"), None),
-            P(("req", "exp"), None),
-            P(None, None, ("req", "exp")),
-            P(("req", "exp"), None),
+            P(flat, None),
+            P(flat, None),
+            P(None, None, flat),
+            P(flat, None),
         ),
-        out_specs=(P(("req", "exp"), None), P(("req", "exp"), None)),
+        out_specs=(P(flat, None), P(flat, None)),
         check_vma=False,
     )

time: 297 us -> 288 us (0.970)
  between operations: 14.2 us -> 0.81 us
  waiting for transfers between devices: 92.5 us -> 80.9 us
  starting transfers between devices: 16 us -> 22.2 us
  local copies, waits for them, and re-layouts: 41.9 us -> 47.3 us
  other arithmetic: 14.9 us -> 20.2 us
    all_gather x1 -> x0, waiting for transfers between devices: 28.3 us -> none  [local(): full_proj = lax.all_gather(out_proj, 'exp', axis=0, tiled=True)]
    all_to_all x2 -> x3, waiting for transfers between devices: 63.5 us -> 80.9 us  [the longest x1 60.9 us: layer(): returned = lax.all_to_all(back, ('req', 'z', 'x'), 0, 0, tiled=True)]
    all_to_all x2 -> x3, starting transfers between devices: 16 us -> 19.8 us  [the longest x1 8.7 us: layer(): returned = lax.all_to_all(back, ('req', 'z', 'x'), 0, 0, tiled=True)]
    gather x2 -> x3, local copies, waits for them, and re-layouts: 8.73 us -> 12.3 us  [the longest x1 5.38 us: layer(): picked = summed[positions] * gate_weights.reshape(-1)[:, None, None]]
    another operation x2 -> x3, other arithmetic: 1.24 us -> 4.37 us  [the longest x1 3.13 us: layer(): stacked = jnp.stack(shifted)]
  transfers between devices with their start and end apart: 3 -> 6, of which waited for: 3 -> 2; matrix products, arithmetic and copies ran while one was open for 12% -> 16% of each run, Pallas kernels for 0% -> 0%
where the time goes in v6:
time: 288 us; the launch traced here: 285 us
  waiting for transfers between devices  80.9 us (28%)
  blocking collectives  71.3 us (25%)
  local copies, waits for them, and re-layouts  47.3 us (16%)
  matrix products  41.8 us (15%)
  starting transfers between devices  22.2 us (8%)
  other arithmetic  20.2 us (7%)
    all_to_all x1, blocking collectives, layer(): arrived = lax.all_to_all(outgoing, ('req', 'z', 'x'), 0, 0, tiled=True)  71.3 us
    all_to_all x1, waiting for transfers between devices, layer(): returned = lax.all_to_all(back, ('req', 'z', 'x'), 0, 0, tiled=True)  60.9 us
    all_to_all x1, waiting for transfers between devices, layer(): partial = lax.all_to_all(partial, 'z', 0, 0, tiled=True)  20 us
    dot_general x2, matrix products, attend_request(): jnp.einsum('htj,jhd->thd', weights_bf, all_vals, preferred_element_type=j...  11.7 us
    dot_general x1, matrix products, layer(): jnp.dot(inner, expert_down, preferred_element_type=jnp.float32)  10.3 us
    reshape x1, local copies, waits for them, and re-layouts, layer(): back = half_out.reshape(sources, capacity * folds, lanes)  8.93 us
    reshape x1, local copies, waits for them, and re-layouts, layer(): rows = arrived.reshape(sources * capacity, model_width)  8.82 us
    all_to_all x1, starting transfers between devices, layer(): returned = lax.all_to_all(back, ('req', 'z', 'x'), 0, 0, tiled=True)  8.7 us
  transfers between devices with their start and end apart: 6, of which 2 were waited for; matrix products, arithmetic and copies ran while one was open for 16% of the time, Pallas kernels for 0%

profile of v6, /device:TPU:37, one launch (start us, length us, event | category | flops | bytes accessed | tf_op | source)
XLA Modules:
  0.0 284.7 jit_solution(6588463341825705375)
XLA Ops:
  3.0 34.1 %while.10 = (s32[]{:T(128)}, bf16[2,512,128]{2,1,0:T(8,128)(2,1)}, bf16[2,2,4096,128]{3,2,1,0:T(8,128)(2,1)}, bf16[2,2,512,128]{3,2,1,0:T(8,128)(2,1)}, s32[2]{0...) while((s32[]{:T(128)}, bf16[2,512,128]{2,1,0:T(8,128)(2,1)}, ...), condition=%wide.region_4.5_spmd, body=%wide.region_0.4_spmd.sunk | while | flops 1231948800 | bytes 70676728 | solution.py:69
  5.1 2.8 fusion.65
  13.3 5.9 %fusion.67 = bf16[1,512,128]{1,2,0:T(8,128)(2,1)S(1)} fusion(f32[1,512,1,1,1,1,512]{6,1,5,4,3,2,0:T(8,128)S(1)} %bitcast.155, f32[1,512,1,1,1,1,4096]{6,1,5,4,3,2,0:T(8,128)} %bitcast.153, f32[512]{0:T(512)S(1)} %reduce_max.27, bf16[512,1,128]{2,0,1:T(8,128)(2,1)S(1)} %dynamic-slice_bitcast_fusion.8, ...), kind=kOutput, calls=%fused_computation.21.clone.1 | convolution fusion | flops 613548032 | bytes 10752000 | tf_op jit(solution)/shard_map/while/body/eval_jaxpr/htj,jhd->thd/dot_general | solution.py:65
  22.1 2.8 fusion.65
  30.4 5.9 %fusion.67 = bf16[1,512,128]{1,2,0:T(8,128)(2,1)S(1)} fusion(f32[1,512,1,1,1,1,512]{6,1,5,4,3,2,0:T(8,128)S(1)} %bitcast.155, f32[1,512,1,1,1,1,4096]{6,1,5,4,3,2,0:T(8,128)} %bitcast.153, f32[512]{0:T(512)S(1)} %reduce_max.27, bf16[512,1,128]{2,0,1:T(8,128)(2,1)S(1)} %dynamic-slice_bitcast_fusion.8, ...), kind=kOutput, calls=%fused_computation.21.clone.1 | convolution fusion | flops 613548032 | bytes 10752000 | tf_op jit(solution)/shard_map/while/body/eval_jaxpr/htj,jhd->thd/dot_general | solution.py:65
  38.8 6.1 %all-to-all-start = ((bf16[4,4,64,128]{3,2,1,0:T(8,128)(2,1)}), bf16[4,4,64,128]{3,2,1,0:T(8,128)(2,1)S(1)}, u32[]{:S(2)}, u32[]{:S(2)}) async-start(bf16[4,4,64,128]{3,2,1,0:T(8,128)(2,1)} %copy.32), calls=%async_computation | async-start | bytes 524288 | tf_op jit(solution)/shard_map/all_to_all | solution.py:85
  45.2 3.1 %pad_maximum_fusion = bf16[4,128,2048]{2,1,0:T(8,128)(2,1)} fusion(bf16[1,128,2048]{2,1,0:T(8,128)(2,1)} %bitcast.21, bf16[1,128,2048]{2,1,0:T(8,128)(2,1)} %bitcast.20, bf16[1,128,2048]{2,1,0:T(8,128)(2,1)} %bitcast.19, bf16[1,128,2048]{2,1,0:T(8,128)(2,1)} %bitcast.161), kind=kLoop, calls=%fused_computation.43 | loop fusion | flops 3145728 | bytes 4194304 | tf_op jit(solution)/shard_map/stack | solution.py:79
  48.4 3.6 %gather_fusion = bf16[4,128,2048]{2,1,0:T(8,128)(2,1)} fusion(bf16[4,128,2048]{2,1,0:T(8,128)(2,1)} %pad_maximum_fusion, s32[1024]{0:T(1024)S(1)} %pad_clamp_fusion.2), kind=kCustom, calls=%fused_computation | custom fusion | bytes 4194320 | tf_op jit(solution)/shard_map/gather | solution.py:81
  51.9 3.7 %convolution_bitcast_fusion = f32[4,64,2048]{2,1,0:T(8,128)} fusion(bf16[4,128,2048]{2,1,0:T(8,128)(2,1)} %gather_fusion, bf16[4,4,64,128]{3,2,1,0:T(8,128)(2,1)S(1)} %all-to-all-done), kind=kOutput, calls=%fused_computation.42 | convolution fusion | flops 536870912 | bytes 4456448 | tf_op jit(solution)/shard_map/dot_general | solution.py:89
  55.6 5.0 %all-to-all-start.1 = ((f32[4,64,2048]{2,1,0:T(8,128)}), f32[4,64,2048]{2,1,0:T(8,128)}, u32[]{:S(2)}, u32[]{:S(2)}) async-start(f32[4,64,2048]{2,1,0:T(8,128)} %convolution_bitcast_fusion), calls=%async_computation.1 | async-start | bytes 4194304 | tf_op jit(solution)/shard_map/all_to_all | solution.py:91
  62.4 2.4 scatter_custom_fusion
  64.9 20.0 %all-to-all-done.1 = f32[4,64,2048]{2,1,0:T(8,128)} async-done(((f32[4,64,2048]{2,1,0:T(8,128)}), f32[4,64,2048]{2,1,0:T(8,128)}, u32[]{:S(2)}, u32[]{:S(2)}) %all-to-all-start.1) | async-done | bytes 2097184 | tf_op jit(solution)/shard_map/all_to_all | solution.py:91
  87.6 3.3 %gather_fusion.1 = bf16[640,16,128]{2,1,0:T(8,128)(2,1)} fusion(bf16[65,16,128]{2,1,0:T(8,128)(2,1)S(1)} %concatenate.42, s32[1024]{0:T(1024)S(1)} %pad_clamp_fusion.1), kind=kCustom, calls=%fused_computation.1 | custom fusion | bytes 5245440 | tf_op jit(solution)/shard_map/gather | solution.py:114
  91.0 2.6 broadcast_in_dim.52
  93.6 71.3 %all_to_all.20 = bf16[128,160,128]{2,1,0:T(8,128)(2,1)} all-to-all(bf16[128,160,128]{2,1,0:T(8,128)(2,1)S(1)} %bitcast.156), channel_id=1, replica_groups=mesh['req'=8,'z'=4,'x'=4] {'req','z','x'}, dimensions={0} | all-to-all | bytes 10485760 | tf_op jit(solution)/shard_map/all_to_all | solution.py:117
  164.9 8.8 %reshape.363 = bf16[1280,2048]{1,0:T(8,128)(2,1)} reshape(bf16[128,160,128]{2,1,0:T(8,128)(2,1)} %all_to_all.20) | data formatting | bytes 10485760 | tf_op jit(solution)/shard_map/reshape | solution.py:119
  173.7 7.5 %fusion.33 = f32[1280,512]{1,0:T(8,128)} fusion(bf16[1280,2048]{1,0:T(8,128)(2,1)} %reshape.363, bf16[2,2048,512]{2,1,0:T(8,128)(2,1)} %param.22), kind=kOutput, calls=%fused_computation.46 | convolution fusion | flops 2684354560 | bytes 9961472 | tf_op jit(solution)/shard_map/dot_general | solution.py:120
  181.2 10.3 %convolution_convert_fusion = bf16[1280,2048]{1,0:T(8,128)(2,1)} fusion(bf16[512,2048]{1,0:T(8,128)(2,1)S(1)} %copy-done, bf16[1280,2048]{1,0:T(8,128)(2,1)} %reshape.363, f32[1280,512]{1,0:T(8,128)} %fusion.33, bf16[2,2048,512]{2,1,0:T(8,128)(2,1)} %param.22), kind=kOutput, calls=%fused_computation.37 | convolution fusion | flops 5375262720 | bytes 17301504 | tf_op jit(solution)/shard_map/dot_general | solution.py:123
  191.6 8.9 %reshape.364 = bf16[128,160,128]{2,1,0:T(8,128)(2,1)} reshape(bf16[1280,2048]{1,0:T(8,128)(2,1)} %convolution_convert_fusion) | data formatting | bytes 10485760 | tf_op jit(solution)/shard_map/reshape | solution.py:124
  200.5 8.7 %all-to-all-start.3 = ((bf16[128,160,128]{2,1,0:T(8,128)(2,1)}), bf16[128,160,128]{2,1,0:T(8,128)(2,1)}, u32[]{:S(2)}, u32[]{:S(2)}) async-start(bf16[128,160,128]{2,1,0:T(8,128)(2,1)} %reshape.364), calls=%async_computation.3 | async-start | bytes 10485760 | tf_op jit(solution)/shard_map/all_to_all | solution.py:125
  209.3 60.9 %all-to-all-done.3 = bf16[128,160,128]{2,1,0:T(8,128)(2,1)} async-done(((bf16[128,160,128]{2,1,0:T(8,128)(2,1)}), bf16[128,160,128]{2,1,0:T(8,128)(2,1)}, u32[]{:S(2)}, u32[]{:S(2)}) %all-to-all-start.3) | async-done | bytes 5242912 | tf_op jit(solution)/shard_map/all_to_all | solution.py:125
  270.2 5.6 %convert_add_fusion = f32[64,1,10,16,128]{4,3,2,1,0:T(8,128)} fusion(bf16[64,2,10,16,128]{4,3,2,1,0:T(8,128)(2,1)} %bitcast.33), kind=kLoop, calls=%fused_computation.38 | loop fusion | flops 3932160 | bytes 10485760 | tf_op jit(solution)/shard_map/add | solution.py:127
  275.9 5.4 %gather_fusion.2 = f32[512,16,128]{2,1,0:T(8,128)} fusion(f32[640,16,128]{2,1,0:T(8,128)} %bitcast.157, s32[1024]{0:T(1024)S(1)} %pad_clamp_fusion), kind=kCustom, calls=%fused_computation.2 | custom fusion | bytes 8390656 | tf_op jit(solution)/shard_map/gather | solution.py:130
  281.2 2.6 multiply_reduce_fusion
  (81 shorter events, 26.4 us)
Async XLA Ops:
  0.6 180.6 %copy-start = (bf16[512,2048]{1,0:T(8,128)(2,1)S(1)}, bf16[512,2048]{1,0:T(8,128)(2,1)}, u32[]{:S(2)}) copy-start(bf16[512,2048]{1,0:T(8,128)(2,1)} %param.23) | copy-start | bytes 6291460
  0.6 44.6 %collective-permute-start = (bf16[128,2048]{1,0:T(8,128)(2,1)}, bf16[128,2048]{1,0:T(8,128)(2,1)}, u32[]{:S(2)}, u32[]{:S(2)}) collective-permute-start(bf16[128,2048]{1,0:T(8,128)(2,1)} %param.17), channel_id=1, source_target_pairs={{0,1},{1,2},{2,3},{3,0},{4,5},{5,6},{6,7},{7,4},{8,9},{9,10},{10,1... | collective-permute-start | bytes 1572872 | tf_op jit(solution)/shard_map/ppermute | solution.py:78
  1.6 43.6 %collective-permute-start.1 = (bf16[128,2048]{1,0:T(8,128)(2,1)}, bf16[128,2048]{1,0:T(8,128)(2,1)}, u32[]{:S(2)}, u32[]{:S(2)}) collective-permute-start(bf16[128,2048]{1,0:T(8,128)(2,1)} %param.17), channel_id=1, source_target_pairs={{0,2},{1,3},{2,0},{3,1},{4,6},{5,7},{6,4},{7,5},{8,10},{9,11},{10,... | collective-permute-start | bytes 1572872 | tf_op jit(solution)/shard_map/ppermute | solution.py:78
  2.2 43.1 %collective-permute-start.2 = (bf16[128,2048]{1,0:T(8,128)(2,1)}, bf16[128,2048]{1,0:T(8,128)(2,1)}, u32[]{:S(2)}, u32[]{:S(2)}) collective-permute-start(bf16[128,2048]{1,0:T(8,128)(2,1)} %param.17), channel_id=1, source_target_pairs={{0,3},{1,0},{2,1},{3,2},{4,7},{5,4},{6,5},{7,6},{8,11},{9,8},{10,9... | collective-permute-start | bytes 1572872 | tf_op jit(solution)/shard_map/ppermute | solution.py:78
  3.0 41.9 %copy-start.6 = (s32[64,8]{0,1:T(8,128)S(1)}, s32[64,8]{0,1:T(8,128)}, u32[]{:S(2)}) copy-start(s32[64,8]{0,1:T(8,128)} %param.20) | copy-start | bytes 6148
  5.0 2.8 copy-start.2
  7.9 3.2 %copy-start.1 = (f32[512,4096]{1,0:T(8,128)}, f32[512,4096]{1,0:T(8,128)S(1)}, u32[]{:S(2)}) copy-start(f32[512,4096]{1,0:T(8,128)S(1)} %get-tuple-element.95) | copy-start | bytes 25165828 | tf_op jit(solution)/shard_map/while
  13.3 6.0 %copy-start.4 = (bf16[2,512,128]{2,1,0:T(8,128)(2,1)S(1)}, bf16[2,512,128]{2,1,0:T(8,128)(2,1)}, u32[]{:S(2)}) copy-start(bf16[2,512,128]{2,1,0:T(8,128)(2,1)} %get-tuple-element.108) | copy-start | bytes 786436 | tf_op jit(solution)/shard_map/while
  19.4 0.7 copy-start.5
  22.1 2.8 copy-start.2
  24.9 3.2 %copy-start.1 = (f32[512,4096]{1,0:T(8,128)}, f32[512,4096]{1,0:T(8,128)S(1)}, u32[]{:S(2)}) copy-start(f32[512,4096]{1,0:T(8,128)S(1)} %get-tuple-element.95) | copy-start | bytes 25165828 | tf_op jit(solution)/shard_map/while
  30.4 6.0 %copy-start.4 = (bf16[2,512,128]{2,1,0:T(8,128)(2,1)S(1)}, bf16[2,512,128]{2,1,0:T(8,128)(2,1)}, u32[]{:S(2)}) copy-start(bf16[2,512,128]{2,1,0:T(8,128)(2,1)} %get-tuple-element.108) | copy-start | bytes 786436 | tf_op jit(solution)/shard_map/while
  36.4 0.7 copy-start.5
  38.8 13.1 %all-to-all-start = ((bf16[4,4,64,128]{3,2,1,0:T(8,128)(2,1)}), bf16[4,4,64,128]{3,2,1,0:T(8,128)(2,1)S(1)}, u32[]{:S(2)}, u32[]{:S(2)}) async-start(bf16[4,4,64,128]{3,2,1,0:T(8,128)(2,1)} %copy.32), calls=%async_computation | async-start | bytes 524288 | tf_op jit(solution)/shard_map/all_to_all | solution.py:85
  55.6 31.0 %copy-start.3 = (bf16[64,2048]{1,0:T(8,128)(2,1)S(1)}, bf16[64,2048]{1,0:T(8,128)(2,1)}, u32[]{:S(2)}) copy-start(bf16[64,2048]{1,0:T(8,128)(2,1)} %param.18) | copy-start | bytes 786436
  55.6 31.2 %copy-start.7 = (f32[2048]{0:T(1024)S(1)}, f32[2048]{0:T(1024)}, u32[]{:S(2)}) copy-start(f32[2048]{0:T(1024)} %param.19) | copy-start | bytes 24580
  55.6 29.3 %all-to-all-start.1 = ((f32[4,64,2048]{2,1,0:T(8,128)}), f32[4,64,2048]{2,1,0:T(8,128)}, u32[]{:S(2)}, u32[]{:S(2)}) async-start(f32[4,64,2048]{2,1,0:T(8,128)} %convolution_bitcast_fusion), calls=%async_computation.1 | async-start | bytes 4194304 | tf_op jit(solution)/shard_map/all_to_all | solution.py:91
  200.5 8.7 %copy-start.8 = (f32[64,8]{0,1:T(8,128)S(1)}, f32[64,8]{0,1:T(8,128)}, u32[]{:S(2)}) copy-start(f32[64,8]{0,1:T(8,128)} %param.21) | copy-start | bytes 6148
  200.5 69.7 %all-to-all-start.3 = ((bf16[128,160,128]{2,1,0:T(8,128)(2,1)}), bf16[128,160,128]{2,1,0:T(8,128)(2,1)}, u32[]{:S(2)}, u32[]{:S(2)}) async-start(bf16[128,160,128]{2,1,0:T(8,128)(2,1)} %reshape.364), calls=%async_computation.3 | async-start | bytes 10485760 | tf_op jit(solution)/shard_map/all_to_all | solution.py:125

commit v7 on v6

--- a/solution.py
+++ b/solution.py
@@ -76,20 +76,20 @@
     for step in range(1, x_count):
         pairs = [(i, (i + step) % x_count) for i in range(x_count)]
         shifted.append(lax.ppermute(out_proj, "x", pairs))
-    stacked = jnp.stack(shifted)
-    order = (x_here - jnp.arange(x_count, dtype=jnp.int32)) % x_count
-    row_proj = stacked[order]
+    row_proj = jnp.stack(shifted)
     row_proj = row_proj.reshape(x_count * width_local, model_width)
     rows_att = attention.reshape(z_count, x_count, tok_local, width_local)
     rows_att = jnp.transpose(rows_att, (1, 0, 2, 3))
     rows_att = lax.all_to_all(rows_att, "x", 0, 0, tiled=True)
+    order = (x_here - jnp.arange(x_count, dtype=jnp.int32)) % x_count
+    rows_att = rows_att[order]
     rows_att = jnp.transpose(rows_att, (1, 2, 0, 3)).reshape(
         z_count * tok_local, x_count * width_local
     )
     partial = jnp.dot(rows_att, row_proj, preferred_element_type=jnp.float32)
-    partial = partial.reshape(z_count, tok_local, model_width)
+    partial = partial.astype(jnp.bfloat16).reshape(z_count, tok_local, model_width)
     partial = lax.all_to_all(partial, "z", 0, 0, tiled=True)
-    projected = jnp.sum(partial, axis=0)
+    projected = jnp.sum(partial.astype(jnp.float32), axis=0)
     hidden = residual.astype(jnp.float32) + projected
     attended = hidden.astype(jnp.bfloat16)
     mean_square = jnp.mean(hidden * hidden, axis=-1, keepdims=True)

time: 288 us -> 272 us (0.944)
  waiting for transfers between devices: 80.9 us -> 69.9 us
  other arithmetic: 20.2 us -> 17.3 us
    all_to_all x1, waiting for transfers between devices: 20 us -> 8.09 us  [layer(): partial = lax.all_to_all(partial, 'z', 0, 0, tiled=True)]
    gather x1, local copies, waits for them, and re-layouts: 3.56 us -> 0.6 us  [layer(): rows_att = rows_att[order]]
  transfers between devices with their start and end apart: 6 -> 6, of which waited for: 2 -> 3; matrix products, arithmetic and copies ran while one was open for 16% -> 15% of each run, Pallas kernels for 0% -> 0%
where the time goes in v7:
time: 272 us; the launch traced here: 269 us
  blocking collectives  74.1 us (27%)
  waiting for transfers between devices  69.9 us (26%)
  local copies, waits for them, and re-layouts  44.6 us (16%)
  matrix products  39.9 us (15%)
  starting transfers between devices  22 us (8%)
  other arithmetic  17.3 us (6%)
    all_to_all x1, blocking collectives, layer(): arrived = lax.all_to_all(outgoing, ('req', 'z', 'x'), 0, 0, tiled=True)  74.1 us
    all_to_all x1, waiting for transfers between devices, layer(): returned = lax.all_to_all(back, ('req', 'z', 'x'), 0, 0, tiled=True)  60.9 us
    dot_general x2, matrix products, attend_request(): jnp.einsum('htj,jhd->thd', weights_bf, all_vals, preferred_element_type=j...  11.7 us
    dot_general x1, matrix products, layer(): jnp.dot(inner, expert_down, preferred_element_type=jnp.float32)  10.3 us
    reshape x1, local copies, waits for them, and re-layouts, layer(): back = half_out.reshape(sources, capacity * folds, lanes)  8.93 us
    reshape x1, local copies, waits for them, and re-layouts, layer(): rows = arrived.reshape(sources * capacity, model_width)  8.82 us
    all_to_all x1, starting transfers between devices, layer(): returned = lax.all_to_all(back, ('req', 'z', 'x'), 0, 0, tiled=True)  8.7 us
    all_to_all x1, waiting for transfers between devices, layer(): partial = lax.all_to_all(partial, 'z', 0, 0, tiled=True)  8.09 us
  transfers between devices with their start and end apart: 6, of which 3 were waited for; matrix products, arithmetic and copies ran while one was open for 15% of the time, Pallas kernels for 0%

profile of v7, /device:TPU:37, one launch (start us, length us, event | category | flops | bytes accessed | tf_op | source)
XLA Modules:
  0.0 268.8 jit_solution(3195606890034771639)
XLA Ops:
  3.0 34.1 %while.10 = (s32[]{:T(128)}, bf16[2,512,128]{2,1,0:T(8,128)(2,1)}, bf16[2,2,4096,128]{3,2,1,0:T(8,128)(2,1)}, bf16[2,2,512,128]{3,2,1,0:T(8,128)(2,1)}, s32[2]{0...) while((s32[]{:T(128)}, bf16[2,512,128]{2,1,0:T(8,128)(2,1)}, ...), condition=%wide.region_4.5_spmd, body=%wide.region_0.4_spmd.sunk | while | flops 1231948800 | bytes 70676728 | solution.py:69
  5.1 2.8 %fusion.66 = (f32[512]{0:T(512)S(1)}, f32[512,4096]{1,0:T(8,128)S(1)}) fusion(bf16[2,2,4096,128]{3,2,1,0:T(8,128)(2,1)} %get-tuple-element.118, s32[]{:T(128)} %get-tuple-element.107, bf16[2,512,128]{2,1,0:T(8,128)(2,1)} %get-tuple-element.121, pred[4096]{0:T(1024)(128)(4,1)S(1)} %iota_compare_fusion.5), kind=kOutput, calls=%fused_computation.90.clone.1 | convolution fusion | flops 543161856 | bytes 9575424 | tf_op jit(solution)/shard_map/while/body/eval_jaxpr/thd,jhd->htj/dot_general | solution.py:41
  13.3 5.9 %fusion.68 = bf16[1,512,128]{1,2,0:T(8,128)(2,1)S(1)} fusion(f32[1,512,1,1,1,1,512]{6,1,5,4,3,2,0:T(8,128)S(1)} %bitcast.154, f32[1,512,1,1,1,1,4096]{6,1,5,4,3,2,0:T(8,128)} %bitcast.152, f32[512]{0:T(512)S(1)} %reduce_max.27, bf16[512,1,128]{2,0,1:T(8,128)(2,1)S(1)} %dynamic-slice_bitcast_fusion.8, ...), kind=kOutput, calls=%fused_computation.21.clone.1 | convolution fusion | flops 613548032 | bytes 10752000 | tf_op jit(solution)/shard_map/while/body/eval_jaxpr/htj,jhd->thd/dot_general | solution.py:65
  22.1 2.8 %fusion.66 = (f32[512]{0:T(512)S(1)}, f32[512,4096]{1,0:T(8,128)S(1)}) fusion(bf16[2,2,4096,128]{3,2,1,0:T(8,128)(2,1)} %get-tuple-element.118, s32[]{:T(128)} %get-tuple-element.107, bf16[2,512,128]{2,1,0:T(8,128)(2,1)} %get-tuple-element.121, pred[4096]{0:T(1024)(128)(4,1)S(1)} %iota_compare_fusion.5), kind=kOutput, calls=%fused_computation.90.clone.1 | convolution fusion | flops 543161856 | bytes 9575424 | tf_op jit(solution)/shard_map/while/body/eval_jaxpr/thd,jhd->htj/dot_general | solution.py:41
  30.4 5.9 %fusion.68 = bf16[1,512,128]{1,2,0:T(8,128)(2,1)S(1)} fusion(f32[1,512,1,1,1,1,512]{6,1,5,4,3,2,0:T(8,128)S(1)} %bitcast.154, f32[1,512,1,1,1,1,4096]{6,1,5,4,3,2,0:T(8,128)} %bitcast.152, f32[512]{0:T(512)S(1)} %reduce_max.27, bf16[512,1,128]{2,0,1:T(8,128)(2,1)S(1)} %dynamic-slice_bitcast_fusion.8, ...), kind=kOutput, calls=%fused_computation.21.clone.1 | convolution fusion | flops 613548032 | bytes 10752000 | tf_op jit(solution)/shard_map/while/body/eval_jaxpr/htj,jhd->thd/dot_general | solution.py:65
  37.1 1.7 copy.25
  38.8 6.1 %all-to-all-start = ((bf16[4,4,64,128]{3,2,1,0:T(8,128)(2,1)}), bf16[4,4,64,128]{3,2,1,0:T(8,128)(2,1)S(1)}, u32[]{:S(2)}, u32[]{:S(2)}) async-start(bf16[4,4,64,128]{3,2,1,0:T(8,128)(2,1)} %copy.25), calls=%async_computation | async-start | bytes 524288 | tf_op jit(solution)/shard_map/all_to_all | solution.py:83
  48.6 1.8 pad_maximum_fusion
  50.4 1.7 convolution_convert_fusion.1
  52.1 4.9 %all-to-all-start.1 = ((bf16[4,64,2048]{2,1,0:T(8,128)(2,1)}), bf16[4,64,2048]{2,1,0:T(8,128)(2,1)S(1)}, u32[]{:S(2)}, u32[]{:S(2)}) async-start(bf16[4,64,2048]{2,1,0:T(8,128)(2,1)} %bitcast.159), calls=%async_computation.1 | async-start | bytes 2097152 | tf_op jit(solution)/shard_map/all_to_all | solution.py:91
  57.2 2.4 scatter_custom_fusion
  59.6 8.1 %all-to-all-done.1 = bf16[4,64,2048]{2,1,0:T(8,128)(2,1)S(1)} async-done(((bf16[4,64,2048]{2,1,0:T(8,128)(2,1)}), bf16[4,64,2048]{2,1,0:T(8,128)(2,1)S(1)}, u32[]{:S(2)}, u32[]{:S(2)}) %all-to-all-start.1) | async-done | bytes 1048608 | tf_op jit(solution)/shard_map/all_to_all | solution.py:91
  68.9 3.3 %gather_fusion.1 = bf16[640,16,128]{2,1,0:T(8,128)(2,1)} fusion(bf16[65,16,128]{2,1,0:T(8,128)(2,1)S(1)} %concatenate.42, s32[1024]{0:T(1024)S(1)} %pad_clamp_fusion.1), kind=kCustom, calls=%fused_computation.1 | custom fusion | bytes 5245440 | tf_op jit(solution)/shard_map/gather | solution.py:114
  72.3 2.6 broadcast_in_dim.52
  74.9 74.1 %all_to_all.20 = bf16[128,160,128]{2,1,0:T(8,128)(2,1)} all-to-all(bf16[128,160,128]{2,1,0:T(8,128)(2,1)S(1)} %bitcast.155), channel_id=1, replica_groups=mesh['req'=8,'z'=4,'x'=4] {'req','z','x'}, dimensions={0} | all-to-all | bytes 10485760 | tf_op jit(solution)/shard_map/all_to_all | solution.py:117
  149.0 8.8 %reshape.370 = bf16[1280,2048]{1,0:T(8,128)(2,1)} reshape(bf16[128,160,128]{2,1,0:T(8,128)(2,1)} %all_to_all.20) | data formatting | bytes 10485760 | tf_op jit(solution)/shard_map/reshape | solution.py:119
  157.9 7.6 %fusion.32 = f32[1280,512]{1,0:T(8,128)} fusion(bf16[1280,2048]{1,0:T(8,128)(2,1)} %reshape.370, bf16[2,2048,512]{2,1,0:T(8,128)(2,1)} %param.22), kind=kOutput, calls=%fused_computation.45 | convolution fusion | flops 2684354560 | bytes 9961472 | tf_op jit(solution)/shard_map/dot_general | solution.py:120
  165.4 10.3 %convolution_convert_fusion = bf16[1280,2048]{1,0:T(8,128)(2,1)} fusion(bf16[512,2048]{1,0:T(8,128)(2,1)S(1)} %copy-done, bf16[1280,2048]{1,0:T(8,128)(2,1)} %reshape.370, f32[1280,512]{1,0:T(8,128)} %fusion.32, bf16[2,2048,512]{2,1,0:T(8,128)(2,1)} %param.22), kind=kOutput, calls=%fused_computation.37 | convolution fusion | flops 5375262720 | bytes 17301504 | tf_op jit(solution)/shard_map/dot_general | solution.py:123
  175.7 8.9 %reshape.371 = bf16[128,160,128]{2,1,0:T(8,128)(2,1)} reshape(bf16[1280,2048]{1,0:T(8,128)(2,1)} %convolution_convert_fusion) | data formatting | bytes 10485760 | tf_op jit(solution)/shard_map/reshape | solution.py:124
  184.7 8.7 %all-to-all-start.3 = ((bf16[128,160,128]{2,1,0:T(8,128)(2,1)}), bf16[128,160,128]{2,1,0:T(8,128)(2,1)}, u32[]{:S(2)}, u32[]{:S(2)}) async-start(bf16[128,160,128]{2,1,0:T(8,128)(2,1)} %reshape.371), calls=%async_computation.3 | async-start | bytes 10485760 | tf_op jit(solution)/shard_map/all_to_all | solution.py:125
  193.5 60.9 %all-to-all-done.3 = bf16[128,160,128]{2,1,0:T(8,128)(2,1)} async-done(((bf16[128,160,128]{2,1,0:T(8,128)(2,1)}), bf16[128,160,128]{2,1,0:T(8,128)(2,1)}, u32[]{:S(2)}, u32[]{:S(2)}) %all-to-all-start.3) | async-done | bytes 5242912 | tf_op jit(solution)/shard_map/all_to_all | solution.py:125
  254.4 5.6 %convert_add_fusion = f32[64,1,10,16,128]{4,3,2,1,0:T(8,128)} fusion(bf16[64,2,10,16,128]{4,3,2,1,0:T(8,128)(2,1)} %bitcast.32), kind=kLoop, calls=%fused_computation.38 | loop fusion | flops 3932160 | bytes 10485760 | tf_op jit(solution)/shard_map/add | solution.py:127
  260.0 5.4 %gather_fusion.2 = f32[512,16,128]{2,1,0:T(8,128)} fusion(f32[640,16,128]{2,1,0:T(8,128)} %bitcast.156, s32[1024]{0:T(1024)S(1)} %pad_clamp_fusion), kind=kCustom, calls=%fused_computation.2 | custom fusion | bytes 8390656 | tf_op jit(solution)/shard_map/gather | solution.py:130
  265.4 2.6 multiply_reduce_fusion
  (82 shorter events, 24.8 us)
Async XLA Ops:
  0.6 164.8 %copy-start = (bf16[512,2048]{1,0:T(8,128)(2,1)S(1)}, bf16[512,2048]{1,0:T(8,128)(2,1)}, u32[]{:S(2)}) copy-start(bf16[512,2048]{1,0:T(8,128)(2,1)} %param.23) | copy-start | bytes 6291460
  0.6 47.9 %collective-permute-start = (bf16[128,2048]{1,0:T(8,128)(2,1)}, bf16[128,2048]{1,0:T(8,128)(2,1)}, u32[]{:S(2)}, u32[]{:S(2)}) collective-permute-start(bf16[128,2048]{1,0:T(8,128)(2,1)} %param.17), channel_id=1, source_target_pairs={{0,1},{1,2},{2,3},{3,0},{4,5},{5,6},{6,7},{7,4},{8,9},{9,10},{10,1... | collective-permute-start | bytes 1572872 | tf_op jit(solution)/shard_map/ppermute | solution.py:78
  1.6 46.9 %collective-permute-start.1 = (bf16[128,2048]{1,0:T(8,128)(2,1)}, bf16[128,2048]{1,0:T(8,128)(2,1)}, u32[]{:S(2)}, u32[]{:S(2)}) collective-permute-start(bf16[128,2048]{1,0:T(8,128)(2,1)} %param.17), channel_id=1, source_target_pairs={{0,2},{1,3},{2,0},{3,1},{4,6},{5,7},{6,4},{7,5},{8,10},{9,11},{10,... | collective-permute-start | bytes 1572872 | tf_op jit(solution)/shard_map/ppermute | solution.py:78
  2.2 46.4 %collective-permute-start.2 = (bf16[128,2048]{1,0:T(8,128)(2,1)}, bf16[128,2048]{1,0:T(8,128)(2,1)}, u32[]{:S(2)}, u32[]{:S(2)}) collective-permute-start(bf16[128,2048]{1,0:T(8,128)(2,1)} %param.17), channel_id=1, source_target_pairs={{0,3},{1,0},{2,1},{3,2},{4,7},{5,4},{6,5},{7,6},{8,11},{9,8},{10,9... | collective-permute-start | bytes 1572872 | tf_op jit(solution)/shard_map/ppermute | solution.py:78
  3.0 41.9 %copy-start.6 = (s32[64,8]{0,1:T(8,128)S(1)}, s32[64,8]{0,1:T(8,128)}, u32[]{:S(2)}) copy-start(s32[64,8]{0,1:T(8,128)} %param.20) | copy-start | bytes 6148
  5.0 2.8 %copy-start.2 = (bf16[2,512,128]{2,1,0:T(8,128)(2,1)S(1)}, bf16[2,512,128]{2,1,0:T(8,128)(2,1)}, u32[]{:S(2)}) copy-start(bf16[2,512,128]{2,1,0:T(8,128)(2,1)} %get-tuple-element.121) | copy-start | bytes 786436 | tf_op jit(solution)/shard_map/while
  7.9 3.2 %copy-start.1 = (f32[512,4096]{1,0:T(8,128)}, f32[512,4096]{1,0:T(8,128)S(1)}, u32[]{:S(2)}) copy-start(f32[512,4096]{1,0:T(8,128)S(1)} %get-tuple-element.95) | copy-start | bytes 25165828 | tf_op jit(solution)/shard_map/while
  13.3 6.0 %copy-start.4 = (bf16[2,512,128]{2,1,0:T(8,128)(2,1)S(1)}, bf16[2,512,128]{2,1,0:T(8,128)(2,1)}, u32[]{:S(2)}) copy-start(bf16[2,512,128]{2,1,0:T(8,128)(2,1)} %get-tuple-element.108) | copy-start | bytes 786436 | tf_op jit(solution)/shard_map/while
  19.4 0.7 copy-start.5
  22.1 2.8 %copy-start.2 = (bf16[2,512,128]{2,1,0:T(8,128)(2,1)S(1)}, bf16[2,512,128]{2,1,0:T(8,128)(2,1)}, u32[]{:S(2)}) copy-start(bf16[2,512,128]{2,1,0:T(8,128)(2,1)} %get-tuple-element.121) | copy-start | bytes 786436 | tf_op jit(solution)/shard_map/while
  24.9 3.2 %copy-start.1 = (f32[512,4096]{1,0:T(8,128)}, f32[512,4096]{1,0:T(8,128)S(1)}, u32[]{:S(2)}) copy-start(f32[512,4096]{1,0:T(8,128)S(1)} %get-tuple-element.95) | copy-start | bytes 25165828 | tf_op jit(solution)/shard_map/while
  30.4 6.0 %copy-start.4 = (bf16[2,512,128]{2,1,0:T(8,128)(2,1)S(1)}, bf16[2,512,128]{2,1,0:T(8,128)(2,1)}, u32[]{:S(2)}) copy-start(bf16[2,512,128]{2,1,0:T(8,128)(2,1)} %get-tuple-element.108) | copy-start | bytes 786436 | tf_op jit(solution)/shard_map/while
  36.4 0.7 copy-start.5
  38.8 9.0 %all-to-all-start = ((bf16[4,4,64,128]{3,2,1,0:T(8,128)(2,1)}), bf16[4,4,64,128]{3,2,1,0:T(8,128)(2,1)S(1)}, u32[]{:S(2)}, u32[]{:S(2)}) async-start(bf16[4,4,64,128]{3,2,1,0:T(8,128)(2,1)} %copy.25), calls=%async_computation | async-start | bytes 524288 | tf_op jit(solution)/shard_map/all_to_all | solution.py:83
  50.4 17.5 %copy-start.3 = (bf16[64,2048]{1,0:T(8,128)(2,1)S(1)}, bf16[64,2048]{1,0:T(8,128)(2,1)}, u32[]{:S(2)}) copy-start(bf16[64,2048]{1,0:T(8,128)(2,1)} %param.18) | copy-start | bytes 786436
  50.4 17.7 %copy-start.7 = (f32[2048]{0:T(1024)S(1)}, f32[2048]{0:T(1024)}, u32[]{:S(2)}) copy-start(f32[2048]{0:T(1024)} %param.19) | copy-start | bytes 24580
  52.1 15.6 %all-to-all-start.1 = ((bf16[4,64,2048]{2,1,0:T(8,128)(2,1)}), bf16[4,64,2048]{2,1,0:T(8,128)(2,1)S(1)}, u32[]{:S(2)}, u32[]{:S(2)}) async-start(bf16[4,64,2048]{2,1,0:T(8,128)(2,1)} %bitcast.159), calls=%async_computation.1 | async-start | bytes 2097152 | tf_op jit(solution)/shard_map/all_to_all | solution.py:91
  184.7 8.7 %copy-start.8 = (f32[64,8]{0,1:T(8,128)S(1)}, f32[64,8]{0,1:T(8,128)}, u32[]{:S(2)}) copy-start(f32[64,8]{0,1:T(8,128)} %param.21) | copy-start | bytes 6148
  184.7 69.7 %all-to-all-start.3 = ((bf16[128,160,128]{2,1,0:T(8,128)(2,1)}), bf16[128,160,128]{2,1,0:T(8,128)(2,1)}, u32[]{:S(2)}, u32[]{:S(2)}) async-start(bf16[128,160,128]{2,1,0:T(8,128)(2,1)} %reshape.371), calls=%async_computation.3 | async-start | bytes 10485760 | tf_op jit(solution)/shard_map/all_to_all | solution.py:125

commit v8 on v7

--- a/solution.py
+++ b/solution.py
@@ -116,11 +116,15 @@
     outgoing = outgoing.reshape(devices, pieces * capacity * folds, lanes)
     arrived = lax.all_to_all(outgoing, ("req", "z", "x"), 0, 0, tiled=True)
     sources = arrived.shape[0]
-    rows = arrived.reshape(sources * capacity, model_width)
-    gate_part = jnp.dot(rows, expert_in[0, :, 0:half_units], preferred_element_type=jnp.float32)
-    up_part = jnp.dot(rows, expert_in[1, :, 0:half_units], preferred_element_type=jnp.float32)
+    rows = arrived.reshape(sources * capacity, folds, lanes)
+    w_in = expert_in[:, :, 0:half_units].reshape(2, folds, lanes, half_units)
+    gate_part = jnp.einsum("tkd,kdf->tf", rows, w_in[0], preferred_element_type=jnp.float32)
+    up_part = jnp.einsum("tkd,kdf->tf", rows, w_in[1], preferred_element_type=jnp.float32)
     inner = (jax.nn.silu(gate_part) * up_part).astype(jnp.bfloat16)
-    half_out = jnp.dot(inner, expert_down, preferred_element_type=jnp.float32).astype(jnp.bfloat16)
+    w_down = expert_down.reshape(half_units, folds, lanes)
+    half_out = jnp.einsum(
+        "tf,fkd->tkd", inner, w_down, preferred_element_type=jnp.float32
+    ).astype(jnp.bfloat16)
     back = half_out.reshape(sources, capacity * folds, lanes)
     returned = lax.all_to_all(back, ("req", "z", "x"), 0, 0, tiled=True)
     halves = returned.reshape(EXPERTS, 2, capacity, folds, lanes)

time: 272 us -> 271 us (level)
  blocking collectives: 74.1 us -> 0 us
  waiting for transfers between devices: 69.9 us -> 126 us
  starting transfers between devices: 22 us -> 34.3 us
  local copies, waits for them, and re-layouts: 44.6 us -> 49.7 us
    all_to_all x1 -> x0, blocking collectives: 74.1 us -> none  [layer(): arrived = lax.all_to_all(outgoing, ('req', 'z', 'x'), 0, 0, tiled=True)]
    all_to_all x0 -> x1, waiting for transfers between devices: none -> 56.5 us  [layer(): arrived = lax.all_to_all(outgoing, ('req', 'z', 'x'), 0, 0, tiled=True)]
    reshape x2 -> x0, local copies, waits for them, and re-layouts: 17.8 us -> none  [the longest x1 8.93 us: layer(): back = half_out.reshape(sources, capacity * folds, lanes)]
    convert_element_type x0 -> x1, local copies, waits for them, and re-layouts: none -> 16 us  [layer(): half_out = jnp.einsum('tf,fkd->tkd', inner, w_down, preferred_element_typ...]
    all_to_all x0 -> x1, starting transfers between devices: none -> 13.5 us  [layer(): arrived = lax.all_to_all(outgoing, ('req', 'z', 'x'), 0, 0, tiled=True)]
    slice x1 -> x2, local copies, waits for them, and re-layouts: 0.23 us -> 4.68 us  [the longest x1 4.45 us: layer(): w_in[0]]
  transfers between devices with their start and end apart: 6 -> 7, of which waited for: 3 -> 4; matrix products, arithmetic and copies ran while one was open for 15% -> 16% of each run, Pallas kernels for 0% -> 0%
where the time goes in v8:
time: 271 us; the launch traced here: 267 us
  waiting for transfers between devices  126 us (46%)
  local copies, waits for them, and re-layouts  49.7 us (18%)
  matrix products  38.8 us (14%)
  starting transfers between devices  34.3 us (13%)
  other arithmetic  17.1 us (6%)
    all_to_all x1, waiting for transfers between devices, layer(): returned = lax.all_to_all(back, ('req', 'z', 'x'), 0, 0, tiled=True)  60.9 us
    all_to_all x1, waiting for transfers between devices, layer(): arrived = lax.all_to_all(outgoing, ('req', 'z', 'x'), 0, 0, tiled=True)  56.5 us
    convert_element_type x1, local copies, waits for them, and re-layouts, layer(): half_out = jnp.einsum('tf,fkd->tkd', inner, w_down, preferred_element_typ...  16 us
    all_to_all x1, starting transfers between devices, layer(): arrived = lax.all_to_all(outgoing, ('req', 'z', 'x'), 0, 0, tiled=True)  13.5 us
    dot_general x2, matrix products, attend_request(): jnp.einsum('htj,jhd->thd', weights_bf, all_vals, preferred_element_type=j...  11.7 us
    dot_general x1, matrix products, layer(): jnp.einsum('tf,fkd->tkd', inner, w_down, preferred_element_type=jnp.float32)  10.3 us
    all_to_all x1, waiting for transfers between devices, layer(): partial = lax.all_to_all(partial, 'z', 0, 0, tiled=True)  8.09 us
    all_to_all x1, starting transfers between devices, layer(): returned = lax.all_to_all(back, ('req', 'z', 'x'), 0, 0, tiled=True)  7.33 us
  transfers between devices with their start and end apart: 7, of which 4 were waited for; matrix products, arithmetic and copies ran while one was open for 16% of the time, Pallas kernels for 0%

profile of v8, /device:TPU:37, one launch (start us, length us, event | category | flops | bytes accessed | tf_op | source)
XLA Modules:
  0.0 267.5 jit_solution(19766117732427773)
XLA Ops:
  3.0 34.1 %while.10 = (s32[]{:T(128)}, bf16[2,512,128]{2,1,0:T(8,128)(2,1)}, bf16[2,2,4096,128]{3,2,1,0:T(8,128)(2,1)}, bf16[2,2,512,128]{3,2,1,0:T(8,128)(2,1)}, s32[2]{0...) while((s32[]{:T(128)}, bf16[2,512,128]{2,1,0:T(8,128)(2,1)}, ...), condition=%wide.region_4.5_spmd, body=%wide.region_0.4_spmd.sunk | while | flops 1231948800 | bytes 70676728 | solution.py:69
  5.1 2.8 %fusion.82 = (f32[512]{0:T(512)S(1)}, f32[512,4096]{1,0:T(8,128)S(1)}) fusion(bf16[2,2,4096,128]{3,2,1,0:T(8,128)(2,1)} %get-tuple-element.120, s32[]{:T(128)} %get-tuple-element.109, bf16[2,512,128]{2,1,0:T(8,128)(2,1)} %get-tuple-element.123, pred[4096]{0:T(1024)(128)(4,1)S(1)} %iota_compare_fusion.5), kind=kOutput, calls=%fused_computation.94.clone.1 | convolution fusion | flops 543161856 | bytes 9575424 | tf_op jit(solution)/shard_map/while/body/eval_jaxpr/thd,jhd->htj/dot_general | solution.py:41
  13.3 5.9 %fusion.84 = bf16[1,512,128]{1,2,0:T(8,128)(2,1)S(1)} fusion(f32[1,512,1,1,1,1,512]{6,1,5,4,3,2,0:T(8,128)S(1)} %bitcast.172, f32[1,512,1,1,1,1,4096]{6,1,5,4,3,2,0:T(8,128)} %bitcast.170, f32[512]{0:T(512)S(1)} %reduce_max.27, bf16[512,1,128]{2,0,1:T(8,128)(2,1)S(1)} %dynamic-slice_bitcast_fusion.8, ...), kind=kOutput, calls=%fused_computation.21.clone.1 | convolution fusion | flops 613548032 | bytes 10752000 | tf_op jit(solution)/shard_map/while/body/eval_jaxpr/htj,jhd->thd/dot_general | solution.py:65
  22.1 2.8 %fusion.82 = (f32[512]{0:T(512)S(1)}, f32[512,4096]{1,0:T(8,128)S(1)}) fusion(bf16[2,2,4096,128]{3,2,1,0:T(8,128)(2,1)} %get-tuple-element.120, s32[]{:T(128)} %get-tuple-element.109, bf16[2,512,128]{2,1,0:T(8,128)(2,1)} %get-tuple-element.123, pred[4096]{0:T(1024)(128)(4,1)S(1)} %iota_compare_fusion.5), kind=kOutput, calls=%fused_computation.94.clone.1 | convolution fusion | flops 543161856 | bytes 9575424 | tf_op jit(solution)/shard_map/while/body/eval_jaxpr/thd,jhd->htj/dot_general | solution.py:41
  30.4 5.9 %fusion.84 = bf16[1,512,128]{1,2,0:T(8,128)(2,1)S(1)} fusion(f32[1,512,1,1,1,1,512]{6,1,5,4,3,2,0:T(8,128)S(1)} %bitcast.172, f32[1,512,1,1,1,1,4096]{6,1,5,4,3,2,0:T(8,128)} %bitcast.170, f32[512]{0:T(512)S(1)} %reduce_max.27, bf16[512,1,128]{2,0,1:T(8,128)(2,1)S(1)} %dynamic-slice_bitcast_fusion.8, ...), kind=kOutput, calls=%fused_computation.21.clone.1 | convolution fusion | flops 613548032 | bytes 10752000 | tf_op jit(solution)/shard_map/while/body/eval_jaxpr/htj,jhd->thd/dot_general | solution.py:65
  37.1 1.7 copy.29
  38.8 6.1 %all-to-all-start = ((bf16[4,4,64,128]{3,2,1,0:T(8,128)(2,1)}), bf16[4,4,64,128]{3,2,1,0:T(8,128)(2,1)S(1)}, u32[]{:S(2)}, u32[]{:S(2)}) async-start(bf16[4,4,64,128]{3,2,1,0:T(8,128)(2,1)} %copy.29), calls=%async_computation | async-start | bytes 524288 | tf_op jit(solution)/shard_map/all_to_all | solution.py:83
  50.3 1.7 convolution_convert_fusion.1
  52.0 5.0 %all-to-all-start.1 = ((bf16[4,64,2048]{2,1,0:T(8,128)(2,1)}), bf16[4,64,2048]{2,1,0:T(8,128)(2,1)S(1)}, u32[]{:S(2)}, u32[]{:S(2)}) async-start(bf16[4,64,2048]{2,1,0:T(8,128)(2,1)} %bitcast.178), calls=%async_computation.1 | async-start | bytes 2097152 | tf_op jit(solution)/shard_map/all_to_all | solution.py:91
  57.2 2.4 scatter_custom_fusion
  59.7 8.1 %all-to-all-done.1 = bf16[4,64,2048]{2,1,0:T(8,128)(2,1)S(1)} async-done(((bf16[4,64,2048]{2,1,0:T(8,128)(2,1)}), bf16[4,64,2048]{2,1,0:T(8,128)(2,1)S(1)}, u32[]{:S(2)}, u32[]{:S(2)}) %all-to-all-start.1) | async-done | bytes 1048608 | tf_op jit(solution)/shard_map/all_to_all | solution.py:91
  69.0 3.3 %gather_fusion.1 = bf16[640,16,128]{2,1,0:T(8,128)(2,1)} fusion(bf16[65,16,128]{2,1,0:T(8,128)(2,1)S(1)} %concatenate.42, s32[1024]{0:T(1024)S(1)} %pad_clamp_fusion.1), kind=kCustom, calls=%fused_computation.1 | custom fusion | bytes 5245440 | tf_op jit(solution)/shard_map/gather | solution.py:114
  72.3 5.0 %broadcast_in_dim.52 = bf16[64,2,160,128]{3,2,1,0:T(8,128)(2,1)} broadcast(bf16[64,160,128]{2,1,0:T(8,128)(2,1)} %bitcast.176), dimensions={0,2,3} | broadcast | bytes 7864320 | tf_op jit(solution)/shard_map/broadcast_in_dim | solution.py:115
  77.3 13.5 %all-to-all-start.2 = ((bf16[128,160,128]{2,1,0:T(8,128)(2,1)}), bf16[128,160,128]{2,1,0:T(8,128)(2,1)}, u32[]{:S(2)}, u32[]{:S(2)}) async-start(bf16[128,160,128]{2,1,0:T(8,128)(2,1)} %bitcast.173), calls=%async_computation.2 | async-start | bytes 10485760 | tf_op jit(solution)/shard_map/all_to_all | solution.py:117
  90.8 4.5 %fusion.70 = (bf16[1,2048,512]{2,1,0:T(8,128)(2,1)}, bf16[1,2048,512]{2,1,0:T(8,128)(2,1)}) fusion(bf16[2,2048,512]{2,1,0:T(8,128)(2,1)} %param.22), kind=kLoop, calls=%fused_computation.96 | loop fusion | bytes 8388608 | tf_op jit(solution)/shard_map/slice | solution.py:121
  95.2 56.5 %all-to-all-done.2 = bf16[128,160,128]{2,1,0:T(8,128)(2,1)} async-done(((bf16[128,160,128]{2,1,0:T(8,128)(2,1)}), bf16[128,160,128]{2,1,0:T(8,128)(2,1)}, u32[]{:S(2)}, u32[]{:S(2)}) %all-to-all-start.2) | async-done | bytes 5242912 | tf_op jit(solution)/shard_map/all_to_all | solution.py:117
  151.8 6.5 %fusion.34 = f32[1280,512]{1,0:T(8,128)} fusion(bf16[16,128,512]{2,1,0:T(8,128)(2,1)} %bitcast.180, bf16[1280,16,128]{2,1,0:T(8,128)(2,1)} %bitcast.30), kind=kOutput, calls=%fused_computation.44 | convolution fusion | flops 2684354560 | bytes 9961472 | tf_op jit(solution)/shard_map/tkd,kdf->tf/dot_general | solution.py:121
  158.3 10.3 %convolution_convert_fusion = bf16[1280,16,128]{2,0,1:T(8,128)(2,1)} fusion(bf16[16,128,512]{2,1,0:T(8,128)(2,1)} %bitcast.179, bf16[1280,16,128]{2,1,0:T(8,128)(2,1)} %bitcast.30, f32[1280,512]{1,0:T(8,128)} %fusion.34, bf16[512,2048]{1,0:T(8,128)(2,1)S(1)} %copy-done), kind=kOutput, calls=%fused_computation.37 | convolution fusion | flops 5375262720 | bytes 17301504 | tf_op jit(solution)/shard_map/tf,fkd->tkd/dot_general | solution.py:125
  168.7 16.0 %copy.38 = bf16[1280,16,128]{2,1,0:T(8,128)(2,1)} copy(bf16[1280,16,128]{2,0,1:T(8,128)(2,1)} %convolution_convert_fusion) | data formatting | bytes 10485760 | tf_op jit(solution)/shard_map/convert_element_type | solution.py:127
  184.7 7.3 %all-to-all-start.3 = ((bf16[128,160,128]{2,1,0:T(8,128)(2,1)}), bf16[128,160,128]{2,1,0:T(8,128)(2,1)}, u32[]{:S(2)}, u32[]{:S(2)}) async-start(bf16[128,160,128]{2,1,0:T(8,128)(2,1)} %bitcast.174), calls=%async_computation.3 | async-start | bytes 10485760 | tf_op jit(solution)/shard_map/all_to_all | solution.py:129
  192.1 60.9 %all-to-all-done.3 = bf16[128,160,128]{2,1,0:T(8,128)(2,1)} async-done(((bf16[128,160,128]{2,1,0:T(8,128)(2,1)}), bf16[128,160,128]{2,1,0:T(8,128)(2,1)}, u32[]{:S(2)}, u32[]{:S(2)}) %all-to-all-start.3) | async-done | bytes 5242912 | tf_op jit(solution)/shard_map/all_to_all | solution.py:129
  253.0 5.6 %convert_add_fusion = f32[64,1,10,16,128]{4,3,2,1,0:T(8,128)} fusion(bf16[64,2,10,16,128]{4,3,2,1,0:T(8,128)(2,1)} %bitcast.37), kind=kLoop, calls=%fused_computation.38 | loop fusion | flops 3932160 | bytes 10485760 | tf_op jit(solution)/shard_map/add | solution.py:131
  258.7 5.4 %gather_fusion.2 = f32[512,16,128]{2,1,0:T(8,128)} fusion(f32[640,16,128]{2,1,0:T(8,128)} %bitcast.175, s32[1024]{0:T(1024)S(1)} %pad_clamp_fusion), kind=kCustom, calls=%fused_computation.2 | custom fusion | bytes 8390656 | tf_op jit(solution)/shard_map/gather | solution.py:134
  264.1 2.6 multiply_reduce_fusion
  (85 shorter events, 26.4 us)
Async XLA Ops:
  0.6 157.7 %copy-start = (bf16[512,2048]{1,0:T(8,128)(2,1)S(1)}, bf16[512,2048]{1,0:T(8,128)(2,1)}, u32[]{:S(2)}) copy-start(bf16[512,2048]{1,0:T(8,128)(2,1)} %param.23) | copy-start | bytes 6291460
  0.6 48.0 %collective-permute-start = (bf16[128,2048]{1,0:T(8,128)(2,1)}, bf16[128,2048]{1,0:T(8,128)(2,1)}, u32[]{:S(2)}, u32[]{:S(2)}) collective-permute-start(bf16[128,2048]{1,0:T(8,128)(2,1)} %param.17), channel_id=1, source_target_pairs={{0,1},{1,2},{2,3},{3,0},{4,5},{5,6},{6,7},{7,4},{8,9},{9,10},{10,1... | collective-permute-start | bytes 1572872 | tf_op jit(solution)/shard_map/ppermute | solution.py:78
  1.6 47.0 %collective-permute-start.1 = (bf16[128,2048]{1,0:T(8,128)(2,1)}, bf16[128,2048]{1,0:T(8,128)(2,1)}, u32[]{:S(2)}, u32[]{:S(2)}) collective-permute-start(bf16[128,2048]{1,0:T(8,128)(2,1)} %param.17), channel_id=1, source_target_pairs={{0,2},{1,3},{2,0},{3,1},{4,6},{5,7},{6,4},{7,5},{8,10},{9,11},{10,... | collective-permute-start | bytes 1572872 | tf_op jit(solution)/shard_map/ppermute | solution.py:78
  2.2 46.5 %collective-permute-start.2 = (bf16[128,2048]{1,0:T(8,128)(2,1)}, bf16[128,2048]{1,0:T(8,128)(2,1)}, u32[]{:S(2)}, u32[]{:S(2)}) collective-permute-start(bf16[128,2048]{1,0:T(8,128)(2,1)} %param.17), channel_id=1, source_target_pairs={{0,3},{1,0},{2,1},{3,2},{4,7},{5,4},{6,5},{7,6},{8,11},{9,8},{10,9... | collective-permute-start | bytes 1572872 | tf_op jit(solution)/shard_map/ppermute | solution.py:78
  3.0 41.9 %copy-start.7 = (s32[64,8]{0,1:T(8,128)S(1)}, s32[64,8]{0,1:T(8,128)}, u32[]{:S(2)}) copy-start(s32[64,8]{0,1:T(8,128)} %param.20) | copy-start | bytes 6148
  5.0 2.8 %copy-start.2 = (bf16[2,512,128]{2,1,0:T(8,128)(2,1)S(1)}, bf16[2,512,128]{2,1,0:T(8,128)(2,1)}, u32[]{:S(2)}) copy-start(bf16[2,512,128]{2,1,0:T(8,128)(2,1)} %get-tuple-element.123) | copy-start | bytes 786436 | tf_op jit(solution)/shard_map/while
  7.9 3.2 %copy-start.1 = (f32[512,4096]{1,0:T(8,128)}, f32[512,4096]{1,0:T(8,128)S(1)}, u32[]{:S(2)}) copy-start(f32[512,4096]{1,0:T(8,128)S(1)} %get-tuple-element.97) | copy-start | bytes 25165828 | tf_op jit(solution)/shard_map/while
  13.3 6.0 %copy-start.5 = (bf16[2,512,128]{2,1,0:T(8,128)(2,1)S(1)}, bf16[2,512,128]{2,1,0:T(8,128)(2,1)}, u32[]{:S(2)}) copy-start(bf16[2,512,128]{2,1,0:T(8,128)(2,1)} %get-tuple-element.110) | copy-start | bytes 786436 | tf_op jit(solution)/shard_map/while
  19.4 0.7 copy-start.6
  22.1 2.8 %copy-start.2 = (bf16[2,512,128]{2,1,0:T(8,128)(2,1)S(1)}, bf16[2,512,128]{2,1,0:T(8,128)(2,1)}, u32[]{:S(2)}) copy-start(bf16[2,512,128]{2,1,0:T(8,128)(2,1)} %get-tuple-element.123) | copy-start | bytes 786436 | tf_op jit(solution)/shard_map/while
  24.9 3.2 %copy-start.1 = (f32[512,4096]{1,0:T(8,128)}, f32[512,4096]{1,0:T(8,128)S(1)}, u32[]{:S(2)}) copy-start(f32[512,4096]{1,0:T(8,128)S(1)} %get-tuple-element.97) | copy-start | bytes 25165828 | tf_op jit(solution)/shard_map/while
  30.4 6.0 %copy-start.5 = (bf16[2,512,128]{2,1,0:T(8,128)(2,1)S(1)}, bf16[2,512,128]{2,1,0:T(8,128)(2,1)}, u32[]{:S(2)}) copy-start(bf16[2,512,128]{2,1,0:T(8,128)(2,1)} %get-tuple-element.110) | copy-start | bytes 786436 | tf_op jit(solution)/shard_map/while
  36.4 0.7 copy-start.6
  37.1 11.5 %copy-start.4 = (bf16[128,2048]{1,0:T(8,128)(2,1)S(1)}, bf16[128,2048]{1,0:T(8,128)(2,1)}, u32[]{:S(2)}) copy-start(bf16[128,2048]{1,0:T(8,128)(2,1)} %param.17) | copy-start | bytes 1572868
  38.8 9.0 %all-to-all-start = ((bf16[4,4,64,128]{3,2,1,0:T(8,128)(2,1)}), bf16[4,4,64,128]{3,2,1,0:T(8,128)(2,1)S(1)}, u32[]{:S(2)}, u32[]{:S(2)}) async-start(bf16[4,4,64,128]{3,2,1,0:T(8,128)(2,1)} %copy.29), calls=%async_computation | async-start | bytes 524288 | tf_op jit(solution)/shard_map/all_to_all | solution.py:83
  52.0 15.9 %copy-start.3 = (bf16[64,2048]{1,0:T(8,128)(2,1)S(1)}, bf16[64,2048]{1,0:T(8,128)(2,1)}, u32[]{:S(2)}) copy-start(bf16[64,2048]{1,0:T(8,128)(2,1)} %param.18) | copy-start | bytes 786436
  52.0 16.1 %copy-start.8 = (f32[2048]{0:T(1024)S(1)}, f32[2048]{0:T(1024)}, u32[]{:S(2)}) copy-start(f32[2048]{0:T(1024)} %param.19) | copy-start | bytes 24580
  52.0 15.8 %all-to-all-start.1 = ((bf16[4,64,2048]{2,1,0:T(8,128)(2,1)}), bf16[4,64,2048]{2,1,0:T(8,128)(2,1)S(1)}, u32[]{:S(2)}, u32[]{:S(2)}) async-start(bf16[4,64,2048]{2,1,0:T(8,128)(2,1)} %bitcast.178), calls=%async_computation.1 | async-start | bytes 2097152 | tf_op jit(solution)/shard_map/all_to_all | solution.py:91
  77.3 74.5 %all-to-all-start.2 = ((bf16[128,160,128]{2,1,0:T(8,128)(2,1)}), bf16[128,160,128]{2,1,0:T(8,128)(2,1)}, u32[]{:S(2)}, u32[]{:S(2)}) async-start(bf16[128,160,128]{2,1,0:T(8,128)(2,1)} %bitcast.173), calls=%async_computation.2 | async-start | bytes 10485760 | tf_op jit(solution)/shard_map/all_to_all | solution.py:117
  184.7 7.3 %copy-start.9 = (f32[64,8]{0,1:T(8,128)S(1)}, f32[64,8]{0,1:T(8,128)}, u32[]{:S(2)}) copy-start(f32[64,8]{0,1:T(8,128)} %param.21) | copy-start | bytes 6148
  184.7 68.4 %all-to-all-start.3 = ((bf16[128,160,128]{2,1,0:T(8,128)(2,1)}), bf16[128,160,128]{2,1,0:T(8,128)(2,1)}, u32[]{:S(2)}, u32[]{:S(2)}) async-start(bf16[128,160,128]{2,1,0:T(8,128)(2,1)} %bitcast.174), calls=%async_computation.3 | async-start | bytes 10485760 | tf_op jit(solution)/shard_map/all_to_all | solution.py:129

commit v9 on v8

--- a/solution.py
+++ b/solution.py
@@ -121,19 +121,22 @@
     gate_part = jnp.einsum("tkd,kdf->tf", rows, w_in[0], preferred_element_type=jnp.float32)
     up_part = jnp.einsum("tkd,kdf->tf", rows, w_in[1], preferred_element_type=jnp.float32)
     inner = (jax.nn.silu(gate_part) * up_part).astype(jnp.bfloat16)
-    w_down = expert_down.reshape(half_units, folds, lanes)
-    half_out = jnp.einsum(
-        "tf,fkd->tkd", inner, w_down, preferred_element_type=jnp.float32
-    ).astype(jnp.bfloat16)
+    half_out = jnp.dot(inner, expert_down, preferred_element_type=jnp.float32).astype(jnp.bfloat16)
     back = half_out.reshape(sources, capacity * folds, lanes)
     returned = lax.all_to_all(back, ("req", "z", "x"), 0, 0, tiled=True)
     halves = returned.reshape(EXPERTS, 2, capacity, folds, lanes)
     summed = (halves[:, 0].astype(jnp.float32) + halves[:, 1].astype(jnp.float32)).reshape(
-        EXPERTS * capacity, folds, lanes
+        EXPERTS * capacity, folds * lanes
     )
-    picked = summed[positions] * gate_weights.reshape(-1)[:, None, None]
-    expert_out = jnp.sum(picked.reshape(tok_local, TOP, folds, lanes), axis=1)
-    expert_out = expert_out.astype(jnp.bfloat16).reshape(tok_local, model_width)
+    slot_ids = jnp.arange(EXPERTS * capacity, dtype=jnp.int32)
+    route_slots = positions.reshape(tok_local, TOP)
+    mixing = jnp.sum(
+        jnp.where(route_slots[:, :, None] == slot_ids[None, None, :], gate_weights[:, :, None], 0.0),
+        axis=1,
+    )
+    expert_out = jnp.dot(
+        mixing, summed, precision=lax.Precision.HIGHEST, preferred_element_type=jnp.float32
+    ).astype(jnp.bfloat16)
     return (attended, expert_out)
 
 

time: 271 us -> 258 us (0.952)
  local copies, waits for them, and re-layouts: 49.7 us -> 36.5 us
  matrix products: 38.8 us -> 44.2 us
  other arithmetic: 17.1 us -> 12.6 us
    convert_element_type x1 -> x0, local copies, waits for them, and re-layouts: 16 us -> none  [layer(): half_out = jnp.einsum('tf,fkd->tkd', inner, w_down, preferred_element_typ...]
    reshape x0 -> x1, local copies, waits for them, and re-layouts: none -> 8.93 us  [layer(): back = half_out.reshape(sources, capacity * folds, lanes)]
    dot_general x1 -> x2, matrix products: 10.3 us -> 15.7 us  [the longest x1 10.3 us: layer(): jnp.dot(inner, expert_down, preferred_element_type=jnp.float32)]
    gather x1 -> x0, local copies, waits for them, and re-layouts: 5.38 us -> none  [layer(): picked = summed[positions] * gate_weights.reshape(-1)[:, None, None]]
  transfers between devices with their start and end apart: 7 -> 7, of which waited for: 4 -> 4; matrix products, arithmetic and copies ran while one was open for 16% -> 17% of each run, Pallas kernels for 0% -> 0%
where the time goes in v9:
time: 258 us; the launch traced here: 255 us
  waiting for transfers between devices  126 us (49%)
  matrix products  44.2 us (17%)
  local copies, waits for them, and re-layouts  36.5 us (14%)
  starting transfers between devices  34.3 us (13%)
  other arithmetic  12.6 us (5%)
    all_to_all x1, waiting for transfers between devices, layer(): returned = lax.all_to_all(back, ('req', 'z', 'x'), 0, 0, tiled=True)  60.4 us
    all_to_all x1, waiting for transfers between devices, layer(): arrived = lax.all_to_all(outgoing, ('req', 'z', 'x'), 0, 0, tiled=True)  56.5 us
    all_to_all x1, starting transfers between devices, layer(): arrived = lax.all_to_all(outgoing, ('req', 'z', 'x'), 0, 0, tiled=True)  13.5 us
    dot_general x2, matrix products, attend_request(): jnp.einsum('htj,jhd->thd', weights_bf, all_vals, preferred_element_type=j...  11.7 us
    dot_general x1, matrix products, layer(): jnp.dot(inner, expert_down, preferred_element_type=jnp.float32)  10.3 us
    reshape x1, local copies, waits for them, and re-layouts, layer(): back = half_out.reshape(sources, capacity * folds, lanes)  8.93 us
    all_to_all x1, waiting for transfers between devices, layer(): partial = lax.all_to_all(partial, 'z', 0, 0, tiled=True)  8.17 us
    all_to_all x1, starting transfers between devices, layer(): returned = lax.all_to_all(back, ('req', 'z', 'x'), 0, 0, tiled=True)  7.34 us
  transfers between devices with their start and end apart: 7, of which 4 were waited for; matrix products, arithmetic and copies ran while one was open for 17% of the time, Pallas kernels for 0%

profile of v9, /device:TPU:37, one launch (start us, length us, event | category | flops | bytes accessed | tf_op | source)
XLA Modules:
  0.0 254.6 jit_solution(10767564185306599188)
XLA Ops:
  3.0 34.1 %while.10 = (s32[]{:T(128)}, bf16[2,512,128]{2,1,0:T(8,128)(2,1)}, bf16[2,2,4096,128]{3,2,1,0:T(8,128)(2,1)}, bf16[2,2,512,128]{3,2,1,0:T(8,128)(2,1)}, s32[2]{0...) while((s32[]{:T(128)}, bf16[2,512,128]{2,1,0:T(8,128)(2,1)}, ...), condition=%wide.region_4.5_spmd, body=%wide.region_0.4_spmd.sunk | while | flops 1231948800 | bytes 70676728 | solution.py:69
  5.1 2.8 %fusion.85 = (f32[512]{0:T(512)S(1)}, f32[512,4096]{1,0:T(8,128)S(1)}) fusion(bf16[2,2,4096,128]{3,2,1,0:T(8,128)(2,1)} %get-tuple-element.122, s32[]{:T(128)} %get-tuple-element.111, bf16[2,512,128]{2,1,0:T(8,128)(2,1)} %get-tuple-element.125, pred[4096]{0:T(1024)(128)(4,1)S(1)} %iota_compare_fusion.6), kind=kOutput, calls=%fused_computation.94.clone.1 | convolution fusion | flops 543161856 | bytes 9575424 | tf_op jit(solution)/shard_map/while/body/eval_jaxpr/thd,jhd->htj/dot_general | solution.py:41
  9.4 1.7 fusion.86
  13.3 5.9 %fusion.87 = bf16[1,512,128]{1,2,0:T(8,128)(2,1)S(1)} fusion(f32[1,512,1,1,1,1,512]{6,1,5,4,3,2,0:T(8,128)S(1)} %bitcast.160, f32[1,512,1,1,1,1,4096]{6,1,5,4,3,2,0:T(8,128)} %bitcast.158, f32[512]{0:T(512)S(1)} %reduce_max.27, bf16[512,1,128]{2,0,1:T(8,128)(2,1)S(1)} %dynamic-slice_bitcast_fusion.8, ...), kind=kOutput, calls=%fused_computation.20.clone.1 | convolution fusion | flops 613548032 | bytes 10752000 | tf_op jit(solution)/shard_map/while/body/eval_jaxpr/htj,jhd->thd/dot_general | solution.py:65
  22.1 2.8 %fusion.85 = (f32[512]{0:T(512)S(1)}, f32[512,4096]{1,0:T(8,128)S(1)}) fusion(bf16[2,2,4096,128]{3,2,1,0:T(8,128)(2,1)} %get-tuple-element.122, s32[]{:T(128)} %get-tuple-element.111, bf16[2,512,128]{2,1,0:T(8,128)(2,1)} %get-tuple-element.125, pred[4096]{0:T(1024)(128)(4,1)S(1)} %iota_compare_fusion.6), kind=kOutput, calls=%fused_computation.94.clone.1 | convolution fusion | flops 543161856 | bytes 9575424 | tf_op jit(solution)/shard_map/while/body/eval_jaxpr/thd,jhd->htj/dot_general | solution.py:41
  30.4 5.9 %fusion.87 = bf16[1,512,128]{1,2,0:T(8,128)(2,1)S(1)} fusion(f32[1,512,1,1,1,1,512]{6,1,5,4,3,2,0:T(8,128)S(1)} %bitcast.160, f32[1,512,1,1,1,1,4096]{6,1,5,4,3,2,0:T(8,128)} %bitcast.158, f32[512]{0:T(512)S(1)} %reduce_max.27, bf16[512,1,128]{2,0,1:T(8,128)(2,1)S(1)} %dynamic-slice_bitcast_fusion.8, ...), kind=kOutput, calls=%fused_computation.20.clone.1 | convolution fusion | flops 613548032 | bytes 10752000 | tf_op jit(solution)/shard_map/while/body/eval_jaxpr/htj,jhd->thd/dot_general | solution.py:65
  37.1 1.7 copy.38
  38.8 6.1 %all-to-all-start = ((bf16[4,4,64,128]{3,2,1,0:T(8,128)(2,1)}), bf16[4,4,64,128]{3,2,1,0:T(8,128)(2,1)S(1)}, u32[]{:S(2)}, u32[]{:S(2)}) async-start(bf16[4,4,64,128]{3,2,1,0:T(8,128)(2,1)} %copy.38), calls=%async_computation | async-start | bytes 524288 | tf_op jit(solution)/shard_map/all_to_all | solution.py:83
  50.3 1.7 convolution_convert_fusion.1
  52.0 5.0 %all-to-all-start.1 = ((bf16[4,64,2048]{2,1,0:T(8,128)(2,1)}), bf16[4,64,2048]{2,1,0:T(8,128)(2,1)S(1)}, u32[]{:S(2)}, u32[]{:S(2)}) async-start(bf16[4,64,2048]{2,1,0:T(8,128)(2,1)} %bitcast.165), calls=%async_computation.1 | async-start | bytes 2097152 | tf_op jit(solution)/shard_map/all_to_all | solution.py:91
  57.1 2.4 scatter_custom_fusion
  59.6 8.2 %all-to-all-done.1 = bf16[4,64,2048]{2,1,0:T(8,128)(2,1)S(1)} async-done(((bf16[4,64,2048]{2,1,0:T(8,128)(2,1)}), bf16[4,64,2048]{2,1,0:T(8,128)(2,1)S(1)}, u32[]{:S(2)}, u32[]{:S(2)}) %all-to-all-start.1) | async-done | bytes 1048608 | tf_op jit(solution)/shard_map/all_to_all | solution.py:91
  69.0 3.3 %gather_fusion.1 = bf16[640,16,128]{2,1,0:T(8,128)(2,1)} fusion(bf16[65,16,128]{2,1,0:T(8,128)(2,1)S(1)} %concatenate.42, s32[1024]{0:T(1024)S(1)} %pad_clamp_fusion), kind=kCustom, calls=%fused_computation.1 | custom fusion | bytes 5245440 | tf_op jit(solution)/shard_map/gather | solution.py:114
  72.3 5.0 %broadcast_in_dim.67 = bf16[64,2,160,128]{3,2,1,0:T(8,128)(2,1)} broadcast(bf16[64,160,128]{2,1,0:T(8,128)(2,1)} %bitcast.163), dimensions={0,2,3} | broadcast | bytes 7864320 | tf_op jit(solution)/shard_map/broadcast_in_dim | solution.py:115
  77.3 13.5 %all-to-all-start.2 = ((bf16[128,160,128]{2,1,0:T(8,128)(2,1)}), bf16[128,160,128]{2,1,0:T(8,128)(2,1)}, u32[]{:S(2)}, u32[]{:S(2)}) async-start(bf16[128,160,128]{2,1,0:T(8,128)(2,1)} %bitcast.161), calls=%async_computation.2 | async-start | bytes 10485760 | tf_op jit(solution)/shard_map/all_to_all | solution.py:117
  90.8 4.5 %fusion.72 = (bf16[1,2048,512]{2,1,0:T(8,128)(2,1)}, bf16[1,2048,512]{2,1,0:T(8,128)(2,1)}) fusion(bf16[2,2048,512]{2,1,0:T(8,128)(2,1)} %param.22), kind=kLoop, calls=%fused_computation.96 | loop fusion | bytes 8388608 | tf_op jit(solution)/shard_map/slice | solution.py:121
  95.2 56.5 %all-to-all-done.2 = bf16[128,160,128]{2,1,0:T(8,128)(2,1)} async-done(((bf16[128,160,128]{2,1,0:T(8,128)(2,1)}), bf16[128,160,128]{2,1,0:T(8,128)(2,1)}, u32[]{:S(2)}, u32[]{:S(2)}) %all-to-all-start.2) | async-done | bytes 5242912 | tf_op jit(solution)/shard_map/all_to_all | solution.py:117
  151.8 6.5 %fusion.37 = f32[1280,512]{1,0:T(8,128)} fusion(bf16[16,128,512]{2,1,0:T(8,128)(2,1)} %bitcast.167, bf16[1280,16,128]{2,1,0:T(8,128)(2,1)} %bitcast.30), kind=kOutput, calls=%fused_computation.45 | convolution fusion | flops 2684354560 | bytes 9961472 | tf_op jit(solution)/shard_map/tkd,kdf->tf/dot_general | solution.py:121
  158.3 10.3 %convolution_convert_fusion = bf16[1280,2048]{1,0:T(8,128)(2,1)} fusion(bf16[512,2048]{1,0:T(8,128)(2,1)S(1)} %copy-done, bf16[16,128,512]{2,1,0:T(8,128)(2,1)} %bitcast.166, bf16[1280,16,128]{2,1,0:T(8,128)(2,1)} %bitcast.30, f32[1280,512]{1,0:T(8,128)} %fusion.37), kind=kOutput, calls=%fused_computation.36 | convolution fusion | flops 5375262720 | bytes 17301504 | tf_op jit(solution)/shard_map/dot_general | solution.py:124
  168.7 8.9 %reshape.378 = bf16[128,160,128]{2,1,0:T(8,128)(2,1)} reshape(bf16[1280,2048]{1,0:T(8,128)(2,1)} %convolution_convert_fusion) | data formatting | bytes 10485760 | tf_op jit(solution)/shard_map/reshape | solution.py:125
  177.6 7.3 %all-to-all-start.3 = ((bf16[128,160,128]{2,1,0:T(8,128)(2,1)}), bf16[128,160,128]{2,1,0:T(8,128)(2,1)}, u32[]{:S(2)}, u32[]{:S(2)}) async-start(bf16[128,160,128]{2,1,0:T(8,128)(2,1)} %reshape.378), calls=%async_computation.3 | async-start | bytes 10485760 | tf_op jit(solution)/shard_map/all_to_all | solution.py:126
  185.5 60.4 %all-to-all-done.3 = bf16[128,160,128]{2,1,0:T(8,128)(2,1)} async-done(((bf16[128,160,128]{2,1,0:T(8,128)(2,1)}), bf16[128,160,128]{2,1,0:T(8,128)(2,1)}, u32[]{:S(2)}, u32[]{:S(2)}) %all-to-all-start.3) | async-done | bytes 5242912 | tf_op jit(solution)/shard_map/all_to_all | solution.py:126
  246.0 3.3 %convert_add_fusion = f32[64,1,10,16,128]{4,3,2,1,0:T(8,128)S(1)} fusion(bf16[64,2,10,16,128]{4,3,2,1,0:T(8,128)(2,1)} %bitcast.35), kind=kLoop, calls=%fused_computation.40 | loop fusion | flops 3932160 | bytes 10485760 | tf_op jit(solution)/shard_map/add | solution.py:128
  249.3 5.4 %fusion.49 = bf16[64,2048]{1,0:T(8,128)(2,1)} fusion(f32[64,640]{1,0:T(8,128)S(1)} %select_reduce_fusion, f32[80,8,16,128]{3,2,1,0:T(8,128)S(1)} %bitcast.162), kind=kOutput, calls=%fused_computation.50 | convolution fusion | flops 1006764032 | bytes 5668864 | tf_op jit(solution)/shard_map/dot_general | solution.py:137
  (83 shorter events, 24.4 us)
Async XLA Ops:
  0.6 157.7 %copy-start = (bf16[512,2048]{1,0:T(8,128)(2,1)S(1)}, bf16[512,2048]{1,0:T(8,128)(2,1)}, u32[]{:S(2)}) copy-start(bf16[512,2048]{1,0:T(8,128)(2,1)} %param.23) | copy-start | bytes 6291460
  0.6 48.0 %collective-permute-start = (bf16[128,2048]{1,0:T(8,128)(2,1)}, bf16[128,2048]{1,0:T(8,128)(2,1)}, u32[]{:S(2)}, u32[]{:S(2)}) collective-permute-start(bf16[128,2048]{1,0:T(8,128)(2,1)} %param.17), channel_id=1, source_target_pairs={{0,1},{1,2},{2,3},{3,0},{4,5},{5,6},{6,7},{7,4},{8,9},{9,10},{10,1... | collective-permute-start | bytes 1572872 | tf_op jit(solution)/shard_map/ppermute | solution.py:78
  1.6 47.0 %collective-permute-start.1 = (bf16[128,2048]{1,0:T(8,128)(2,1)}, bf16[128,2048]{1,0:T(8,128)(2,1)}, u32[]{:S(2)}, u32[]{:S(2)}) collective-permute-start(bf16[128,2048]{1,0:T(8,128)(2,1)} %param.17), channel_id=1, source_target_pairs={{0,2},{1,3},{2,0},{3,1},{4,6},{5,7},{6,4},{7,5},{8,10},{9,11},{10,... | collective-permute-start | bytes 1572872 | tf_op jit(solution)/shard_map/ppermute | solution.py:78
  2.2 46.5 %collective-permute-start.2 = (bf16[128,2048]{1,0:T(8,128)(2,1)}, bf16[128,2048]{1,0:T(8,128)(2,1)}, u32[]{:S(2)}, u32[]{:S(2)}) collective-permute-start(bf16[128,2048]{1,0:T(8,128)(2,1)} %param.17), channel_id=1, source_target_pairs={{0,3},{1,0},{2,1},{3,2},{4,7},{5,4},{6,5},{7,6},{8,11},{9,8},{10,9... | collective-permute-start | bytes 1572872 | tf_op jit(solution)/shard_map/ppermute | solution.py:78
  3.0 41.9 %copy-start.8 = (s32[64,8]{0,1:T(8,128)S(1)}, s32[64,8]{0,1:T(8,128)}, u32[]{:S(2)}) copy-start(s32[64,8]{0,1:T(8,128)} %param.20) | copy-start | bytes 6148
  5.0 2.8 %copy-start.2 = (bf16[2,512,128]{2,1,0:T(8,128)(2,1)S(1)}, bf16[2,512,128]{2,1,0:T(8,128)(2,1)}, u32[]{:S(2)}) copy-start(bf16[2,512,128]{2,1,0:T(8,128)(2,1)} %get-tuple-element.125) | copy-start | bytes 786436 | tf_op jit(solution)/shard_map/while
  7.9 3.2 %copy-start.1 = (f32[512,4096]{1,0:T(8,128)}, f32[512,4096]{1,0:T(8,128)S(1)}, u32[]{:S(2)}) copy-start(f32[512,4096]{1,0:T(8,128)S(1)} %get-tuple-element.99) | copy-start | bytes 25165828 | tf_op jit(solution)/shard_map/while
  13.3 6.0 %copy-start.5 = (bf16[2,512,128]{2,1,0:T(8,128)(2,1)S(1)}, bf16[2,512,128]{2,1,0:T(8,128)(2,1)}, u32[]{:S(2)}) copy-start(bf16[2,512,128]{2,1,0:T(8,128)(2,1)} %get-tuple-element.112) | copy-start | bytes 786436 | tf_op jit(solution)/shard_map/while
  19.4 0.7 copy-start.6
  22.1 2.8 %copy-start.2 = (bf16[2,512,128]{2,1,0:T(8,128)(2,1)S(1)}, bf16[2,512,128]{2,1,0:T(8,128)(2,1)}, u32[]{:S(2)}) copy-start(bf16[2,512,128]{2,1,0:T(8,128)(2,1)} %get-tuple-element.125) | copy-start | bytes 786436 | tf_op jit(solution)/shard_map/while
  24.9 3.2 %copy-start.1 = (f32[512,4096]{1,0:T(8,128)}, f32[512,4096]{1,0:T(8,128)S(1)}, u32[]{:S(2)}) copy-start(f32[512,4096]{1,0:T(8,128)S(1)} %get-tuple-element.99) | copy-start | bytes 25165828 | tf_op jit(solution)/shard_map/while
  30.4 6.0 %copy-start.5 = (bf16[2,512,128]{2,1,0:T(8,128)(2,1)S(1)}, bf16[2,512,128]{2,1,0:T(8,128)(2,1)}, u32[]{:S(2)}) copy-start(bf16[2,512,128]{2,1,0:T(8,128)(2,1)} %get-tuple-element.112) | copy-start | bytes 786436 | tf_op jit(solution)/shard_map/while
  36.4 0.7 copy-start.6
  37.1 11.5 %copy-start.4 = (bf16[128,2048]{1,0:T(8,128)(2,1)S(1)}, bf16[128,2048]{1,0:T(8,128)(2,1)}, u32[]{:S(2)}) copy-start(bf16[128,2048]{1,0:T(8,128)(2,1)} %param.17) | copy-start | bytes 1572868
  38.8 9.0 %all-to-all-start = ((bf16[4,4,64,128]{3,2,1,0:T(8,128)(2,1)}), bf16[4,4,64,128]{3,2,1,0:T(8,128)(2,1)S(1)}, u32[]{:S(2)}, u32[]{:S(2)}) async-start(bf16[4,4,64,128]{3,2,1,0:T(8,128)(2,1)} %copy.38), calls=%async_computation | async-start | bytes 524288 | tf_op jit(solution)/shard_map/all_to_all | solution.py:83
  52.0 15.9 %copy-start.3 = (bf16[64,2048]{1,0:T(8,128)(2,1)S(1)}, bf16[64,2048]{1,0:T(8,128)(2,1)}, u32[]{:S(2)}) copy-start(bf16[64,2048]{1,0:T(8,128)(2,1)} %param.18) | copy-start | bytes 786436
  52.0 16.1 %copy-start.7 = (f32[2048]{0:T(1024)S(1)}, f32[2048]{0:T(1024)}, u32[]{:S(2)}) copy-start(f32[2048]{0:T(1024)} %param.19) | copy-start | bytes 24580
  52.0 15.8 %all-to-all-start.1 = ((bf16[4,64,2048]{2,1,0:T(8,128)(2,1)}), bf16[4,64,2048]{2,1,0:T(8,128)(2,1)S(1)}, u32[]{:S(2)}, u32[]{:S(2)}) async-start(bf16[4,64,2048]{2,1,0:T(8,128)(2,1)} %bitcast.165), calls=%async_computation.1 | async-start | bytes 2097152 | tf_op jit(solution)/shard_map/all_to_all | solution.py:91
  77.3 74.5 %all-to-all-start.2 = ((bf16[128,160,128]{2,1,0:T(8,128)(2,1)}), bf16[128,160,128]{2,1,0:T(8,128)(2,1)}, u32[]{:S(2)}, u32[]{:S(2)}) async-start(bf16[128,160,128]{2,1,0:T(8,128)(2,1)} %bitcast.161), calls=%async_computation.2 | async-start | bytes 10485760 | tf_op jit(solution)/shard_map/all_to_all | solution.py:117
  177.6 7.4 %copy-start.9 = (f32[64,8]{0,1:T(8,128)S(1)}, f32[64,8]{0,1:T(8,128)}, u32[]{:S(2)}) copy-start(f32[64,8]{0,1:T(8,128)} %param.21) | copy-start | bytes 6148
  177.6 68.4 %all-to-all-start.3 = ((bf16[128,160,128]{2,1,0:T(8,128)(2,1)}), bf16[128,160,128]{2,1,0:T(8,128)(2,1)}, u32[]{:S(2)}, u32[]{:S(2)}) async-start(bf16[128,160,128]{2,1,0:T(8,128)(2,1)} %reshape.378), calls=%async_computation.3 | async-start | bytes 10485760 | tf_op jit(solution)/shard_map/all_to_all | solution.py:126

commit v10 on v9

--- a/solution.py
+++ b/solution.py
@@ -1,6 +1,8 @@
 import jax
 import jax.numpy as jnp
 from jax import lax
+from jax.experimental import pallas as pl
+from jax.experimental.pallas import tpu as pltpu
 from jax.sharding import Mesh, PartitionSpec as P
 
 
@@ -8,6 +10,56 @@
 EXPERTS = 64
 FF = 1024
 TOP = 8
+TQ = 256
+
+
+def _attn_kernel(len_ref, q_ref, ck_ref, cv_ref, nk_ref, nv_ref, o_ref):
+    r = pl.program_id(0)
+    qb = pl.program_id(1)
+    length = len_ref[r]
+    q = q_ref[0]
+    scale = HD ** (-0.5)
+    dims = (((1,), (1,)), ((), ()))
+    cache_s = lax.dot_general(q, ck_ref[0, 0], dims, preferred_element_type=jnp.float32) * scale
+    new_s = lax.dot_general(q, nk_ref[0, 0], dims, preferred_element_type=jnp.float32) * scale
+    cache_j = lax.broadcasted_iota(jnp.int32, cache_s.shape, 1)
+    cache_s = jnp.where(cache_j < length, cache_s, -1e30)
+    row = lax.broadcasted_iota(jnp.int32, new_s.shape, 0) + qb * TQ
+    col = lax.broadcasted_iota(jnp.int32, new_s.shape, 1)
+    new_s = jnp.where(col <= row, new_s, -1e30)
+    peak = jnp.maximum(
+        jnp.max(cache_s, axis=1, keepdims=True), jnp.max(new_s, axis=1, keepdims=True)
+    )
+    cache_w = jnp.exp(cache_s - peak)
+    new_w = jnp.exp(new_s - peak)
+    denom = jnp.sum(cache_w, axis=1, keepdims=True) + jnp.sum(new_w, axis=1, keepdims=True)
+    mixed = jnp.dot(
+        cache_w.astype(jnp.bfloat16), cv_ref[0, 0], preferred_element_type=jnp.float32
+    ) + jnp.dot(new_w.astype(jnp.bfloat16), nv_ref[0, 0], preferred_element_type=jnp.float32)
+    o_ref[0] = (mixed / denom).astype(o_ref.dtype)
+
+
+def attention_kernel(queries, new_entries, cache_entries, cache_lengths, interpret=False):
+    reqs, new_len, width = queries.shape
+    cache_len = cache_entries.shape[2]
+    grid_spec = pltpu.PrefetchScalarGridSpec(
+        num_scalar_prefetch=1,
+        grid=(reqs, new_len // TQ),
+        in_specs=[
+            pl.BlockSpec((1, TQ, width), lambda r, b, lens: (r, b, 0)),
+            pl.BlockSpec((1, 1, cache_len, width), lambda r, b, lens: (r, 0, 0, 0)),
+            pl.BlockSpec((1, 1, cache_len, width), lambda r, b, lens: (r, 1, 0, 0)),
+            pl.BlockSpec((1, 1, new_len, width), lambda r, b, lens: (r, 0, 0, 0)),
+            pl.BlockSpec((1, 1, new_len, width), lambda r, b, lens: (r, 1, 0, 0)),
+        ],
+        out_specs=pl.BlockSpec((1, TQ, width), lambda r, b, lens: (r, b, 0)),
+    )
+    return pl.pallas_call(
+        _attn_kernel,
+        grid_spec=grid_spec,
+        out_shape=jax.ShapeDtypeStruct((reqs, new_len, width), jnp.bfloat16),
+        interpret=interpret,
+    )(cache_lengths, queries, cache_entries, cache_entries, new_entries, new_entries)
 
 
 def layer(
@@ -24,49 +76,10 @@
     expert_down,
 ):
     req_local, new_len, width_local = queries.shape
-    heads_local = width_local // HD
-    cache_len = cache_entries.shape[2]
     tok_local = residual.shape[0]
     model_width = residual.shape[1]
 
-    def attend_request(packed):
-        query_rows, new_rows, cache_rows, length = packed
-        query_heads = query_rows.reshape(new_len, heads_local, HD)
-        cache_keys = cache_rows[0].reshape(cache_len, heads_local, HD)
-        cache_vals = cache_rows[1].reshape(cache_len, heads_local, HD)
-        new_keys = new_rows[0].reshape(new_len, heads_local, HD)
-        new_vals = new_rows[1].reshape(new_len, heads_local, HD)
-        scale = HD ** (-0.5)
-        cache_scores = (
-            jnp.einsum("thd,jhd->htj", query_heads, cache_keys, preferred_element_type=jnp.float32)
-            * scale
-        )
-        new_scores = (
-            jnp.einsum("thd,jhd->htj", query_heads, new_keys, preferred_element_type=jnp.float32)
-            * scale
-        )
-        cache_valid = jnp.arange(cache_len, dtype=jnp.int32) < length
-        causal = (
-            jnp.arange(new_len, dtype=jnp.int32)[None, :]
-            <= jnp.arange(new_len, dtype=jnp.int32)[:, None]
-        )
-        scores = jnp.concatenate(
-            [
-                jnp.where(cache_valid[None, None, :], cache_scores, -1e30),
-                jnp.where(causal[None, :, :], new_scores, -1e30),
-            ],
-            axis=-1,
-        )
-        peak = jnp.max(scores, axis=-1, keepdims=True)
-        weights = jnp.exp(scores - peak)
-        denoms = jnp.sum(weights, axis=-1)
-        weights_bf = weights.astype(jnp.bfloat16)
-        all_vals = jnp.concatenate([cache_vals, new_vals], axis=0)
-        mixed = jnp.einsum("htj,jhd->thd", weights_bf, all_vals, preferred_element_type=jnp.float32)
-        mixed = mixed / jnp.transpose(denoms)[:, :, None]
-        return mixed.astype(jnp.bfloat16).reshape(new_len, width_local)
-
-    attention = lax.map(attend_request, (queries, new_entries, cache_entries, cache_lengths))
+    attention = attention_kernel(queries, new_entries, cache_entries, cache_lengths)
     attention = attention.reshape(req_local * new_len, width_local)
     req_count = lax.axis_size("req")
     z_count = lax.axis_size("z")

time: 258 us -> 239 us (0.926)
  matrix products: 44.2 us -> 24 us
  Pallas kernels: 0 us -> 12.4 us
  local copies, waits for them, and re-layouts: 36.5 us -> 27.5 us
  other arithmetic: 12.6 us -> 7.9 us
    dot_general x6 -> x0, matrix products: 20.3 us -> none  [the longest x2 11.7 us: attend_request(): jnp.einsum('htj,jhd->thd', weights_bf, all_vals, preferred_element_type=j...]
    pallas_call x0 -> x1, Pallas kernels: none -> 12.4 us  [attention_kernel(): pl.pallas_call(_attn_kernel, grid_spec=grid_spec, out_shape=jax.ShapeDtyp...]
    squeeze x4 -> x0, local copies, waits for them, and re-layouts: 4.43 us -> none  [the longest x2 2.58 us: attend_request(): cache_vals = cache_rows[1].reshape(cache_len, heads_local, HD)]
    reduce_sum x2 -> x0, other arithmetic: 3.3 us -> none  [attend_request(): denoms = jnp.sum(weights, axis=-1)]
    dynamic_slice x2 -> x0, local copies, waits for them, and re-layouts: 2.65 us -> none  [layer(): lax.map(attend_request, (queries, new_entries, cache_entries, cache_lengt...]
  transfers between devices with their start and end apart: 7 -> 7, of which waited for: 4 -> 4; matrix products, arithmetic and copies ran while one was open for 17% -> 5% of each run, Pallas kernels for 0% -> 5%
where the time goes in v10:
time: 239 us; the launch traced here: 236 us
  waiting for transfers between devices  128 us (54%)
  starting transfers between devices  34.8 us (15%)
  local copies, waits for them, and re-layouts  27.5 us (12%)
  matrix products  24 us (10%)
  Pallas kernels  12.4 us (5%)
  other arithmetic  7.9 us (3%)
    all_to_all x1, waiting for transfers between devices, layer(): returned = lax.all_to_all(back, ('req', 'z', 'x'), 0, 0, tiled=True)  60.4 us
    all_to_all x1, waiting for transfers between devices, layer(): arrived = lax.all_to_all(outgoing, ('req', 'z', 'x'), 0, 0, tiled=True)  56.5 us
    all_to_all x1, starting transfers between devices, layer(): arrived = lax.all_to_all(outgoing, ('req', 'z', 'x'), 0, 0, tiled=True)  14 us
    pallas_call x1, Pallas kernels, attention_kernel(): pl.pallas_call(_attn_kernel, grid_spec=grid_spec, out_shape=jax.ShapeDtyp...  12.4 us
    dot_general x1, matrix products, layer(): jnp.dot(inner, expert_down, preferred_element_type=jnp.float32)  10.3 us
    reshape x1, local copies, waits for them, and re-layouts, layer(): back = half_out.reshape(sources, capacity * folds, lanes)  8.93 us
    all_to_all x1, waiting for transfers between devices, layer(): partial = lax.all_to_all(partial, 'z', 0, 0, tiled=True)  8.47 us
    all_to_all x1, starting transfers between devices, layer(): returned = lax.all_to_all(back, ('req', 'z', 'x'), 0, 0, tiled=True)  7.34 us
  transfers between devices with their start and end apart: 7, of which 4 were waited for; matrix products, arithmetic and copies ran while one was open for 5% of the time, Pallas kernels for 5%

profile of v10, /device:TPU:37, one launch (start us, length us, event | category | flops | bytes accessed | tf_op | source)
XLA Modules:
  0.0 235.7 jit_solution(9813907856089445879)
XLA Ops:
  0.7 1.0 collective-permute-start
  2.2 0.9 collective-permute-start.2
  3.0 12.4 %shard_map.122 = bf16[2,512,128]{2,1,0:T(8,128)(2,1)} custom-call(s32[2]{0:T(128)} %len_ref.1, bf16[2,512,128]{2,1,0:T(8,128)(2,1)} %q_ref.1, bf16[2,2,4096,128]{3,2,1,0:T(8,128)(2,1)} %cv_ref.1, bf16[2,2,4096,128]{3,2,1,0:T(8,128)(2,1)} %cv_ref.1, bf16[2,2,512,128]{3,2,1,0:T(8,128)(2,1)} %nv_ref.1, bf16[2,2,512,128]{3,2,1,0:T(8,128)(2,1)} %nv_ref.1), custom_call_target="tpu_custom_call" | custom-call | tf_op jit(solution)/shard_map/pallas_call | solution.py:57
  15.5 1.7 copy.69
  17.2 6.1 %all-to-all-start = ((bf16[4,4,64,128]{3,2,1,0:T(8,128)(2,1)}), bf16[4,4,64,128]{3,2,1,0:T(8,128)(2,1)S(1)}, u32[]{:S(2)}, u32[]{:S(2)}) async-start(bf16[4,4,64,128]{3,2,1,0:T(8,128)(2,1)} %bitcast.65), calls=%async_computation | async-start | bytes 524288 | tf_op jit(solution)/shard_map/all_to_all | solution.py:96
  23.6 1.2 reduce-window.6
  25.4 2.7 %all-to-all-done = bf16[4,4,64,128]{3,2,1,0:T(8,128)(2,1)S(1)} async-done(((bf16[4,4,64,128]{3,2,1,0:T(8,128)(2,1)}), bf16[4,4,64,128]{3,2,1,0:T(8,128)(2,1)S(1)}, u32[]{:S(2)}, u32[]{:S(2)}) %all-to-all-start) | async-done | bytes 262176 | tf_op jit(solution)/shard_map/all_to_all | solution.py:96
  28.9 1.6 pad_maximum_fusion
  30.6 1.7 convolution_convert_fusion.1
  32.3 5.0 %all-to-all-start.1 = ((bf16[4,64,2048]{2,1,0:T(8,128)(2,1)}), bf16[4,64,2048]{2,1,0:T(8,128)(2,1)S(1)}, u32[]{:S(2)}, u32[]{:S(2)}) async-start(bf16[4,64,2048]{2,1,0:T(8,128)(2,1)} %bitcast.70), calls=%async_computation.1 | async-start | bytes 2097152 | tf_op jit(solution)/shard_map/all_to_all | solution.py:104
  37.4 2.4 %scatter_custom_fusion = s32[640]{0:T(1024)S(1)} fusion(s32[512]{0:T(512)S(1)} %bitcast.79, s32[512]{0:T(512)S(1)} %add_select_fusion, s32[]{:T(128)} %constant.60.clone.1), kind=kCustom, calls=%fused_computation.52 | custom fusion | bytes 2564 | tf_op jit(solution)/shard_map/scatter | solution.py:123
  39.9 8.5 %all-to-all-done.1 = bf16[4,64,2048]{2,1,0:T(8,128)(2,1)S(1)} async-done(((bf16[4,64,2048]{2,1,0:T(8,128)(2,1)}), bf16[4,64,2048]{2,1,0:T(8,128)(2,1)S(1)}, u32[]{:S(2)}, u32[]{:S(2)}) %all-to-all-start.1) | async-done | bytes 1048608 | tf_op jit(solution)/shard_map/all_to_all | solution.py:104
  49.5 3.3 %gather_fusion.1 = bf16[640,16,128]{2,1,0:T(8,128)(2,1)} fusion(bf16[65,16,128]{2,1,0:T(8,128)(2,1)S(1)} %concatenate.3, s32[1024]{0:T(1024)S(1)} %pad_clamp_fusion), kind=kCustom, calls=%fused_computation.1 | custom fusion | bytes 5245440 | tf_op jit(solution)/shard_map/gather | solution.py:127
  52.9 5.0 %broadcast_in_dim.38 = bf16[64,2,160,128]{3,2,1,0:T(8,128)(2,1)} broadcast(bf16[64,160,128]{2,1,0:T(8,128)(2,1)} %bitcast.68), dimensions={0,2,3} | broadcast | bytes 7864320 | tf_op jit(solution)/shard_map/broadcast_in_dim | solution.py:128
  57.9 14.0 %all-to-all-start.2 = ((bf16[128,160,128]{2,1,0:T(8,128)(2,1)}), bf16[128,160,128]{2,1,0:T(8,128)(2,1)}, u32[]{:S(2)}, u32[]{:S(2)}) async-start(bf16[128,160,128]{2,1,0:T(8,128)(2,1)} %bitcast.66), calls=%async_computation.2 | async-start | bytes 10485760 | tf_op jit(solution)/shard_map/all_to_all | solution.py:130
  71.8 4.5 %fusion.40 = (bf16[1,2048,512]{2,1,0:T(8,128)(2,1)}, bf16[1,2048,512]{2,1,0:T(8,128)(2,1)}) fusion(bf16[2,2048,512]{2,1,0:T(8,128)(2,1)} %param.20), kind=kLoop, calls=%fused_computation.62 | loop fusion | bytes 8388608 | tf_op jit(solution)/shard_map/slice | solution.py:134
  76.3 56.5 %all-to-all-done.2 = bf16[128,160,128]{2,1,0:T(8,128)(2,1)} async-done(((bf16[128,160,128]{2,1,0:T(8,128)(2,1)}), bf16[128,160,128]{2,1,0:T(8,128)(2,1)}, u32[]{:S(2)}, u32[]{:S(2)}) %all-to-all-start.2) | async-done | bytes 5242912 | tf_op jit(solution)/shard_map/all_to_all | solution.py:130
  132.8 6.5 %fusion.7 = f32[1280,512]{1,0:T(8,128)} fusion(bf16[16,128,512]{2,1,0:T(8,128)(2,1)} %bitcast.72, bf16[1280,16,128]{2,1,0:T(8,128)(2,1)} %bitcast.15), kind=kOutput, calls=%fused_computation.12 | convolution fusion | flops 2684354560 | bytes 9961472 | tf_op jit(solution)/shard_map/tkd,kdf->tf/dot_general | solution.py:134
  139.4 10.3 %convolution_convert_fusion = bf16[1280,2048]{1,0:T(8,128)(2,1)} fusion(bf16[512,2048]{1,0:T(8,128)(2,1)S(1)} %copy-done, bf16[16,128,512]{2,1,0:T(8,128)(2,1)} %bitcast.71, bf16[1280,16,128]{2,1,0:T(8,128)(2,1)} %bitcast.15, f32[1280,512]{1,0:T(8,128)} %fusion.7), kind=kOutput, calls=%fused_computation.3 | convolution fusion | flops 5375262720 | bytes 17301504 | tf_op jit(solution)/shard_map/dot_general | solution.py:137
  149.7 8.9 %reshape.167 = bf16[128,160,128]{2,1,0:T(8,128)(2,1)} reshape(bf16[1280,2048]{1,0:T(8,128)(2,1)} %convolution_convert_fusion) | data formatting | bytes 10485760 | tf_op jit(solution)/shard_map/reshape | solution.py:138
  158.7 7.3 %all-to-all-start.3 = ((bf16[128,160,128]{2,1,0:T(8,128)(2,1)}), bf16[128,160,128]{2,1,0:T(8,128)(2,1)}, u32[]{:S(2)}, u32[]{:S(2)}) async-start(bf16[128,160,128]{2,1,0:T(8,128)(2,1)} %reshape.167), calls=%async_computation.3 | async-start | bytes 10485760 | tf_op jit(solution)/shard_map/all_to_all | solution.py:139
  166.6 60.4 %all-to-all-done.3 = bf16[128,160,128]{2,1,0:T(8,128)(2,1)} async-done(((bf16[128,160,128]{2,1,0:T(8,128)(2,1)}), bf16[128,160,128]{2,1,0:T(8,128)(2,1)}, u32[]{:S(2)}, u32[]{:S(2)}) %all-to-all-start.3) | async-done | bytes 5242912 | tf_op jit(solution)/shard_map/all_to_all | solution.py:139
  227.0 3.3 %convert_add_fusion = f32[64,1,10,16,128]{4,3,2,1,0:T(8,128)S(1)} fusion(bf16[64,2,10,16,128]{4,3,2,1,0:T(8,128)(2,1)} %bitcast.20), kind=kLoop, calls=%fused_computation.7 | loop fusion | flops 3932160 | bytes 10485760 | tf_op jit(solution)/shard_map/add | solution.py:141
  230.3 5.4 %fusion.19 = bf16[64,2048]{1,0:T(8,128)(2,1)} fusion(f32[64,640]{1,0:T(8,128)S(1)} %select_reduce_fusion, f32[80,8,16,128]{3,2,1,0:T(8,128)S(1)} %bitcast.67), kind=kOutput, calls=%fused_computation.17 | convolution fusion | flops 1006764032 | bytes 5668864 | tf_op jit(solution)/shard_map/dot_general | solution.py:150
  (44 shorter events, 4.0 us)
Async XLA Ops:
  0.6 138.8 %copy-start = (bf16[512,2048]{1,0:T(8,128)(2,1)S(1)}, bf16[512,2048]{1,0:T(8,128)(2,1)}, u32[]{:S(2)}) copy-start(bf16[512,2048]{1,0:T(8,128)(2,1)} %param.21) | copy-start | bytes 6291460
  0.6 22.7 %copy-start.4 = (s32[64,8]{0,1:T(8,128)S(1)}, s32[64,8]{0,1:T(8,128)}, u32[]{:S(2)}) copy-start(s32[64,8]{0,1:T(8,128)} %param.18) | copy-start | bytes 6148
  0.7 28.3 %collective-permute-start = (bf16[128,2048]{1,0:T(8,128)(2,1)}, bf16[128,2048]{1,0:T(8,128)(2,1)}, u32[]{:S(2)}, u32[]{:S(2)}) collective-permute-start(bf16[128,2048]{1,0:T(8,128)(2,1)} %param.15), channel_id=1, source_target_pairs={{0,1},{1,2},{2,3},{3,0},{4,5},{5,6},{6,7},{7,4},{8,9},{9,10},{10,1... | collective-permute-start | bytes 1572872 | tf_op jit(solution)/shard_map/ppermute | solution.py:91
  1.6 27.3 %collective-permute-start.1 = (bf16[128,2048]{1,0:T(8,128)(2,1)}, bf16[128,2048]{1,0:T(8,128)(2,1)}, u32[]{:S(2)}, u32[]{:S(2)}) collective-permute-start(bf16[128,2048]{1,0:T(8,128)(2,1)} %param.15), channel_id=1, source_target_pairs={{0,2},{1,3},{2,0},{3,1},{4,6},{5,7},{6,4},{7,5},{8,10},{9,11},{10,... | collective-permute-start | bytes 1572872 | tf_op jit(solution)/shard_map/ppermute | solution.py:91
  2.2 26.8 %collective-permute-start.2 = (bf16[128,2048]{1,0:T(8,128)(2,1)}, bf16[128,2048]{1,0:T(8,128)(2,1)}, u32[]{:S(2)}, u32[]{:S(2)}) collective-permute-start(bf16[128,2048]{1,0:T(8,128)(2,1)} %param.15), channel_id=1, source_target_pairs={{0,3},{1,0},{2,1},{3,2},{4,7},{5,4},{6,5},{7,6},{8,11},{9,8},{10,9... | collective-permute-start | bytes 1572872 | tf_op jit(solution)/shard_map/ppermute | solution.py:91
  15.5 13.5 %copy-start.2 = (bf16[128,2048]{1,0:T(8,128)(2,1)S(1)}, bf16[128,2048]{1,0:T(8,128)(2,1)}, u32[]{:S(2)}) copy-start(bf16[128,2048]{1,0:T(8,128)(2,1)} %param.15) | copy-start | bytes 1572868
  17.2 10.9 %all-to-all-start = ((bf16[4,4,64,128]{3,2,1,0:T(8,128)(2,1)}), bf16[4,4,64,128]{3,2,1,0:T(8,128)(2,1)S(1)}, u32[]{:S(2)}, u32[]{:S(2)}) async-start(bf16[4,4,64,128]{3,2,1,0:T(8,128)(2,1)} %bitcast.65), calls=%async_computation | async-start | bytes 524288 | tf_op jit(solution)/shard_map/all_to_all | solution.py:96
  32.3 16.2 %copy-start.1 = (bf16[64,2048]{1,0:T(8,128)(2,1)S(1)}, bf16[64,2048]{1,0:T(8,128)(2,1)}, u32[]{:S(2)}) copy-start(bf16[64,2048]{1,0:T(8,128)(2,1)} %param.16) | copy-start | bytes 786436
  32.3 16.4 %copy-start.3 = (f32[2048]{0:T(1024)S(1)}, f32[2048]{0:T(1024)}, u32[]{:S(2)}) copy-start(f32[2048]{0:T(1024)} %param.17) | copy-start | bytes 24580
  32.3 16.1 %all-to-all-start.1 = ((bf16[4,64,2048]{2,1,0:T(8,128)(2,1)}), bf16[4,64,2048]{2,1,0:T(8,128)(2,1)S(1)}, u32[]{:S(2)}, u32[]{:S(2)}) async-start(bf16[4,64,2048]{2,1,0:T(8,128)(2,1)} %bitcast.70), calls=%async_computation.1 | async-start | bytes 2097152 | tf_op jit(solution)/shard_map/all_to_all | solution.py:104
  57.9 75.0 %all-to-all-start.2 = ((bf16[128,160,128]{2,1,0:T(8,128)(2,1)}), bf16[128,160,128]{2,1,0:T(8,128)(2,1)}, u32[]{:S(2)}, u32[]{:S(2)}) async-start(bf16[128,160,128]{2,1,0:T(8,128)(2,1)} %bitcast.66), calls=%async_computation.2 | async-start | bytes 10485760 | tf_op jit(solution)/shard_map/all_to_all | solution.py:130
  158.7 7.4 %copy-start.5 = (f32[64,8]{0,1:T(8,128)S(1)}, f32[64,8]{0,1:T(8,128)}, u32[]{:S(2)}) copy-start(f32[64,8]{0,1:T(8,128)} %param.19) | copy-start | bytes 6148
  158.7 68.4 %all-to-all-start.3 = ((bf16[128,160,128]{2,1,0:T(8,128)(2,1)}), bf16[128,160,128]{2,1,0:T(8,128)(2,1)}, u32[]{:S(2)}, u32[]{:S(2)}) async-start(bf16[128,160,128]{2,1,0:T(8,128)(2,1)} %reshape.167), calls=%async_computation.3 | async-start | bytes 10485760 | tf_op jit(solution)/shard_map/all_to_all | solution.py:139

commit v11 on v10

--- a/solution.py
+++ b/solution.py
@@ -124,8 +124,8 @@
     normed_fold = jnp.concatenate(
         [normed.reshape(tok_local, folds, lanes), jnp.zeros((1, folds, lanes), jnp.bfloat16)], axis=0
     )
-    slot_rows = normed_fold[rows_table].reshape(EXPERTS, 1, capacity * folds, lanes)
-    outgoing = jnp.broadcast_to(slot_rows, (EXPERTS, 2, capacity * folds, lanes))
+    dest_table = jnp.broadcast_to(rows_table.reshape(EXPERTS, 1, capacity), (EXPERTS, 2, capacity))
+    outgoing = normed_fold[dest_table.reshape(-1)]
     outgoing = outgoing.reshape(devices, pieces * capacity * folds, lanes)
     arrived = lax.all_to_all(outgoing, ("req", "z", "x"), 0, 0, tiled=True)
     sources = arrived.shape[0]
@@ -137,19 +137,20 @@
     half_out = jnp.dot(inner, expert_down, preferred_element_type=jnp.float32).astype(jnp.bfloat16)
     back = half_out.reshape(sources, capacity * folds, lanes)
     returned = lax.all_to_all(back, ("req", "z", "x"), 0, 0, tiled=True)
-    halves = returned.reshape(EXPERTS, 2, capacity, folds, lanes)
-    summed = (halves[:, 0].astype(jnp.float32) + halves[:, 1].astype(jnp.float32)).reshape(
-        EXPERTS * capacity, folds * lanes
-    )
     slot_ids = jnp.arange(EXPERTS * capacity, dtype=jnp.int32)
     route_slots = positions.reshape(tok_local, TOP)
     mixing = jnp.sum(
         jnp.where(route_slots[:, :, None] == slot_ids[None, None, :], gate_weights[:, :, None], 0.0),
         axis=1,
     )
-    expert_out = jnp.dot(
-        mixing, summed, precision=lax.Precision.HIGHEST, preferred_element_type=jnp.float32
-    ).astype(jnp.bfloat16)
+    mixing = jnp.broadcast_to(mixing.reshape(tok_local, EXPERTS, 1, capacity), (tok_local, EXPERTS, 2, capacity))
+    mixing = mixing.reshape(tok_local, EXPERTS * 2 * capacity)
+    both = returned.reshape(EXPERTS * 2 * capacity, folds, lanes).astype(jnp.float32)
+    expert_out = jnp.einsum(
+        "ts,skd->tkd", mixing, both, precision=lax.Precision.HIGHEST,
+        preferred_element_type=jnp.float32,
+    )
+    expert_out = expert_out.astype(jnp.bfloat16).reshape(tok_local, model_width)
     return (attended, expert_out)
 
 

time: 239 us -> 234 us (0.979)
  starting transfers between devices: 34.8 us -> 30.7 us
  other arithmetic: 7.9 us -> 4.64 us
    add x1, other arithmetic: 3.28 us -> 0.01 us  [layer(): positions = flat_routes * capacity + slot_index]
    all_to_all x1, waiting for transfers between devices: 60.4 us -> 57.4 us  [layer(): returned = lax.all_to_all(back, ('req', 'z', 'x'), 0, 0, tiled=True)]
    all_to_all x1, waiting for transfers between devices: 2.72 us -> 5.73 us  [layer(): rows_att = lax.all_to_all(rows_att, 'x', 0, 0, tiled=True)]
    all_to_all x1, starting transfers between devices: 14 us -> 11.1 us  [layer(): arrived = lax.all_to_all(outgoing, ('req', 'z', 'x'), 0, 0, tiled=True)]
    broadcast_in_dim x1 -> x4, local copies, waits for them, and re-layouts: 4.96 us -> 2.14 us  [the longest x2 1.99 us: layer(): jnp.broadcast_to(mixing.reshape(tok_local, EXPERTS, 1, capacity), (tok_lo...]
  transfers between devices with their start and end apart: 7 -> 7, of which waited for: 4 -> 4; matrix products, arithmetic and copies ran while one was open for 5% -> 7% of each run, Pallas kernels for 5% -> 5%
where the time goes in v11:
time: 234 us; the launch traced here: 231 us
  waiting for transfers between devices  129 us (55%)
  starting transfers between devices  30.7 us (13%)
  local copies, waits for them, and re-layouts  28.4 us (12%)
  matrix products  24.4 us (10%)
  Pallas kernels  12.4 us (5%)
  other arithmetic  4.64 us (2%)
    all_to_all x1, waiting for transfers between devices, layer(): returned = lax.all_to_all(back, ('req', 'z', 'x'), 0, 0, tiled=True)  57.4 us
    all_to_all x1, waiting for transfers between devices, layer(): arrived = lax.all_to_all(outgoing, ('req', 'z', 'x'), 0, 0, tiled=True)  56.5 us
    pallas_call x1, Pallas kernels, attention_kernel(): pl.pallas_call(_attn_kernel, grid_spec=grid_spec, out_shape=jax.ShapeDtyp...  12.4 us
    all_to_all x1, starting transfers between devices, layer(): arrived = lax.all_to_all(outgoing, ('req', 'z', 'x'), 0, 0, tiled=True)  11.1 us
    dot_general x1, matrix products, layer(): jnp.dot(inner, expert_down, preferred_element_type=jnp.float32)  10.4 us
    all_to_all x1, waiting for transfers between devices, layer(): partial = lax.all_to_all(partial, 'z', 0, 0, tiled=True)  9.56 us
    reshape x1, local copies, waits for them, and re-layouts, layer(): back = half_out.reshape(sources, capacity * folds, lanes)  8.93 us
    all_to_all x1, starting transfers between devices, layer(): returned = lax.all_to_all(back, ('req', 'z', 'x'), 0, 0, tiled=True)  7.32 us
  transfers between devices with their start and end apart: 7, of which 4 were waited for; matrix products, arithmetic and copies ran while one was open for 7% of the time, Pallas kernels for 5%

profile of v11, /device:TPU:37, one launch (start us, length us, event | category | flops | bytes accessed | tf_op | source)
XLA Modules:
  0.0 230.6 jit_solution(1150431134489537275)
XLA Ops:
  1.0 2.5 %collective-permute-start.1 = (bf16[128,2048]{1,0:T(8,128)(2,1)}, bf16[128,2048]{1,0:T(8,128)(2,1)}, u32[]{:S(2)}, u32[]{:S(2)}) collective-permute-start(bf16[128,2048]{1,0:T(8,128)(2,1)} %param.15), channel_id=1, source_target_pairs={{0,2},{1,3},{2,0},{3,1},{4,6},{5,7},{6,4},{7,5},{8,10},{9,11},{10,... | collective-permute-start | bytes 1572872 | tf_op jit(solution)/shard_map/ppermute | solution.py:91
  3.4 12.4 %shard_map.122 = bf16[2,512,128]{2,1,0:T(8,128)(2,1)} custom-call(s32[2]{0:T(128)} %len_ref.1, bf16[2,512,128]{2,1,0:T(8,128)(2,1)} %q_ref.1, bf16[2,2,4096,128]{3,2,1,0:T(8,128)(2,1)} %cv_ref.1, bf16[2,2,4096,128]{3,2,1,0:T(8,128)(2,1)} %cv_ref.1, bf16[2,2,512,128]{3,2,1,0:T(8,128)(2,1)} %nv_ref.1, bf16[2,2,512,128]{3,2,1,0:T(8,128)(2,1)} %nv_ref.1), custom_call_target="tpu_custom_call" | custom-call | tf_op jit(solution)/shard_map/pallas_call | solution.py:57
  15.9 1.7 copy.83
  17.6 4.5 %all-to-all-start = ((bf16[4,4,64,128]{3,2,1,0:T(8,128)(2,1)}), bf16[4,4,64,128]{3,2,1,0:T(8,128)(2,1)S(1)}, u32[]{:S(2)}, u32[]{:S(2)}) async-start(bf16[4,4,64,128]{3,2,1,0:T(8,128)(2,1)} %bitcast.68), calls=%async_computation | async-start | bytes 524288 | tf_op jit(solution)/shard_map/all_to_all | solution.py:96
  22.4 1.2 reduce-window.6
  24.2 5.7 %all-to-all-done = bf16[4,4,64,128]{3,2,1,0:T(8,128)(2,1)S(1)} async-done(((bf16[4,4,64,128]{3,2,1,0:T(8,128)(2,1)}), bf16[4,4,64,128]{3,2,1,0:T(8,128)(2,1)S(1)}, u32[]{:S(2)}, u32[]{:S(2)}) %all-to-all-start) | async-done | bytes 262176 | tf_op jit(solution)/shard_map/all_to_all | solution.py:96
  30.7 1.6 pad_maximum_fusion
  32.4 1.7 convolution_convert_fusion.1
  34.1 5.0 %all-to-all-start.1 = ((bf16[4,64,2048]{2,1,0:T(8,128)(2,1)}), bf16[4,64,2048]{2,1,0:T(8,128)(2,1)S(1)}, u32[]{:S(2)}, u32[]{:S(2)}) async-start(bf16[4,64,2048]{2,1,0:T(8,128)(2,1)} %bitcast.71), calls=%async_computation.1 | async-start | bytes 2097152 | tf_op jit(solution)/shard_map/all_to_all | solution.py:104
  39.2 2.4 %scatter_custom_fusion = s32[640]{0:T(1024)S(1)} fusion(s32[512]{0:T(512)S(1)} %bitcast.81, s32[512]{0:T(512)S(1)} %add_select_fusion, s32[]{:T(128)} %constant.60.clone.1), kind=kCustom, calls=%fused_computation.54 | custom fusion | bytes 2564 | tf_op jit(solution)/shard_map/scatter | solution.py:123
  42.0 9.6 %all-to-all-done.1 = bf16[4,64,2048]{2,1,0:T(8,128)(2,1)S(1)} async-done(((bf16[4,64,2048]{2,1,0:T(8,128)(2,1)}), bf16[4,64,2048]{2,1,0:T(8,128)(2,1)S(1)}, u32[]{:S(2)}, u32[]{:S(2)}) %all-to-all-start.1) | async-done | bytes 1048608 | tf_op jit(solution)/shard_map/all_to_all | solution.py:104
  52.8 5.0 %gather_fusion.1 = bf16[1280,16,128]{2,1,0:T(8,128)(2,1)} fusion(bf16[65,16,128]{2,1,0:T(8,128)(2,1)S(1)} %concatenate.3, s32[2048]{0:T(1024)S(1)} %pad_clamp_fusion), kind=kCustom, calls=%fused_computation.1 | custom fusion | bytes 10490880 | tf_op jit(solution)/shard_map/gather | solution.py:128
  57.8 11.1 %all-to-all-start.2 = ((bf16[128,160,128]{2,1,0:T(8,128)(2,1)}), bf16[128,160,128]{2,1,0:T(8,128)(2,1)}, u32[]{:S(2)}, u32[]{:S(2)}) async-start(bf16[128,160,128]{2,1,0:T(8,128)(2,1)} %bitcast.69), calls=%async_computation.2 | async-start | bytes 10485760 | tf_op jit(solution)/shard_map/all_to_all | solution.py:130
  68.9 4.5 %fusion.44 = (bf16[1,2048,512]{2,1,0:T(8,128)(2,1)}, bf16[1,2048,512]{2,1,0:T(8,128)(2,1)}) fusion(bf16[2,2048,512]{2,1,0:T(8,128)(2,1)} %param.20), kind=kLoop, calls=%fused_computation.64 | loop fusion | bytes 8388608 | tf_op jit(solution)/shard_map/slice | solution.py:134
  73.3 56.5 %all-to-all-done.2 = bf16[128,160,128]{2,1,0:T(8,128)(2,1)} async-done(((bf16[128,160,128]{2,1,0:T(8,128)(2,1)}), bf16[128,160,128]{2,1,0:T(8,128)(2,1)}, u32[]{:S(2)}, u32[]{:S(2)}) %all-to-all-start.2) | async-done | bytes 5242912 | tf_op jit(solution)/shard_map/all_to_all | solution.py:130
  129.9 6.5 %fusion.6 = f32[1280,512]{1,0:T(8,128)} fusion(bf16[16,128,512]{2,1,0:T(8,128)(2,1)} %bitcast.73, bf16[1280,16,128]{2,1,0:T(8,128)(2,1)} %bitcast.15), kind=kOutput, calls=%fused_computation.10 | convolution fusion | flops 2684354560 | bytes 9961472 | tf_op jit(solution)/shard_map/tkd,kdf->tf/dot_general | solution.py:134
  136.4 10.4 %convolution_convert_fusion = bf16[1280,2048]{1,0:T(8,128)(2,1)} fusion(bf16[512,2048]{1,0:T(8,128)(2,1)S(1)} %copy-done, bf16[16,128,512]{2,1,0:T(8,128)(2,1)} %bitcast.72, bf16[1280,16,128]{2,1,0:T(8,128)(2,1)} %bitcast.15, f32[1280,512]{1,0:T(8,128)} %fusion.6), kind=kOutput, calls=%fused_computation.3 | convolution fusion | flops 5375262720 | bytes 17301504 | tf_op jit(solution)/shard_map/dot_general | solution.py:137
  146.8 8.9 %reshape.202 = bf16[128,160,128]{2,1,0:T(8,128)(2,1)} reshape(bf16[1280,2048]{1,0:T(8,128)(2,1)} %convolution_convert_fusion) | data formatting | bytes 10485760 | tf_op jit(solution)/shard_map/reshape | solution.py:138
  155.7 7.3 %all-to-all-start.3 = ((bf16[128,160,128]{2,1,0:T(8,128)(2,1)}), bf16[128,160,128]{2,1,0:T(8,128)(2,1)}, u32[]{:S(2)}, u32[]{:S(2)}) async-start(bf16[128,160,128]{2,1,0:T(8,128)(2,1)} %reshape.202), calls=%async_computation.3 | async-start | bytes 10485760 | tf_op jit(solution)/shard_map/all_to_all | solution.py:139
  163.8 0.9 broadcast_in_dim.40
  164.7 1.1 broadcast_in_dim.41
  165.8 0.9 reshape.197
  166.7 57.4 %all-to-all-done.3 = bf16[128,160,128]{2,1,0:T(8,128)(2,1)} async-done(((bf16[128,160,128]{2,1,0:T(8,128)(2,1)}), bf16[128,160,128]{2,1,0:T(8,128)(2,1)}, u32[]{:S(2)}, u32[]{:S(2)}) %all-to-all-start.3) | async-done | bytes 5242912 | tf_op jit(solution)/shard_map/all_to_all | solution.py:139
  224.1 5.8 %fusion.23 = bf16[16,8,8,128]{3,2,1,0:T(8,128)(2,1)S(1)} fusion(bf16[1280,16,128]{2,1,0:T(8,128)(2,1)} %bitcast.20, f32[64,1280]{0,1:T(8,128)} %reshape.197), kind=kOutput, calls=%fused_computation.20 | convolution fusion | flops 2013396992 | bytes 5832704 | tf_op jit(solution)/shard_map/ts,skd->tkd/dot_general | solution.py:149
  (50 shorter events, 5.0 us)
Async XLA Ops:
  0.6 135.8 %copy-start = (bf16[512,2048]{1,0:T(8,128)(2,1)S(1)}, bf16[512,2048]{1,0:T(8,128)(2,1)}, u32[]{:S(2)}) copy-start(bf16[512,2048]{1,0:T(8,128)(2,1)} %param.21) | copy-start | bytes 6291460
  0.6 21.5 %copy-start.4 = (s32[64,8]{0,1:T(8,128)S(1)}, s32[64,8]{0,1:T(8,128)}, u32[]{:S(2)}) copy-start(s32[64,8]{0,1:T(8,128)} %param.18) | copy-start | bytes 6148
  0.7 30.0 %collective-permute-start.2 = (bf16[128,2048]{1,0:T(8,128)(2,1)}, bf16[128,2048]{1,0:T(8,128)(2,1)}, u32[]{:S(2)}, u32[]{:S(2)}) collective-permute-start(bf16[128,2048]{1,0:T(8,128)(2,1)} %param.15), channel_id=1, source_target_pairs={{0,3},{1,0},{2,1},{3,2},{4,7},{5,4},{6,5},{7,6},{8,11},{9,8},{10,9... | collective-permute-start | bytes 1572872 | tf_op jit(solution)/shard_map/ppermute | solution.py:91
  1.0 29.7 %collective-permute-start.1 = (bf16[128,2048]{1,0:T(8,128)(2,1)}, bf16[128,2048]{1,0:T(8,128)(2,1)}, u32[]{:S(2)}, u32[]{:S(2)}) collective-permute-start(bf16[128,2048]{1,0:T(8,128)(2,1)} %param.15), channel_id=1, source_target_pairs={{0,2},{1,3},{2,0},{3,1},{4,6},{5,7},{6,4},{7,5},{8,10},{9,11},{10,... | collective-permute-start | bytes 1572872 | tf_op jit(solution)/shard_map/ppermute | solution.py:91
  3.4 27.3 %collective-permute-start = (bf16[128,2048]{1,0:T(8,128)(2,1)}, bf16[128,2048]{1,0:T(8,128)(2,1)}, u32[]{:S(2)}, u32[]{:S(2)}) collective-permute-start(bf16[128,2048]{1,0:T(8,128)(2,1)} %param.15), channel_id=1, source_target_pairs={{0,1},{1,2},{2,3},{3,0},{4,5},{5,6},{6,7},{7,4},{8,9},{9,10},{10,1... | collective-permute-start | bytes 1572872 | tf_op jit(solution)/shard_map/ppermute | solution.py:91
  15.9 14.9 %copy-start.2 = (bf16[128,2048]{1,0:T(8,128)(2,1)S(1)}, bf16[128,2048]{1,0:T(8,128)(2,1)}, u32[]{:S(2)}) copy-start(bf16[128,2048]{1,0:T(8,128)(2,1)} %param.15) | copy-start | bytes 1572868
  17.6 12.3 %all-to-all-start = ((bf16[4,4,64,128]{3,2,1,0:T(8,128)(2,1)}), bf16[4,4,64,128]{3,2,1,0:T(8,128)(2,1)S(1)}, u32[]{:S(2)}, u32[]{:S(2)}) async-start(bf16[4,4,64,128]{3,2,1,0:T(8,128)(2,1)} %bitcast.68), calls=%async_computation | async-start | bytes 524288 | tf_op jit(solution)/shard_map/all_to_all | solution.py:96
  34.1 17.6 %copy-start.1 = (bf16[64,2048]{1,0:T(8,128)(2,1)S(1)}, bf16[64,2048]{1,0:T(8,128)(2,1)}, u32[]{:S(2)}) copy-start(bf16[64,2048]{1,0:T(8,128)(2,1)} %param.16) | copy-start | bytes 786436
  34.1 17.8 %copy-start.3 = (f32[2048]{0:T(1024)S(1)}, f32[2048]{0:T(1024)}, u32[]{:S(2)}) copy-start(f32[2048]{0:T(1024)} %param.17) | copy-start | bytes 24580
  34.1 17.5 %all-to-all-start.1 = ((bf16[4,64,2048]{2,1,0:T(8,128)(2,1)}), bf16[4,64,2048]{2,1,0:T(8,128)(2,1)S(1)}, u32[]{:S(2)}, u32[]{:S(2)}) async-start(bf16[4,64,2048]{2,1,0:T(8,128)(2,1)} %bitcast.71), calls=%async_computation.1 | async-start | bytes 2097152 | tf_op jit(solution)/shard_map/all_to_all | solution.py:104
  57.8 72.1 %all-to-all-start.2 = ((bf16[128,160,128]{2,1,0:T(8,128)(2,1)}), bf16[128,160,128]{2,1,0:T(8,128)(2,1)}, u32[]{:S(2)}, u32[]{:S(2)}) async-start(bf16[128,160,128]{2,1,0:T(8,128)(2,1)} %bitcast.69), calls=%async_computation.2 | async-start | bytes 10485760 | tf_op jit(solution)/shard_map/all_to_all | solution.py:130
  155.7 7.3 %copy-start.5 = (f32[64,8]{0,1:T(8,128)S(1)}, f32[64,8]{0,1:T(8,128)}, u32[]{:S(2)}) copy-start(f32[64,8]{0,1:T(8,128)} %param.19) | copy-start | bytes 6148
  155.7 68.3 %all-to-all-start.3 = ((bf16[128,160,128]{2,1,0:T(8,128)(2,1)}), bf16[128,160,128]{2,1,0:T(8,128)(2,1)}, u32[]{:S(2)}, u32[]{:S(2)}) async-start(bf16[128,160,128]{2,1,0:T(8,128)(2,1)} %reshape.202), calls=%async_computation.3 | async-start | bytes 10485760 | tf_op jit(solution)/shard_map/all_to_all | solution.py:139

commit v12 on v11

--- a/solution.py
+++ b/solution.py
@@ -1,3 +1,4 @@
+import numpy as np
 import jax
 import jax.numpy as jnp
 from jax import lax
@@ -81,9 +82,18 @@
 
     attention = attention_kernel(queries, new_entries, cache_entries, cache_lengths)
     attention = attention.reshape(req_local * new_len, width_local)
-    req_count = lax.axis_size("req")
+    y_count = lax.axis_size("y")
+    c_count = lax.axis_size("c")
+    req_count = y_count * c_count
     z_count = lax.axis_size("z")
     x_count = lax.axis_size("x")
+    swap_pairs = []
+    for c in range(c_count):
+        for x in range(x_count):
+            partner = (1 - c, x + 1 - 2 * (x % 2)) if c != x % 2 else (c, x)
+            swap_pairs.append((c * x_count + x, partner[0] * x_count + partner[1]))
+    my_in = lax.ppermute(expert_in, ("c", "x"), swap_pairs)
+    my_down = lax.ppermute(expert_down, ("c", "x"), swap_pairs)
     x_here = lax.axis_index("x")
     shifted = [out_proj]
     for step in range(1, x_count):
@@ -109,7 +119,6 @@
     normed = (hidden * lax.rsqrt(mean_square + 1e-05) * norm_gain).astype(jnp.bfloat16)
     devices = req_count * z_count * x_count
     half_units = FF // 2
-    pieces = expert_in.shape[2] // half_units
     capacity = max(2, tok_local * TOP * 5 // (EXPERTS * 4))
     lanes = 128
     folds = model_width // lanes
@@ -124,30 +133,42 @@
     normed_fold = jnp.concatenate(
         [normed.reshape(tok_local, folds, lanes), jnp.zeros((1, folds, lanes), jnp.bfloat16)], axis=0
     )
-    dest_table = jnp.broadcast_to(rows_table.reshape(EXPERTS, 1, capacity), (EXPERTS, 2, capacity))
-    outgoing = normed_fold[dest_table.reshape(-1)]
-    outgoing = outgoing.reshape(devices, pieces * capacity * folds, lanes)
-    arrived = lax.all_to_all(outgoing, ("req", "z", "x"), 0, 0, tiled=True)
+    split = capacity // c_count
+    dev = np.arange(devices)
+    dev_c = (dev // (z_count * x_count)) % c_count
+    dev_y = dev // (c_count * z_count * x_count)
+    dev_zx = dev % (z_count * x_count)
+    dev_x = dev % x_count
+    chip_expert = ((dev_y * c_count + dev_x % c_count) * z_count * x_count + dev_zx) // 2
+    slot_of = (
+        chip_expert[:, None] * capacity + dev_c[:, None] * split + np.arange(split)[None, :]
+    ).reshape(-1)
+    slot_of = jnp.asarray(slot_of, jnp.int32)
+    outgoing = normed_fold[rows_table[slot_of]]
+    outgoing = outgoing.reshape(devices, split * folds, lanes)
+    arrived = lax.all_to_all(outgoing, ("y", "c", "z", "x"), 0, 0, tiled=True)
+    other = lax.ppermute(arrived, "c", [(0, 1), (1, 0)])
     sources = arrived.shape[0]
-    rows = arrived.reshape(sources * capacity, folds, lanes)
-    w_in = expert_in[:, :, 0:half_units].reshape(2, folds, lanes, half_units)
+    rows = jnp.concatenate([arrived, other], axis=0).reshape(2 * sources * split, folds, lanes)
+    w_in = my_in.reshape(2, folds, lanes, half_units)
     gate_part = jnp.einsum("tkd,kdf->tf", rows, w_in[0], preferred_element_type=jnp.float32)
     up_part = jnp.einsum("tkd,kdf->tf", rows, w_in[1], preferred_element_type=jnp.float32)
     inner = (jax.nn.silu(gate_part) * up_part).astype(jnp.bfloat16)
-    half_out = jnp.dot(inner, expert_down, preferred_element_type=jnp.float32).astype(jnp.bfloat16)
-    back = half_out.reshape(sources, capacity * folds, lanes)
-    returned = lax.all_to_all(back, ("req", "z", "x"), 0, 0, tiled=True)
+    half_out = jnp.dot(inner, my_down, preferred_element_type=jnp.float32).astype(jnp.bfloat16)
+    half_out = half_out.reshape(2, sources, split * folds, lanes)
+    theirs = lax.ppermute(half_out[1], "c", [(0, 1), (1, 0)])
+    both = (half_out[0].astype(jnp.float32) + theirs.astype(jnp.float32)).astype(jnp.bfloat16)
+    returned = lax.all_to_all(both, ("y", "c", "z", "x"), 0, 0, tiled=True)
     slot_ids = jnp.arange(EXPERTS * capacity, dtype=jnp.int32)
     route_slots = positions.reshape(tok_local, TOP)
     mixing = jnp.sum(
         jnp.where(route_slots[:, :, None] == slot_ids[None, None, :], gate_weights[:, :, None], 0.0),
         axis=1,
     )
-    mixing = jnp.broadcast_to(mixing.reshape(tok_local, EXPERTS, 1, capacity), (tok_local, EXPERTS, 2, capacity))
-    mixing = mixing.reshape(tok_local, EXPERTS * 2 * capacity)
-    both = returned.reshape(EXPERTS * 2 * capacity, folds, lanes).astype(jnp.float32)
+    mixing = mixing[:, slot_of]
+    summed = returned.reshape(devices * split, folds, lanes).astype(jnp.float32)
     expert_out = jnp.einsum(
-        "ts,skd->tkd", mixing, both, precision=lax.Precision.HIGHEST,
+        "ts,skd->tkd", mixing, summed, precision=lax.Precision.HIGHEST,
         preferred_element_type=jnp.float32,
     )
     expert_out = expert_out.astype(jnp.bfloat16).reshape(tok_local, model_width)
@@ -158,18 +179,19 @@
     req_size, exp_size = mesh.devices.shape
     x_size = 4 if exp_size % 4 == 0 else 1
     sub_mesh = Mesh(
-        mesh.devices.reshape(req_size, exp_size // x_size, x_size), ("req", "z", "x")
+        mesh.devices.reshape(req_size // 2, 2, exp_size // x_size, x_size), ("y", "c", "z", "x")
     )
     exp = ("z", "x")
-    flat = ("req", "z", "x")
+    req = ("y", "c")
+    flat = ("y", "c", "z", "x")
     return jax.shard_map(
         layer,
         mesh=sub_mesh,
         in_specs=(
-            P("req", None, exp),
-            P("req", None, None, exp),
-            P("req", None, None, exp),
-            P("req"),
+            P(req, None, exp),
+            P(req, None, None, exp),
+            P(req, None, None, exp),
+            P(req),
             P(exp, None),
             P(flat, None),
             P(),

time: 234 us -> 245 us (1.047)
  the two profiles are of different devices: /device:TPU:37 before, /device:TPU:1 now
where the time goes in v12:
time: 245 us; the launch traced here: 242 us
  waiting for transfers between devices  130 us (53%)
  starting transfers between devices  36.5 us (15%)
  local copies, waits for them, and re-layouts  29.6 us (12%)
  matrix products  18 us (7%)
  other arithmetic  13.9 us (6%)
  Pallas kernels  12.5 us (5%)
    ppermute x1, waiting for transfers between devices, layer(): my_in = lax.ppermute(expert_in, ('c', 'x'), swap_pairs)  36 us
    all_to_all x1, waiting for transfers between devices, layer(): returned = lax.all_to_all(both, ('y', 'c', 'z', 'x'), 0, 0, tiled=True)  32.5 us
    all_to_all x1, waiting for transfers between devices, layer(): arrived = lax.all_to_all(outgoing, ('y', 'c', 'z', 'x'), 0, 0, tiled=True)  31.9 us
    ppermute x1, waiting for transfers between devices, layer(): my_down = lax.ppermute(expert_down, ('c', 'x'), swap_pairs)  13.6 us
    pallas_call x1, Pallas kernels, attention_kernel(): pl.pallas_call(_attn_kernel, grid_spec=grid_spec, out_shape=jax.ShapeDtyp...  12.5 us
    dot_general x1, matrix products, layer(): jnp.dot(inner, my_down, preferred_element_type=jnp.float32)  10.3 us
    all_to_all x1, starting transfers between devices, layer(): returned = lax.all_to_all(both, ('y', 'c', 'z', 'x'), 0, 0, tiled=True)  9.43 us
    all_to_all x1, waiting for transfers between devices, layer(): partial = lax.all_to_all(partial, 'z', 0, 0, tiled=True)  8.22 us
  transfers between devices with their start and end apart: 11, of which 6 were waited for; matrix products, arithmetic and copies ran while one was open for 11% of the time, Pallas kernels for 5%

profile of v12, /device:TPU:1, one launch (start us, length us, event | category | flops | bytes accessed | tf_op | source)
XLA Modules:
  0.0 241.8 jit_solution(13463944684173659860)
XLA Ops:
  0.6 3.4 %collective-permute-start.2 = (bf16[128,2048]{1,0:T(8,128)(2,1)}, bf16[128,2048]{1,0:T(8,128)(2,1)S(1)}, u32[]{:S(2)}, u32[]{:S(2)}) collective-permute-start(bf16[128,2048]{1,0:T(8,128)(2,1)} %param.16), channel_id=1, source_target_pairs={{0,3},{1,0},{2,1},{3,2},{4,7},{5,4},{6,5},{7,6},{8,11},{9,8},{10,9... | collective-permute-start | bytes 1572872 | tf_op jit(solution)/shard_map/ppermute | solution.py:101
  5.1 12.5 %shard_map.131 = bf16[2,512,128]{2,1,0:T(8,128)(2,1)} custom-call(s32[2]{0:T(128)} %len_ref.1, bf16[2,512,128]{2,1,0:T(8,128)(2,1)} %q_ref.1, bf16[2,2,4096,128]{3,2,1,0:T(8,128)(2,1)} %cv_ref.1, bf16[2,2,4096,128]{3,2,1,0:T(8,128)(2,1)} %cv_ref.1, bf16[2,2,512,128]{3,2,1,0:T(8,128)(2,1)} %nv_ref.1, bf16[2,2,512,128]{3,2,1,0:T(8,128)(2,1)} %nv_ref.1), custom_call_target="tpu_custom_call" | custom-call | tf_op jit(solution)/shard_map/pallas_call | solution.py:58
  19.3 3.4 %all-to-all-start = ((bf16[4,4,64,128]{3,2,1,0:T(8,128)(2,1)}), bf16[4,4,64,128]{3,2,1,0:T(8,128)(2,1)S(1)}, u32[]{:S(2)}, u32[]{:S(2)}) async-start(bf16[4,4,64,128]{3,2,1,0:T(8,128)(2,1)} %bitcast.62), calls=%async_computation | async-start | bytes 524288 | tf_op jit(solution)/shard_map/all_to_all | solution.py:106
  24.8 8.1 %all-to-all-done = bf16[4,4,64,128]{3,2,1,0:T(8,128)(2,1)S(1)} async-done(((bf16[4,4,64,128]{3,2,1,0:T(8,128)(2,1)}), bf16[4,4,64,128]{3,2,1,0:T(8,128)(2,1)S(1)}, u32[]{:S(2)}, u32[]{:S(2)}) %all-to-all-start) | async-done | bytes 262176 | tf_op jit(solution)/shard_map/all_to_all | solution.py:106
  35.7 5.0 %all-to-all-start.1 = ((bf16[4,64,2048]{2,1,0:T(8,128)(2,1)}), bf16[4,64,2048]{2,1,0:T(8,128)(2,1)S(1)}, u32[]{:S(2)}, u32[]{:S(2)}) async-start(bf16[4,64,2048]{2,1,0:T(8,128)(2,1)} %bitcast.9), calls=%async_computation.1 | async-start | bytes 2097152 | tf_op jit(solution)/shard_map/all_to_all | solution.py:114
  40.9 2.4 %scatter_custom_fusion = s32[640]{0:T(1024)S(1)} fusion(s32[512]{0:T(512)S(1)} %bitcast.80, s32[512]{0:T(512)S(1)} %add_select_fusion, s32[]{:T(128)} %constant.64.clone.1), kind=kCustom, calls=%fused_computation.60 | custom fusion | bytes 2564 | tf_op jit(solution)/shard_map/scatter | solution.py:132
  43.4 2.8 %gather_fusion.2 = s32[640]{0:T(1024)S(1)} fusion(s32[640]{0:T(1024)S(1)} %scatter_custom_fusion, s32[1024]{0:T(1024)S(1)} %pad_clamp_fusion.1), kind=kCustom, calls=%fused_computation.2 | custom fusion | bytes 7680 | tf_op jit(solution)/shard_map/gather | solution.py:147
  46.2 8.2 %all-to-all-done.1 = bf16[4,64,2048]{2,1,0:T(8,128)(2,1)S(1)} async-done(((bf16[4,64,2048]{2,1,0:T(8,128)(2,1)}), bf16[4,64,2048]{2,1,0:T(8,128)(2,1)S(1)}, u32[]{:S(2)}, u32[]{:S(2)}) %all-to-all-start.1) | async-done | bytes 1048608 | tf_op jit(solution)/shard_map/all_to_all | solution.py:114
  55.7 3.3 %gather_fusion.3 = bf16[640,16,128]{2,1,0:T(8,128)(2,1)} fusion(bf16[65,16,128]{2,1,0:T(8,128)(2,1)S(1)} %concatenate.6, s32[1024]{0:T(1024)S(1)} %pad_clamp_fusion), kind=kCustom, calls=%fused_computation.3 | custom fusion | bytes 5245440 | tf_op jit(solution)/shard_map/gather | solution.py:147
  59.0 7.3 %all-to-all-start.2 = ((bf16[128,80,128]{2,1,0:T(8,128)(2,1)}), bf16[128,80,128]{2,1,0:T(8,128)(2,1)S(1)}, u32[]{:S(2)}, u32[]{:S(2)}) async-start(bf16[128,80,128]{2,1,0:T(8,128)(2,1)} %bitcast.64), calls=%async_computation.2 | async-start | bytes 5242880 | tf_op jit(solution)/shard_map/all_to_all | solution.py:149
  66.3 3.5 %collective-permute-start.4 = (bf16[2,2048,512]{2,1,0:T(8,128)(2,1)}, bf16[2,2048,512]{2,1,0:T(8,128)(2,1)}, u32[]{:S(2)}, u32[]{:S(2)}) collective-permute-start(bf16[2,2048,512]{2,1,0:T(8,128)(2,1)} %param.21), channel_id=1, source_target_pairs={{0,0},{1,16},{2,2},{3,18},{16,1},{17,17},{18,3},{19,19},{4,4},{5,2... | collective-permute-start | bytes 12582920 | tf_op jit(solution)/shard_map/ppermute | solution.py:95
  69.8 31.9 %all-to-all-done.2 = bf16[128,80,128]{2,1,0:T(8,128)(2,1)S(1)} async-done(((bf16[128,80,128]{2,1,0:T(8,128)(2,1)}), bf16[128,80,128]{2,1,0:T(8,128)(2,1)S(1)}, u32[]{:S(2)}, u32[]{:S(2)}) %all-to-all-start.2) | async-done | bytes 2621472 | tf_op jit(solution)/shard_map/all_to_all | solution.py:149
  102.4 2.7 %collective-permute-start.5 = (bf16[512,2048]{1,0:T(8,128)(2,1)}, bf16[512,2048]{1,0:T(8,128)(2,1)S(1)}, u32[]{:S(2)}, u32[]{:S(2)}) collective-permute-start(bf16[512,2048]{1,0:T(8,128)(2,1)} %param.22), channel_id=1, source_target_pairs={{0,0},{1,16},{2,2},{3,18},{16,1},{17,17},{18,3},{19,19},{4,4},{5,2... | collective-permute-start | bytes 6291464 | tf_op jit(solution)/shard_map/ppermute | solution.py:96
  105.1 36.0 %collective-permute-done.4 = bf16[2,2048,512]{2,1,0:T(8,128)(2,1)} collective-permute-done((bf16[2,2048,512]{2,1,0:T(8,128)(2,1)}, bf16[2,2048,512]{2,1,0:T(8,128)(2,1)}, u32[]{:S(2)}, u32[]{:S(2)}) %collective-permute-start.4) | collective-permute-done | bytes 4194336 | tf_op jit(solution)/shard_map/ppermute | solution.py:95
  141.1 3.9 %fusion.42 = (bf16[1,2048,512]{2,1,0:T(8,128)(2,1)}, bf16[1,2048,512]{2,1,0:T(8,128)(2,1)S(1)}) fusion(bf16[2,2048,512]{2,1,0:T(8,128)(2,1)} %collective-permute-done.4), kind=kLoop, calls=%fused_computation.71 | loop fusion | bytes 8388608 | tf_op jit(solution)/shard_map/slice | solution.py:155
  145.4 4.4 %fusion.4 = f32[1280,512]{1,0:T(8,128)} fusion(bf16[16,128,512]{2,1,0:T(8,128)(2,1)S(1)} %bitcast.69, bf16[1280,16,128]{2,1,0:T(8,128)(2,1)S(1)} %bitcast.66), kind=kOutput, calls=%fused_computation.12 | convolution fusion | flops 2684354560 | bytes 9961472 | tf_op jit(solution)/shard_map/tkd,kdf->tf/dot_general | solution.py:154
  149.8 13.6 %collective-permute-done.5 = bf16[512,2048]{1,0:T(8,128)(2,1)S(1)} collective-permute-done((bf16[512,2048]{1,0:T(8,128)(2,1)}, bf16[512,2048]{1,0:T(8,128)(2,1)S(1)}, u32[]{:S(2)}, u32[]{:S(2)}) %collective-permute-start.5) | collective-permute-done | bytes 2097184 | tf_op jit(solution)/shard_map/ppermute | solution.py:96
  164.7 10.3 %convolution_convert_fusion = bf16[1280,2048]{1,0:T(8,128)(2,1)} fusion(bf16[512,2048]{1,0:T(8,128)(2,1)} %copy-done.8, f32[1280,512]{1,0:T(8,128)} %fusion.4, bf16[16,128,512]{2,1,0:T(8,128)(2,1)S(1)} %bitcast.68, bf16[1280,16,128]{2,1,0:T(8,128)(2,1)} %bitcast.67), kind=kOutput, calls=%fused_computation.5 | convolution fusion | flops 5375262720 | bytes 17301504 | tf_op jit(solution)/shard_map/dot_general | solution.py:157
  175.1 5.6 %fusion.41 = (bf16[640,2048]{1,0:T(8,128)(2,1)S(1)}, f32[640,2048]{1,0:T(8,128)}) fusion(bf16[1280,2048]{1,0:T(8,128)(2,1)} %convolution_convert_fusion), kind=kLoop, calls=%fused_computation.70 | loop fusion | flops 1310720 | bytes 13107200 | tf_op jit(solution)/shard_map/slice | solution.py:159
  180.7 3.2 %squeeze.12 = bf16[128,80,128]{2,1,0:T(8,128)(2,1)} reshape(bf16[640,2048]{1,0:T(8,128)(2,1)S(1)} %get-tuple-element.2) | data formatting | bytes 5242880 | tf_op jit(solution)/shard_map/squeeze | solution.py:159
  183.9 6.7 %reshape.181 = f32[128,80,128]{2,1,0:T(8,128)} reshape(f32[640,2048]{1,0:T(8,128)} %get-tuple-element.3) | data formatting | bytes 10485760 | tf_op jit(solution)/shard_map/convert_element_type | solution.py:160
  190.6 4.5 %add_convert_fusion = bf16[128,80,128]{2,1,0:T(8,128)(2,1)} fusion(f32[128,80,128]{2,1,0:T(8,128)} %reshape.181, bf16[128,80,128]{2,1,0:T(8,128)(2,1)S(1)} %collective-permute-done.6), kind=kLoop, calls=%fused_computation.7 | loop fusion | flops 3932160 | bytes 10485760 | tf_op jit(solution)/shard_map/convert_element_type | solution.py:160
  195.1 9.4 %all-to-all-start.3 = ((bf16[128,80,128]{2,1,0:T(8,128)(2,1)}), bf16[128,80,128]{2,1,0:T(8,128)(2,1)S(1)}, u32[]{:S(2)}, u32[]{:S(2)}) async-start(bf16[128,80,128]{2,1,0:T(8,128)(2,1)} %add_convert_fusion), calls=%async_computation.3 | async-start | bytes 5242880 | tf_op jit(solution)/shard_map/all_to_all | solution.py:161
  206.9 32.5 %all-to-all-done.3 = bf16[128,80,128]{2,1,0:T(8,128)(2,1)S(1)} async-done(((bf16[128,80,128]{2,1,0:T(8,128)(2,1)}), bf16[128,80,128]{2,1,0:T(8,128)(2,1)S(1)}, u32[]{:S(2)}, u32[]{:S(2)}) %all-to-all-start.3) | async-done | bytes 2621472 | tf_op jit(solution)/shard_map/all_to_all | solution.py:161
  (65 shorter events, 16.1 us)
Async XLA Ops:
  0.6 22.1 %copy-start.5 = (s32[64,8]{0,1:T(8,128)S(1)}, s32[64,8]{0,1:T(8,128)}, u32[]{:S(2)}) copy-start(s32[64,8]{0,1:T(8,128)} %param.19) | copy-start | bytes 6148
  0.6 33.1 %collective-permute-start.2 = (bf16[128,2048]{1,0:T(8,128)(2,1)}, bf16[128,2048]{1,0:T(8,128)(2,1)S(1)}, u32[]{:S(2)}, u32[]{:S(2)}) collective-permute-start(bf16[128,2048]{1,0:T(8,128)(2,1)} %param.16), channel_id=1, source_target_pairs={{0,3},{1,0},{2,1},{3,2},{4,7},{5,4},{6,5},{7,6},{8,11},{9,8},{10,9... | collective-permute-start | bytes 1572872 | tf_op jit(solution)/shard_map/ppermute | solution.py:101
  4.0 29.7 %collective-permute-start.1 = (bf16[128,2048]{1,0:T(8,128)(2,1)}, bf16[128,2048]{1,0:T(8,128)(2,1)S(1)}, u32[]{:S(2)}, u32[]{:S(2)}) collective-permute-start(bf16[128,2048]{1,0:T(8,128)(2,1)} %param.16), channel_id=1, source_target_pairs={{0,2},{1,3},{2,0},{3,1},{4,6},{5,7},{6,4},{7,5},{8,10},{9,11},{10,... | collective-permute-start | bytes 1572872 | tf_op jit(solution)/shard_map/ppermute | solution.py:101
  4.5 29.2 %collective-permute-start = (bf16[128,2048]{1,0:T(8,128)(2,1)}, bf16[128,2048]{1,0:T(8,128)(2,1)S(1)}, u32[]{:S(2)}, u32[]{:S(2)}) collective-permute-start(bf16[128,2048]{1,0:T(8,128)(2,1)} %param.16), channel_id=1, source_target_pairs={{0,1},{1,2},{2,3},{3,0},{4,5},{5,6},{6,7},{7,4},{8,9},{9,10},{10,1... | collective-permute-start | bytes 1572872 | tf_op jit(solution)/shard_map/ppermute | solution.py:101
  17.6 16.2 %copy-start.3 = (bf16[128,2048]{1,0:T(8,128)(2,1)S(1)}, bf16[128,2048]{1,0:T(8,128)(2,1)}, u32[]{:S(2)}) copy-start(bf16[128,2048]{1,0:T(8,128)(2,1)} %param.16) | copy-start | bytes 1572868
  19.3 13.6 %all-to-all-start = ((bf16[4,4,64,128]{3,2,1,0:T(8,128)(2,1)}), bf16[4,4,64,128]{3,2,1,0:T(8,128)(2,1)S(1)}, u32[]{:S(2)}, u32[]{:S(2)}) async-start(bf16[4,4,64,128]{3,2,1,0:T(8,128)(2,1)} %bitcast.62), calls=%async_computation | async-start | bytes 524288 | tf_op jit(solution)/shard_map/all_to_all | solution.py:106
  34.0 9.3 %copy-start.7 = (s32[640]{0:T(1024)S(1)}, s32[640]{0:T(1024)}, u32[]{:S(2)}) copy-start(s32[640]{0:T(1024)} %constant.83) | copy-start | bytes 7684
  35.7 18.7 %all-to-all-start.1 = ((bf16[4,64,2048]{2,1,0:T(8,128)(2,1)}), bf16[4,64,2048]{2,1,0:T(8,128)(2,1)S(1)}, u32[]{:S(2)}, u32[]{:S(2)}) async-start(bf16[4,64,2048]{2,1,0:T(8,128)(2,1)} %bitcast.9), calls=%async_computation.1 | async-start | bytes 2097152 | tf_op jit(solution)/shard_map/all_to_all | solution.py:114
  43.4 11.2 %copy-start.2 = (bf16[64,2048]{1,0:T(8,128)(2,1)S(1)}, bf16[64,2048]{1,0:T(8,128)(2,1)}, u32[]{:S(2)}) copy-start(bf16[64,2048]{1,0:T(8,128)(2,1)} %param.17) | copy-start | bytes 786436
  43.4 11.4 %copy-start.4 = (f32[2048]{0:T(1024)S(1)}, f32[2048]{0:T(1024)}, u32[]{:S(2)}) copy-start(f32[2048]{0:T(1024)} %param.18) | copy-start | bytes 24580
  59.0 42.7 %all-to-all-start.2 = ((bf16[128,80,128]{2,1,0:T(8,128)(2,1)}), bf16[128,80,128]{2,1,0:T(8,128)(2,1)S(1)}, u32[]{:S(2)}, u32[]{:S(2)}) async-start(bf16[128,80,128]{2,1,0:T(8,128)(2,1)} %bitcast.64), calls=%async_computation.2 | async-start | bytes 5242880 | tf_op jit(solution)/shard_map/all_to_all | solution.py:149
  66.3 74.8 %collective-permute-start.4 = (bf16[2,2048,512]{2,1,0:T(8,128)(2,1)}, bf16[2,2048,512]{2,1,0:T(8,128)(2,1)}, u32[]{:S(2)}, u32[]{:S(2)}) collective-permute-start(bf16[2,2048,512]{2,1,0:T(8,128)(2,1)} %param.21), channel_id=1, source_target_pairs={{0,0},{1,16},{2,2},{3,18},{16,1},{17,17},{18,3},{19,19},{4,4},{5,2... | collective-permute-start | bytes 12582920 | tf_op jit(solution)/shard_map/ppermute | solution.py:95
  101.7 43.2 %collective-permute-start.3 = (bf16[128,80,128]{2,1,0:T(8,128)(2,1)S(1)}, bf16[128,80,128]{2,1,0:T(8,128)(2,1)S(1)}, u32[]{:S(2)}, u32[]{:S(2)}) collective-permute-start(bf16[128,80,128]{2,1,0:T(8,128)(2,1)S(1)} %all-to-all-done.2), channel_id=1, source_target_pairs={{0,16},{16,0},{1,17},{17,1},{2,18},{18,2},{3,19},{19,3},{4,20},{20... | collective-permute-start | bytes 7864328 | tf_op jit(solution)/shard_map/ppermute | solution.py:150
  102.4 61.0 %collective-permute-start.5 = (bf16[512,2048]{1,0:T(8,128)(2,1)}, bf16[512,2048]{1,0:T(8,128)(2,1)S(1)}, u32[]{:S(2)}, u32[]{:S(2)}) collective-permute-start(bf16[512,2048]{1,0:T(8,128)(2,1)} %param.22), channel_id=1, source_target_pairs={{0,0},{1,16},{2,2},{3,18},{16,1},{17,17},{18,3},{19,19},{4,4},{5,2... | collective-permute-start | bytes 6291464 | tf_op jit(solution)/shard_map/ppermute | solution.py:96
  145.4 4.4 %copy-start = (bf16[256,80,128]{2,1,0:T(8,128)(2,1)}, bf16[256,80,128]{2,1,0:T(8,128)(2,1)S(1)}, u32[]{:S(2)}) copy-start(bf16[256,80,128]{2,1,0:T(8,128)(2,1)S(1)} %pad_maximum_fusion) | copy-start | bytes 15728644
  145.4 19.4 %copy-start.1 = (bf16[1,2048,512]{2,1,0:T(8,128)(2,1)S(1)}, bf16[1,2048,512]{2,1,0:T(8,128)(2,1)}, u32[]{:S(2)}) copy-start(bf16[1,2048,512]{2,1,0:T(8,128)(2,1)} %get-tuple-element.4) | copy-start | bytes 6291460
  163.4 1.3 copy-start.8
  183.8 6.7 %collective-permute-start.6 = (bf16[128,80,128]{2,1,0:T(8,128)(2,1)}, bf16[128,80,128]{2,1,0:T(8,128)(2,1)S(1)}, u32[]{:S(2)}, u32[]{:S(2)}) collective-permute-start(bf16[128,80,128]{2,1,0:T(8,128)(2,1)} %squeeze.12), channel_id=1, source_target_pairs={{0,16},{16,0},{1,17},{17,1},{2,18},{18,2},{3,19},{19,3},{4,20},{20... | collective-permute-start | bytes 7864328 | tf_op jit(solution)/shard_map/ppermute | solution.py:159
  195.1 9.4 %copy-start.6 = (f32[64,8]{0,1:T(8,128)S(1)}, f32[64,8]{0,1:T(8,128)}, u32[]{:S(2)}) copy-start(f32[64,8]{0,1:T(8,128)} %param.20) | copy-start | bytes 6148
  195.1 44.4 %all-to-all-start.3 = ((bf16[128,80,128]{2,1,0:T(8,128)(2,1)}), bf16[128,80,128]{2,1,0:T(8,128)(2,1)S(1)}, u32[]{:S(2)}, u32[]{:S(2)}) async-start(bf16[128,80,128]{2,1,0:T(8,128)(2,1)} %add_convert_fusion), calls=%async_computation.3 | async-start | bytes 5242880 | tf_op jit(solution)/shard_map/all_to_all | solution.py:161

commit v13 on v11

--- a/solution.py
+++ b/solution.py
@@ -130,9 +130,11 @@
     arrived = lax.all_to_all(outgoing, ("req", "z", "x"), 0, 0, tiled=True)
     sources = arrived.shape[0]
     rows = arrived.reshape(sources * capacity, folds, lanes)
-    w_in = expert_in[:, :, 0:half_units].reshape(2, folds, lanes, half_units)
-    gate_part = jnp.einsum("tkd,kdf->tf", rows, w_in[0], preferred_element_type=jnp.float32)
-    up_part = jnp.einsum("tkd,kdf->tf", rows, w_in[1], preferred_element_type=jnp.float32)
+    w_in = jnp.concatenate([expert_in[0, :, 0:half_units], expert_in[1, :, 0:half_units]], axis=1)
+    w_in = w_in.reshape(folds, lanes, 2 * half_units)
+    both_parts = jnp.einsum("tkd,kdf->tf", rows, w_in, preferred_element_type=jnp.float32)
+    gate_part = both_parts[:, :half_units]
+    up_part = both_parts[:, half_units:]
     inner = (jax.nn.silu(gate_part) * up_part).astype(jnp.bfloat16)
     half_out = jnp.dot(inner, expert_down, preferred_element_type=jnp.float32).astype(jnp.bfloat16)
     back = half_out.reshape(sources, capacity * folds, lanes)
@@ -145,11 +147,12 @@
     )
     mixing = jnp.broadcast_to(mixing.reshape(tok_local, EXPERTS, 1, capacity), (tok_local, EXPERTS, 2, capacity))
     mixing = mixing.reshape(tok_local, EXPERTS * 2 * capacity)
-    both = returned.reshape(EXPERTS * 2 * capacity, folds, lanes).astype(jnp.float32)
+    both = returned.reshape(EXPERTS * 2 * capacity, folds, lanes)
+    mixing_hi = mixing.astype(jnp.bfloat16)
+    mixing_lo = (mixing - mixing_hi.astype(jnp.float32)).astype(jnp.bfloat16)
     expert_out = jnp.einsum(
-        "ts,skd->tkd", mixing, both, precision=lax.Precision.HIGHEST,
-        preferred_element_type=jnp.float32,
-    )
+        "ts,skd->tkd", mixing_hi, both, preferred_element_type=jnp.float32
+    ) + jnp.einsum("ts,skd->tkd", mixing_lo, both, preferred_element_type=jnp.float32)
     expert_out = expert_out.astype(jnp.bfloat16).reshape(tok_local, model_width)
     return (attended, expert_out)
 

time: 234 us -> 231 us (0.987)
  matrix products: 24.4 us -> 21.7 us
    dot_general x1, matrix products: 10.4 us -> 4.69 us  [layer(): jnp.dot(inner, expert_down, preferred_element_type=jnp.float32)]
    dot_general x2 -> x3, matrix products: 12.3 us -> 15.3 us  [the longest x1 8.19 us: layer(): jnp.einsum('tkd,kdf->tf', rows, w_in, preferred_element_type=jnp.float32)]
  transfers between devices with their start and end apart: 7 -> 7, of which waited for: 4 -> 4; matrix products, arithmetic and copies ran while one was open for 7% -> 6% of each run, Pallas kernels for 5% -> 5%
where the time goes in v13:
time: 231 us; the launch traced here: 228 us
  waiting for transfers between devices  131 us (57%)
  starting transfers between devices  30.7 us (13%)
  local copies, waits for them, and re-layouts  26.1 us (11%)
  matrix products  21.7 us (9%)
  Pallas kernels  12.4 us (5%)
  other arithmetic  4.71 us (2%)
    all_to_all x1, waiting for transfers between devices, layer(): returned = lax.all_to_all(back, ('req', 'z', 'x'), 0, 0, tiled=True)  59.6 us
    all_to_all x1, waiting for transfers between devices, layer(): arrived = lax.all_to_all(outgoing, ('req', 'z', 'x'), 0, 0, tiled=True)  56.4 us
    pallas_call x1, Pallas kernels, attention_kernel(): pl.pallas_call(_attn_kernel, grid_spec=grid_spec, out_shape=jax.ShapeDtyp...  12.4 us
    all_to_all x1, starting transfers between devices, layer(): arrived = lax.all_to_all(outgoing, ('req', 'z', 'x'), 0, 0, tiled=True)  11.1 us
    all_to_all x1, waiting for transfers between devices, layer(): partial = lax.all_to_all(partial, 'z', 0, 0, tiled=True)  9.56 us
    reshape x1, local copies, waits for them, and re-layouts, layer(): back = half_out.reshape(sources, capacity * folds, lanes)  8.93 us
    dot_general x1, matrix products, layer(): jnp.einsum('tkd,kdf->tf', rows, w_in, preferred_element_type=jnp.float32)  8.19 us
    all_to_all x1, starting transfers between devices, layer(): returned = lax.all_to_all(back, ('req', 'z', 'x'), 0, 0, tiled=True)  7.37 us
  transfers between devices with their start and end apart: 7, of which 4 were waited for; matrix products, arithmetic and copies ran while one was open for 6% of the time, Pallas kernels for 5%

profile of v13, /device:TPU:37, one launch (start us, length us, event | category | flops | bytes accessed | tf_op | source)
XLA Modules:
  0.0 228.0 jit_solution(11028553233725279165)
XLA Ops:
  1.0 2.5 %collective-permute-start.1 = (bf16[128,2048]{1,0:T(8,128)(2,1)}, bf16[128,2048]{1,0:T(8,128)(2,1)}, u32[]{:S(2)}, u32[]{:S(2)}) collective-permute-start(bf16[128,2048]{1,0:T(8,128)(2,1)} %param.15), channel_id=1, source_target_pairs={{0,2},{1,3},{2,0},{3,1},{4,6},{5,7},{6,4},{7,5},{8,10},{9,11},{10,... | collective-permute-start | bytes 1572872 | tf_op jit(solution)/shard_map/ppermute | solution.py:91
  3.4 12.4 %shard_map.122 = bf16[2,512,128]{2,1,0:T(8,128)(2,1)} custom-call(s32[2]{0:T(128)} %len_ref.1, bf16[2,512,128]{2,1,0:T(8,128)(2,1)} %q_ref.1, bf16[2,2,4096,128]{3,2,1,0:T(8,128)(2,1)} %cv_ref.1, bf16[2,2,4096,128]{3,2,1,0:T(8,128)(2,1)} %cv_ref.1, bf16[2,2,512,128]{3,2,1,0:T(8,128)(2,1)} %nv_ref.1, bf16[2,2,512,128]{3,2,1,0:T(8,128)(2,1)} %nv_ref.1), custom_call_target="tpu_custom_call" | custom-call | tf_op jit(solution)/shard_map/pallas_call | solution.py:57
  15.9 1.7 copy.83
  17.6 4.5 %all-to-all-start = ((bf16[4,4,64,128]{3,2,1,0:T(8,128)(2,1)}), bf16[4,4,64,128]{3,2,1,0:T(8,128)(2,1)S(1)}, u32[]{:S(2)}, u32[]{:S(2)}) async-start(bf16[4,4,64,128]{3,2,1,0:T(8,128)(2,1)} %bitcast.63), calls=%async_computation | async-start | bytes 524288 | tf_op jit(solution)/shard_map/all_to_all | solution.py:96
  22.4 1.2 reduce-window.6
  24.2 5.7 %all-to-all-done = bf16[4,4,64,128]{3,2,1,0:T(8,128)(2,1)S(1)} async-done(((bf16[4,4,64,128]{3,2,1,0:T(8,128)(2,1)}), bf16[4,4,64,128]{3,2,1,0:T(8,128)(2,1)S(1)}, u32[]{:S(2)}, u32[]{:S(2)}) %all-to-all-start) | async-done | bytes 262176 | tf_op jit(solution)/shard_map/all_to_all | solution.py:96
  30.7 1.6 pad_maximum_fusion
  32.4 1.7 convolution_convert_fusion.1
  34.1 5.0 %all-to-all-start.1 = ((bf16[4,64,2048]{2,1,0:T(8,128)(2,1)}), bf16[4,64,2048]{2,1,0:T(8,128)(2,1)S(1)}, u32[]{:S(2)}, u32[]{:S(2)}) async-start(bf16[4,64,2048]{2,1,0:T(8,128)(2,1)} %bitcast.66), calls=%async_computation.1 | async-start | bytes 2097152 | tf_op jit(solution)/shard_map/all_to_all | solution.py:104
  39.2 2.4 %scatter_custom_fusion = s32[640]{0:T(1024)S(1)} fusion(s32[512]{0:T(512)S(1)} %bitcast.76, s32[512]{0:T(512)S(1)} %add_select_fusion, s32[]{:T(128)} %constant.60.clone.1), kind=kCustom, calls=%fused_computation.60 | custom fusion | bytes 2564 | tf_op jit(solution)/shard_map/scatter | solution.py:123
  42.0 9.6 %all-to-all-done.1 = bf16[4,64,2048]{2,1,0:T(8,128)(2,1)S(1)} async-done(((bf16[4,64,2048]{2,1,0:T(8,128)(2,1)}), bf16[4,64,2048]{2,1,0:T(8,128)(2,1)S(1)}, u32[]{:S(2)}, u32[]{:S(2)}) %all-to-all-start.1) | async-done | bytes 1048608 | tf_op jit(solution)/shard_map/all_to_all | solution.py:104
  51.9 0.8 fusion.26
  52.8 5.0 %gather_fusion.1 = bf16[1280,16,128]{2,1,0:T(8,128)(2,1)} fusion(bf16[65,16,128]{2,1,0:T(8,128)(2,1)S(1)} %concatenate.11, s32[2048]{0:T(1024)S(1)} %pad_clamp_fusion), kind=kCustom, calls=%fused_computation.1 | custom fusion | bytes 10490880 | tf_op jit(solution)/shard_map/gather | solution.py:128
  57.8 11.1 %all-to-all-start.2 = ((bf16[128,160,128]{2,1,0:T(8,128)(2,1)}), bf16[128,160,128]{2,1,0:T(8,128)(2,1)}, u32[]{:S(2)}, u32[]{:S(2)}) async-start(bf16[128,160,128]{2,1,0:T(8,128)(2,1)} %bitcast.64), calls=%async_computation.2 | async-start | bytes 10485760 | tf_op jit(solution)/shard_map/all_to_all | solution.py:130
  68.9 4.6 %fusion.44 = (bf16[1,2048,512]{2,1,0:T(8,128)(2,1)}, bf16[1,2048,512]{2,1,0:T(8,128)(2,1)}) fusion(bf16[2,2048,512]{2,1,0:T(8,128)(2,1)} %param.20), kind=kLoop, calls=%fused_computation.71 | loop fusion | bytes 8388608 | tf_op jit(solution)/shard_map/slice | solution.py:133
  73.4 56.4 %all-to-all-done.2 = bf16[128,160,128]{2,1,0:T(8,128)(2,1)} async-done(((bf16[128,160,128]{2,1,0:T(8,128)(2,1)}), bf16[128,160,128]{2,1,0:T(8,128)(2,1)}, u32[]{:S(2)}, u32[]{:S(2)}) %all-to-all-start.2) | async-done | bytes 5242912 | tf_op jit(solution)/shard_map/all_to_all | solution.py:130
  129.9 8.2 %fusion.6 = f32[1280,1024]{1,0:T(8,128)S(1)} fusion(bf16[1280,16,128]{2,1,0:T(8,128)(2,1)} %bitcast.15, bf16[16,128,512]{2,1,0:T(8,128)(2,1)} %bitcast.68, bf16[16,128,512]{2,1,0:T(8,128)(2,1)} %bitcast.67), kind=kOutput, calls=%fused_computation.10 | convolution fusion | flops 5377097728 | bytes 14680064 | tf_op jit(solution)/shard_map/tkd,kdf->tf/dot_general | solution.py:135
  138.1 4.7 %convolution_convert_fusion = bf16[1280,2048]{1,0:T(8,128)(2,1)} fusion(bf16[512,2048]{1,0:T(8,128)(2,1)S(1)} %copy-done, f32[1280,1024]{1,0:T(8,128)S(1)} %fusion.6), kind=kOutput, calls=%fused_computation.3 | convolution fusion | flops 2690908160 | bytes 12582912 | tf_op jit(solution)/shard_map/dot_general | solution.py:139
  142.8 8.9 %reshape.201 = bf16[128,160,128]{2,1,0:T(8,128)(2,1)} reshape(bf16[1280,2048]{1,0:T(8,128)(2,1)} %convolution_convert_fusion) | data formatting | bytes 10485760 | tf_op jit(solution)/shard_map/reshape | solution.py:140
  151.7 7.4 %all-to-all-start.3 = ((bf16[128,160,128]{2,1,0:T(8,128)(2,1)}), bf16[128,160,128]{2,1,0:T(8,128)(2,1)}, u32[]{:S(2)}, u32[]{:S(2)}) async-start(bf16[128,160,128]{2,1,0:T(8,128)(2,1)} %reshape.201), calls=%async_computation.3 | async-start | bytes 10485760 | tf_op jit(solution)/shard_map/all_to_all | solution.py:141
  160.5 59.6 %all-to-all-done.3 = bf16[128,160,128]{2,1,0:T(8,128)(2,1)} async-done(((bf16[128,160,128]{2,1,0:T(8,128)(2,1)}), bf16[128,160,128]{2,1,0:T(8,128)(2,1)}, u32[]{:S(2)}, u32[]{:S(2)}) %all-to-all-start.3) | async-done | bytes 5242912 | tf_op jit(solution)/shard_map/all_to_all | solution.py:141
  220.1 3.6 %fusion.2 = f32[64,16,128]{2,0,1:T(8,128)S(1)} fusion(bf16[1280,16,128]{2,1,0:T(8,128)(2,1)} %bitcast.19, bf16[64,1280]{0,1:T(8,128)(2,1)S(1)} %convert_element_type.62), kind=kOutput, calls=%fused_computation.6 | convolution fusion | flops 335544320 | bytes 5931008 | tf_op jit(solution)/shard_map/ts,skd->tkd/dot_general | solution.py:155
  223.7 3.6 %fusion.21 = bf16[16,8,8,128]{3,2,1,0:T(8,128)(2,1)S(1)} fusion(f32[64,16,128]{2,0,1:T(8,128)S(1)} %fusion.2, bf16[1280,16,128]{2,1,0:T(8,128)(2,1)} %bitcast.19, bf16[64,1280]{0,1:T(8,128)(2,1)S(1)} %convert_element_type.56), kind=kOutput, calls=%fused_computation.24 | convolution fusion | flops 335806464 | bytes 6193152 | tf_op jit(solution)/shard_map/ts,skd->tkd/dot_general | solution.py:153
  227.2 0.8 copy.82
  (54 shorter events, 4.1 us)
Async XLA Ops:
  0.6 137.4 %copy-start = (bf16[512,2048]{1,0:T(8,128)(2,1)S(1)}, bf16[512,2048]{1,0:T(8,128)(2,1)}, u32[]{:S(2)}) copy-start(bf16[512,2048]{1,0:T(8,128)(2,1)} %param.21) | copy-start | bytes 6291460
  0.6 21.5 %copy-start.4 = (s32[64,8]{0,1:T(8,128)S(1)}, s32[64,8]{0,1:T(8,128)}, u32[]{:S(2)}) copy-start(s32[64,8]{0,1:T(8,128)} %param.18) | copy-start | bytes 6148
  0.7 30.0 %collective-permute-start.2 = (bf16[128,2048]{1,0:T(8,128)(2,1)}, bf16[128,2048]{1,0:T(8,128)(2,1)}, u32[]{:S(2)}, u32[]{:S(2)}) collective-permute-start(bf16[128,2048]{1,0:T(8,128)(2,1)} %param.15), channel_id=1, source_target_pairs={{0,3},{1,0},{2,1},{3,2},{4,7},{5,4},{6,5},{7,6},{8,11},{9,8},{10,9... | collective-permute-start | bytes 1572872 | tf_op jit(solution)/shard_map/ppermute | solution.py:91
  1.0 29.7 %collective-permute-start.1 = (bf16[128,2048]{1,0:T(8,128)(2,1)}, bf16[128,2048]{1,0:T(8,128)(2,1)}, u32[]{:S(2)}, u32[]{:S(2)}) collective-permute-start(bf16[128,2048]{1,0:T(8,128)(2,1)} %param.15), channel_id=1, source_target_pairs={{0,2},{1,3},{2,0},{3,1},{4,6},{5,7},{6,4},{7,5},{8,10},{9,11},{10,... | collective-permute-start | bytes 1572872 | tf_op jit(solution)/shard_map/ppermute | solution.py:91
  3.4 27.3 %collective-permute-start = (bf16[128,2048]{1,0:T(8,128)(2,1)}, bf16[128,2048]{1,0:T(8,128)(2,1)}, u32[]{:S(2)}, u32[]{:S(2)}) collective-permute-start(bf16[128,2048]{1,0:T(8,128)(2,1)} %param.15), channel_id=1, source_target_pairs={{0,1},{1,2},{2,3},{3,0},{4,5},{5,6},{6,7},{7,4},{8,9},{9,10},{10,1... | collective-permute-start | bytes 1572872 | tf_op jit(solution)/shard_map/ppermute | solution.py:91
  15.9 14.9 %copy-start.2 = (bf16[128,2048]{1,0:T(8,128)(2,1)S(1)}, bf16[128,2048]{1,0:T(8,128)(2,1)}, u32[]{:S(2)}) copy-start(bf16[128,2048]{1,0:T(8,128)(2,1)} %param.15) | copy-start | bytes 1572868
  17.6 12.3 %all-to-all-start = ((bf16[4,4,64,128]{3,2,1,0:T(8,128)(2,1)}), bf16[4,4,64,128]{3,2,1,0:T(8,128)(2,1)S(1)}, u32[]{:S(2)}, u32[]{:S(2)}) async-start(bf16[4,4,64,128]{3,2,1,0:T(8,128)(2,1)} %bitcast.63), calls=%async_computation | async-start | bytes 524288 | tf_op jit(solution)/shard_map/all_to_all | solution.py:96
  34.1 17.6 %copy-start.1 = (bf16[64,2048]{1,0:T(8,128)(2,1)S(1)}, bf16[64,2048]{1,0:T(8,128)(2,1)}, u32[]{:S(2)}) copy-start(bf16[64,2048]{1,0:T(8,128)(2,1)} %param.16) | copy-start | bytes 786436
  34.1 17.8 %copy-start.3 = (f32[2048]{0:T(1024)S(1)}, f32[2048]{0:T(1024)}, u32[]{:S(2)}) copy-start(f32[2048]{0:T(1024)} %param.17) | copy-start | bytes 24580
  34.1 17.5 %all-to-all-start.1 = ((bf16[4,64,2048]{2,1,0:T(8,128)(2,1)}), bf16[4,64,2048]{2,1,0:T(8,128)(2,1)S(1)}, u32[]{:S(2)}, u32[]{:S(2)}) async-start(bf16[4,64,2048]{2,1,0:T(8,128)(2,1)} %bitcast.66), calls=%async_computation.1 | async-start | bytes 2097152 | tf_op jit(solution)/shard_map/all_to_all | solution.py:104
  57.8 72.1 %all-to-all-start.2 = ((bf16[128,160,128]{2,1,0:T(8,128)(2,1)}), bf16[128,160,128]{2,1,0:T(8,128)(2,1)}, u32[]{:S(2)}, u32[]{:S(2)}) async-start(bf16[128,160,128]{2,1,0:T(8,128)(2,1)} %bitcast.64), calls=%async_computation.2 | async-start | bytes 10485760 | tf_op jit(solution)/shard_map/all_to_all | solution.py:130
  151.7 7.4 %copy-start.5 = (f32[64,8]{0,1:T(8,128)S(1)}, f32[64,8]{0,1:T(8,128)}, u32[]{:S(2)}) copy-start(f32[64,8]{0,1:T(8,128)} %param.19) | copy-start | bytes 6148
  151.7 68.4 %all-to-all-start.3 = ((bf16[128,160,128]{2,1,0:T(8,128)(2,1)}), bf16[128,160,128]{2,1,0:T(8,128)(2,1)}, u32[]{:S(2)}, u32[]{:S(2)}) async-start(bf16[128,160,128]{2,1,0:T(8,128)(2,1)} %reshape.201), calls=%async_computation.3 | async-start | bytes 10485760 | tf_op jit(solution)/shard_map/all_to_all | solution.py:141

commit v14 on v11

--- a/solution.py
+++ b/solution.py
@@ -1,3 +1,5 @@
+import functools
+
 import jax
 import jax.numpy as jnp
 from jax import lax
@@ -13,8 +15,7 @@
 TQ = 256
 
 
-def _attn_kernel(len_ref, q_ref, ck_ref, cv_ref, nk_ref, nv_ref, o_ref):
-    r = pl.program_id(0)
+def _attn_kernel(len_ref, q_ref, ck_ref, cv_ref, nk_ref, nv_ref, o_ref, *, r):
     qb = pl.program_id(1)
     length = len_ref[r]
     q = q_ref[0]
@@ -39,25 +40,25 @@
     o_ref[0] = (mixed / denom).astype(o_ref.dtype)
 
 
-def attention_kernel(queries, new_entries, cache_entries, cache_lengths, interpret=False):
-    reqs, new_len, width = queries.shape
+def attention_kernel(queries, new_entries, cache_entries, cache_lengths, req, interpret=False):
+    _, new_len, width = queries.shape
     cache_len = cache_entries.shape[2]
     grid_spec = pltpu.PrefetchScalarGridSpec(
         num_scalar_prefetch=1,
-        grid=(reqs, new_len // TQ),
+        grid=(1, new_len // TQ),
         in_specs=[
-            pl.BlockSpec((1, TQ, width), lambda r, b, lens: (r, b, 0)),
-            pl.BlockSpec((1, 1, cache_len, width), lambda r, b, lens: (r, 0, 0, 0)),
-            pl.BlockSpec((1, 1, cache_len, width), lambda r, b, lens: (r, 1, 0, 0)),
-            pl.BlockSpec((1, 1, new_len, width), lambda r, b, lens: (r, 0, 0, 0)),
-            pl.BlockSpec((1, 1, new_len, width), lambda r, b, lens: (r, 1, 0, 0)),
+            pl.BlockSpec((1, TQ, width), lambda r, b, lens: (req, b, 0)),
+            pl.BlockSpec((1, 1, cache_len, width), lambda r, b, lens: (req, 0, 0, 0)),
+            pl.BlockSpec((1, 1, cache_len, width), lambda r, b, lens: (req, 1, 0, 0)),
+            pl.BlockSpec((1, 1, new_len, width), lambda r, b, lens: (req, 0, 0, 0)),
+            pl.BlockSpec((1, 1, new_len, width), lambda r, b, lens: (req, 1, 0, 0)),
         ],
-        out_specs=pl.BlockSpec((1, TQ, width), lambda r, b, lens: (r, b, 0)),
+        out_specs=pl.BlockSpec((1, TQ, width), lambda r, b, lens: (0, b, 0)),
     )
     return pl.pallas_call(
-        _attn_kernel,
+        functools.partial(_attn_kernel, r=req),
         grid_spec=grid_spec,
-        out_shape=jax.ShapeDtypeStruct((reqs, new_len, width), jnp.bfloat16),
+        out_shape=jax.ShapeDtypeStruct((1, new_len, width), jnp.bfloat16),
         interpret=interpret,
     )(cache_lengths, queries, cache_entries, cache_entries, new_entries, new_entries)
 
@@ -75,12 +76,10 @@
     expert_in,
     expert_down,
 ):
-    req_local, new_len, width_local = queries.shape
+    req_local, _, width_local = queries.shape
     tok_local = residual.shape[0]
     model_width = residual.shape[1]
 
-    attention = attention_kernel(queries, new_entries, cache_entries, cache_lengths)
-    attention = attention.reshape(req_local * new_len, width_local)
     req_count = lax.axis_size("req")
     z_count = lax.axis_size("z")
     x_count = lax.axis_size("x")
@@ -91,9 +90,13 @@
         shifted.append(lax.ppermute(out_proj, "x", pairs))
     row_proj = jnp.stack(shifted)
     row_proj = row_proj.reshape(x_count * width_local, model_width)
-    rows_att = attention.reshape(z_count, x_count, tok_local, width_local)
-    rows_att = jnp.transpose(rows_att, (1, 0, 2, 3))
-    rows_att = lax.all_to_all(rows_att, "x", 0, 0, tiled=True)
+    parts = []
+    for req in range(req_local):
+        att_req = attention_kernel(queries, new_entries, cache_entries, cache_lengths, req)
+        att_req = att_req.reshape(z_count // req_local, x_count, tok_local, width_local)
+        att_req = jnp.transpose(att_req, (1, 0, 2, 3))
+        parts.append(lax.all_to_all(att_req, "x", 0, 0, tiled=True))
+    rows_att = jnp.concatenate(parts, axis=1)
     order = (x_here - jnp.arange(x_count, dtype=jnp.int32)) % x_count
     rows_att = rows_att[order]
     rows_att = jnp.transpose(rows_att, (1, 2, 0, 3)).reshape(
@@ -130,9 +133,11 @@
     arrived = lax.all_to_all(outgoing, ("req", "z", "x"), 0, 0, tiled=True)
     sources = arrived.shape[0]
     rows = arrived.reshape(sources * capacity, folds, lanes)
-    w_in = expert_in[:, :, 0:half_units].reshape(2, folds, lanes, half_units)
-    gate_part = jnp.einsum("tkd,kdf->tf", rows, w_in[0], preferred_element_type=jnp.float32)
-    up_part = jnp.einsum("tkd,kdf->tf", rows, w_in[1], preferred_element_type=jnp.float32)
+    w_in = jnp.concatenate([expert_in[0, :, 0:half_units], expert_in[1, :, 0:half_units]], axis=1)
+    w_in = w_in.reshape(folds, lanes, 2 * half_units)
+    both_parts = jnp.einsum("tkd,kdf->tf", rows, w_in, preferred_element_type=jnp.float32)
+    gate_part = both_parts[:, :half_units]
+    up_part = both_parts[:, half_units:]
     inner = (jax.nn.silu(gate_part) * up_part).astype(jnp.bfloat16)
     half_out = jnp.dot(inner, expert_down, preferred_element_type=jnp.float32).astype(jnp.bfloat16)
     back = half_out.reshape(sources, capacity * folds, lanes)

time: 234 us -> 238 us (1.017)
  starting transfers between devices: 30.7 us -> 37.5 us
  matrix products: 24.4 us -> 20.4 us
  waiting for transfers between devices: 129 us -> 125 us
  Pallas kernels: 12.4 us -> 15.5 us
    all_to_all x1 -> x2, starting transfers between devices: 4.5 us -> 10.2 us  [layer(): parts.append(lax.all_to_all(att_req, 'x', 0, 0, tiled=True))]
    dot_general x1, matrix products: 10.4 us -> 4.71 us  [layer(): jnp.dot(inner, expert_down, preferred_element_type=jnp.float32)]
    reshape x0 -> x2, local copies, waits for them, and re-layouts: none -> 3.13 us  [layer(): att_req.reshape(z_count // req_local, x_count, tok_local, width_local)]
    pallas_call x1 -> x2, Pallas kernels: 12.4 us -> 15.5 us  [attention_kernel(): pl.pallas_call(functools.partial(_attn_kernel, r=req), grid_spec=grid_spe...]
    all_to_all x1 -> x2, waiting for transfers between devices: 5.73 us -> 2.68 us  [layer(): parts.append(lax.all_to_all(att_req, 'x', 0, 0, tiled=True))]
  transfers between devices with their start and end apart: 7 -> 8, of which waited for: 4 -> 5; matrix products, arithmetic and copies ran while one was open for 7% -> 7% of each run, Pallas kernels for 5% -> 7%
where the time goes in v14:
time: 238 us; the launch traced here: 234 us
  waiting for transfers between devices  125 us (53%)
  starting transfers between devices  37.5 us (16%)
  local copies, waits for them, and re-layouts  29.9 us (13%)
  matrix products  20.4 us (9%)
  Pallas kernels  15.5 us (7%)
  other arithmetic  4.66 us (2%)
    all_to_all x1, waiting for transfers between devices, layer(): returned = lax.all_to_all(back, ('req', 'z', 'x'), 0, 0, tiled=True)  57.4 us
    all_to_all x1, waiting for transfers between devices, layer(): arrived = lax.all_to_all(outgoing, ('req', 'z', 'x'), 0, 0, tiled=True)  56.4 us
    pallas_call x2, Pallas kernels, attention_kernel(): pl.pallas_call(functools.partial(_attn_kernel, r=req), grid_spec=grid_spe...  15.5 us
    all_to_all x1, starting transfers between devices, layer(): arrived = lax.all_to_all(outgoing, ('req', 'z', 'x'), 0, 0, tiled=True)  12.2 us
    all_to_all x2, starting transfers between devices, layer(): parts.append(lax.all_to_all(att_req, 'x', 0, 0, tiled=True))  10.2 us
    reshape x1, local copies, waits for them, and re-layouts, layer(): back = half_out.reshape(sources, capacity * folds, lanes)  8.93 us
    all_to_all x1, waiting for transfers between devices, layer(): partial = lax.all_to_all(partial, 'z', 0, 0, tiled=True)  8.76 us
    dot_general x1, matrix products, layer(): jnp.einsum('tkd,kdf->tf', rows, w_in, preferred_element_type=jnp.float32)  8.19 us
  transfers between devices with their start and end apart: 8, of which 5 were waited for; matrix products, arithmetic and copies ran while one was open for 7% of the time, Pallas kernels for 7%

profile of v14, /device:TPU:37, one launch (start us, length us, event | category | flops | bytes accessed | tf_op | source)
XLA Modules:
  0.0 234.1 jit_solution(4794668215472042029)
XLA Ops:
  1.0 2.5 %collective-permute-start.1 = (bf16[128,2048]{1,0:T(8,128)(2,1)}, bf16[128,2048]{1,0:T(8,128)(2,1)}, u32[]{:S(2)}, u32[]{:S(2)}) collective-permute-start(bf16[128,2048]{1,0:T(8,128)(2,1)} %param.15), channel_id=1, source_target_pairs={{0,2},{1,3},{2,0},{3,1},{4,6},{5,7},{6,4},{7,5},{8,10},{9,11},{10,... | collective-permute-start | bytes 1572872 | tf_op jit(solution)/shard_map/ppermute | solution.py:90
  3.4 7.7 %shard_map.123 = bf16[1,512,128]{2,1,0:T(8,128)(2,1)} custom-call(s32[2]{0:T(128)} %len_ref.3, bf16[2,512,128]{2,1,0:T(8,128)(2,1)} %q_ref.3, bf16[2,2,4096,128]{3,2,1,0:T(8,128)(2,1)} %cv_ref.3, bf16[2,2,4096,128]{3,2,1,0:T(8,128)(2,1)} %cv_ref.3, bf16[2,2,512,128]{3,2,1,0:T(8,128)(2,1)} %nv_ref.3, bf16[2,2,512,128]{3,2,1,0:T(8,128)(2,1)} %nv_ref.3), custom_call_target="tpu_custom_call" | custom-call | tf_op jit(solution)/shard_map/pallas_call | solution.py:58
  11.1 1.6 copy.74
  12.7 4.5 %all-to-all-start.1 = ((bf16[4,2,64,128]{3,2,1,0:T(8,128)(2,1)}), bf16[4,2,64,128]{3,2,1,0:T(8,128)(2,1)S(1)}, u32[]{:S(2)}, u32[]{:S(2)}) async-start(bf16[4,2,64,128]{3,2,1,0:T(8,128)(2,1)} %bitcast.61), calls=%async_computation.1 | async-start | bytes 262144 | tf_op jit(solution)/shard_map/all_to_all | solution.py:98
  17.1 7.8 %shard_map.122 = bf16[1,512,128]{2,1,0:T(8,128)(2,1)} custom-call(s32[2]{0:T(128)} %len_ref.3, bf16[2,512,128]{2,1,0:T(8,128)(2,1)} %q_ref.3, bf16[2,2,4096,128]{3,2,1,0:T(8,128)(2,1)} %cv_ref.3, bf16[2,2,4096,128]{3,2,1,0:T(8,128)(2,1)} %cv_ref.3, bf16[2,2,512,128]{3,2,1,0:T(8,128)(2,1)} %nv_ref.3, bf16[2,2,512,128]{3,2,1,0:T(8,128)(2,1)} %nv_ref.3), custom_call_target="tpu_custom_call" | custom-call | tf_op jit(solution)/shard_map/pallas_call | solution.py:58
  25.2 1.6 copy.75
  26.8 1.2 reduce-window.6
  28.8 5.7 %all-to-all-start = ((bf16[4,2,64,128]{3,2,1,0:T(8,128)(2,1)}), bf16[4,2,64,128]{3,2,1,0:T(8,128)(2,1)S(1)}, u32[]{:S(2)}, u32[]{:S(2)}) async-start(bf16[4,2,64,128]{3,2,1,0:T(8,128)(2,1)} %bitcast.62), calls=%async_computation | async-start | bytes 262144 | tf_op jit(solution)/shard_map/all_to_all | solution.py:98
  34.6 2.4 %all-to-all-done = bf16[4,2,64,128]{3,2,1,0:T(8,128)(2,1)S(1)} async-done(((bf16[4,2,64,128]{3,2,1,0:T(8,128)(2,1)}), bf16[4,2,64,128]{3,2,1,0:T(8,128)(2,1)S(1)}, u32[]{:S(2)}, u32[]{:S(2)}) %all-to-all-start) | async-done | bytes 131104 | tf_op jit(solution)/shard_map/all_to_all | solution.py:98
  37.9 1.6 pad_maximum_fusion
  39.5 1.7 convolution_convert_fusion.1
  41.2 5.0 %all-to-all-start.2 = ((bf16[4,64,2048]{2,1,0:T(8,128)(2,1)}), bf16[4,64,2048]{2,1,0:T(8,128)(2,1)S(1)}, u32[]{:S(2)}, u32[]{:S(2)}) async-start(bf16[4,64,2048]{2,1,0:T(8,128)(2,1)} %bitcast.65), calls=%async_computation.2 | async-start | bytes 2097152 | tf_op jit(solution)/shard_map/all_to_all | solution.py:107
  46.3 2.4 %scatter_custom_fusion = s32[640]{0:T(1024)S(1)} fusion(s32[512]{0:T(512)S(1)} %bitcast.76, s32[512]{0:T(512)S(1)} %add_select_fusion, s32[]{:T(128)} %constant.60.clone.1), kind=kCustom, calls=%fused_computation.57 | custom fusion | bytes 2564 | tf_op jit(solution)/shard_map/scatter | solution.py:126
  49.1 8.8 %all-to-all-done.2 = bf16[4,64,2048]{2,1,0:T(8,128)(2,1)S(1)} async-done(((bf16[4,64,2048]{2,1,0:T(8,128)(2,1)}), bf16[4,64,2048]{2,1,0:T(8,128)(2,1)S(1)}, u32[]{:S(2)}, u32[]{:S(2)}) %all-to-all-start.2) | async-done | bytes 1048608 | tf_op jit(solution)/shard_map/all_to_all | solution.py:107
  59.1 5.0 %gather_fusion.1 = bf16[1280,16,128]{2,1,0:T(8,128)(2,1)} fusion(bf16[65,16,128]{2,1,0:T(8,128)(2,1)S(1)} %concatenate.15, s32[2048]{0:T(1024)S(1)} %pad_clamp_fusion), kind=kCustom, calls=%fused_computation.1 | custom fusion | bytes 10490880 | tf_op jit(solution)/shard_map/gather | solution.py:131
  64.1 12.2 %all-to-all-start.3 = ((bf16[128,160,128]{2,1,0:T(8,128)(2,1)}), bf16[128,160,128]{2,1,0:T(8,128)(2,1)}, u32[]{:S(2)}, u32[]{:S(2)}) async-start(bf16[128,160,128]{2,1,0:T(8,128)(2,1)} %bitcast.63), calls=%async_computation.3 | async-start | bytes 10485760 | tf_op jit(solution)/shard_map/all_to_all | solution.py:133
  76.3 4.6 %fusion.38 = (bf16[1,2048,512]{2,1,0:T(8,128)(2,1)}, bf16[1,2048,512]{2,1,0:T(8,128)(2,1)}) fusion(bf16[2,2048,512]{2,1,0:T(8,128)(2,1)} %param.20), kind=kLoop, calls=%fused_computation.68 | loop fusion | bytes 8388608 | tf_op jit(solution)/shard_map/slice | solution.py:136
  80.9 56.4 %all-to-all-done.3 = bf16[128,160,128]{2,1,0:T(8,128)(2,1)} async-done(((bf16[128,160,128]{2,1,0:T(8,128)(2,1)}), bf16[128,160,128]{2,1,0:T(8,128)(2,1)}, u32[]{:S(2)}, u32[]{:S(2)}) %all-to-all-start.3) | async-done | bytes 5242912 | tf_op jit(solution)/shard_map/all_to_all | solution.py:133
  137.3 8.2 %fusion.4 = f32[1280,1024]{1,0:T(8,128)S(1)} fusion(bf16[1280,16,128]{2,1,0:T(8,128)(2,1)} %bitcast.17, bf16[16,128,512]{2,1,0:T(8,128)(2,1)} %bitcast.67, bf16[16,128,512]{2,1,0:T(8,128)(2,1)} %bitcast.66), kind=kOutput, calls=%fused_computation.8 | convolution fusion | flops 5377097728 | bytes 14680064 | tf_op jit(solution)/shard_map/tkd,kdf->tf/dot_general | solution.py:138
  145.5 4.7 %convolution_convert_fusion = bf16[1280,2048]{1,0:T(8,128)(2,1)} fusion(bf16[512,2048]{1,0:T(8,128)(2,1)S(1)} %copy-done, f32[1280,1024]{1,0:T(8,128)S(1)} %fusion.4), kind=kOutput, calls=%fused_computation.3 | convolution fusion | flops 2690908160 | bytes 12582912 | tf_op jit(solution)/shard_map/dot_general | solution.py:142
  150.3 8.9 %reshape.210 = bf16[128,160,128]{2,1,0:T(8,128)(2,1)} reshape(bf16[1280,2048]{1,0:T(8,128)(2,1)} %convolution_convert_fusion) | data formatting | bytes 10485760 | tf_op jit(solution)/shard_map/reshape | solution.py:143
  159.2 7.3 %all-to-all-start.4 = ((bf16[128,160,128]{2,1,0:T(8,128)(2,1)}), bf16[128,160,128]{2,1,0:T(8,128)(2,1)}, u32[]{:S(2)}, u32[]{:S(2)}) async-start(bf16[128,160,128]{2,1,0:T(8,128)(2,1)} %reshape.210), calls=%async_computation.4 | async-start | bytes 10485760 | tf_op jit(solution)/shard_map/all_to_all | solution.py:144
  170.2 57.4 %all-to-all-done.4 = bf16[128,160,128]{2,1,0:T(8,128)(2,1)} async-done(((bf16[128,160,128]{2,1,0:T(8,128)(2,1)}), bf16[128,160,128]{2,1,0:T(8,128)(2,1)}, u32[]{:S(2)}, u32[]{:S(2)}) %all-to-all-start.4) | async-done | bytes 5242912 | tf_op jit(solution)/shard_map/all_to_all | solution.py:144
  227.5 5.8 %fusion.16 = bf16[16,8,8,128]{3,2,1,0:T(8,128)(2,1)S(1)} fusion(bf16[1280,16,128]{2,1,0:T(8,128)(2,1)} %bitcast.21, f32[64,1280]{0,1:T(8,128)} %reshape.205), kind=kOutput, calls=%fused_computation.21 | convolution fusion | flops 2013396992 | bytes 5832704 | tf_op jit(solution)/shard_map/ts,skd->tkd/dot_general | solution.py:154
  (55 shorter events, 8.2 us)
Async XLA Ops:
  0.6 144.9 %copy-start = (bf16[512,2048]{1,0:T(8,128)(2,1)S(1)}, bf16[512,2048]{1,0:T(8,128)(2,1)}, u32[]{:S(2)}) copy-start(bf16[512,2048]{1,0:T(8,128)(2,1)} %param.21) | copy-start | bytes 6291460
  0.6 37.2 %collective-permute-start.2 = (bf16[128,2048]{1,0:T(8,128)(2,1)}, bf16[128,2048]{1,0:T(8,128)(2,1)}, u32[]{:S(2)}, u32[]{:S(2)}) collective-permute-start(bf16[128,2048]{1,0:T(8,128)(2,1)} %param.15), channel_id=1, source_target_pairs={{0,3},{1,0},{2,1},{3,2},{4,7},{5,4},{6,5},{7,6},{8,11},{9,8},{10,9... | collective-permute-start | bytes 1572872 | tf_op jit(solution)/shard_map/ppermute | solution.py:90
  1.0 36.9 %collective-permute-start.1 = (bf16[128,2048]{1,0:T(8,128)(2,1)}, bf16[128,2048]{1,0:T(8,128)(2,1)}, u32[]{:S(2)}, u32[]{:S(2)}) collective-permute-start(bf16[128,2048]{1,0:T(8,128)(2,1)} %param.15), channel_id=1, source_target_pairs={{0,2},{1,3},{2,0},{3,1},{4,6},{5,7},{6,4},{7,5},{8,10},{9,11},{10,... | collective-permute-start | bytes 1572872 | tf_op jit(solution)/shard_map/ppermute | solution.py:90
  3.4 34.4 %collective-permute-start = (bf16[128,2048]{1,0:T(8,128)(2,1)}, bf16[128,2048]{1,0:T(8,128)(2,1)}, u32[]{:S(2)}, u32[]{:S(2)}) collective-permute-start(bf16[128,2048]{1,0:T(8,128)(2,1)} %param.15), channel_id=1, source_target_pairs={{0,1},{1,2},{2,3},{3,0},{4,5},{5,6},{6,7},{7,4},{8,9},{9,10},{10,1... | collective-permute-start | bytes 1572872 | tf_op jit(solution)/shard_map/ppermute | solution.py:90
  12.7 16.2 %all-to-all-start.1 = ((bf16[4,2,64,128]{3,2,1,0:T(8,128)(2,1)}), bf16[4,2,64,128]{3,2,1,0:T(8,128)(2,1)S(1)}, u32[]{:S(2)}, u32[]{:S(2)}) async-start(bf16[4,2,64,128]{3,2,1,0:T(8,128)(2,1)} %bitcast.61), calls=%async_computation.1 | async-start | bytes 262144 | tf_op jit(solution)/shard_map/all_to_all | solution.py:98
  17.1 7.8 %copy-start.4 = (s32[64,8]{0,1:T(8,128)S(1)}, s32[64,8]{0,1:T(8,128)}, u32[]{:S(2)}) copy-start(s32[64,8]{0,1:T(8,128)} %param.18) | copy-start | bytes 6148
  25.0 12.9 %copy-start.2 = (bf16[128,2048]{1,0:T(8,128)(2,1)S(1)}, bf16[128,2048]{1,0:T(8,128)(2,1)}, u32[]{:S(2)}) copy-start(bf16[128,2048]{1,0:T(8,128)(2,1)} %param.15) | copy-start | bytes 1572868
  28.8 8.1 %all-to-all-start = ((bf16[4,2,64,128]{3,2,1,0:T(8,128)(2,1)}), bf16[4,2,64,128]{3,2,1,0:T(8,128)(2,1)S(1)}, u32[]{:S(2)}, u32[]{:S(2)}) async-start(bf16[4,2,64,128]{3,2,1,0:T(8,128)(2,1)} %bitcast.62), calls=%async_computation | async-start | bytes 262144 | tf_op jit(solution)/shard_map/all_to_all | solution.py:98
  41.2 16.8 %copy-start.1 = (bf16[64,2048]{1,0:T(8,128)(2,1)S(1)}, bf16[64,2048]{1,0:T(8,128)(2,1)}, u32[]{:S(2)}) copy-start(bf16[64,2048]{1,0:T(8,128)(2,1)} %param.16) | copy-start | bytes 786436
  41.2 17.0 %copy-start.3 = (f32[2048]{0:T(1024)S(1)}, f32[2048]{0:T(1024)}, u32[]{:S(2)}) copy-start(f32[2048]{0:T(1024)} %param.17) | copy-start | bytes 24580
  41.2 16.7 %all-to-all-start.2 = ((bf16[4,64,2048]{2,1,0:T(8,128)(2,1)}), bf16[4,64,2048]{2,1,0:T(8,128)(2,1)S(1)}, u32[]{:S(2)}, u32[]{:S(2)}) async-start(bf16[4,64,2048]{2,1,0:T(8,128)(2,1)} %bitcast.65), calls=%async_computation.2 | async-start | bytes 2097152 | tf_op jit(solution)/shard_map/all_to_all | solution.py:107
  64.1 73.2 %all-to-all-start.3 = ((bf16[128,160,128]{2,1,0:T(8,128)(2,1)}), bf16[128,160,128]{2,1,0:T(8,128)(2,1)}, u32[]{:S(2)}, u32[]{:S(2)}) async-start(bf16[128,160,128]{2,1,0:T(8,128)(2,1)} %bitcast.63), calls=%async_computation.3 | async-start | bytes 10485760 | tf_op jit(solution)/shard_map/all_to_all | solution.py:133
  159.2 7.3 %copy-start.5 = (f32[64,8]{0,1:T(8,128)S(1)}, f32[64,8]{0,1:T(8,128)}, u32[]{:S(2)}) copy-start(f32[64,8]{0,1:T(8,128)} %param.19) | copy-start | bytes 6148
  159.2 68.4 %all-to-all-start.4 = ((bf16[128,160,128]{2,1,0:T(8,128)(2,1)}), bf16[128,160,128]{2,1,0:T(8,128)(2,1)}, u32[]{:S(2)}, u32[]{:S(2)}) async-start(bf16[128,160,128]{2,1,0:T(8,128)(2,1)} %reshape.210), calls=%async_computation.4 | async-start | bytes 10485760 | tf_op jit(solution)/shard_map/all_to_all | solution.py:144

commit v15 on v13

--- a/solution.py
+++ b/solution.py
@@ -10,7 +10,7 @@
 EXPERTS = 64
 FF = 1024
 TOP = 8
-TQ = 256
+TQ = 128
 
 
 def _attn_kernel(len_ref, q_ref, ck_ref, cv_ref, nk_ref, nv_ref, o_ref):
@@ -147,12 +147,11 @@
     )
     mixing = jnp.broadcast_to(mixing.reshape(tok_local, EXPERTS, 1, capacity), (tok_local, EXPERTS, 2, capacity))
     mixing = mixing.reshape(tok_local, EXPERTS * 2 * capacity)
-    both = returned.reshape(EXPERTS * 2 * capacity, folds, lanes)
-    mixing_hi = mixing.astype(jnp.bfloat16)
-    mixing_lo = (mixing - mixing_hi.astype(jnp.float32)).astype(jnp.bfloat16)
+    both = returned.reshape(EXPERTS * 2 * capacity, folds, lanes).astype(jnp.float32)
     expert_out = jnp.einsum(
-        "ts,skd->tkd", mixing_hi, both, preferred_element_type=jnp.float32
-    ) + jnp.einsum("ts,skd->tkd", mixing_lo, both, preferred_element_type=jnp.float32)
+        "ts,skd->tkd", mixing, both, precision=lax.Precision.HIGH,
+        preferred_element_type=jnp.float32,
+    )
     expert_out = expert_out.astype(jnp.bfloat16).reshape(tok_local, model_width)
     return (attended, expert_out)
 

time: 231 us -> 229 us (level)
  waiting for transfers between devices: 131 us -> 127 us
  local copies, waits for them, and re-layouts: 26.1 us -> 28.5 us
    dot_general x2 -> x1, matrix products: 7.12 us -> 4.84 us  [layer(): jnp.einsum('ts,skd->tkd', mixing, both, precision=lax.Precision.HIGH, pre...]
  transfers between devices with their start and end apart: 7 -> 7, of which waited for: 4 -> 4; matrix products, arithmetic and copies ran while one was open for 6% -> 7% of each run, Pallas kernels for 5% -> 6%
where the time goes in v15:
time: 229 us; the launch traced here: 226 us
  waiting for transfers between devices  127 us (55%)
  starting transfers between devices  30.7 us (13%)
  local copies, waits for them, and re-layouts  28.5 us (12%)
  matrix products  19.4 us (8%)
  Pallas kernels  14.2 us (6%)
  other arithmetic  4.64 us (2%)
    all_to_all x1, waiting for transfers between devices, layer(): returned = lax.all_to_all(back, ('req', 'z', 'x'), 0, 0, tiled=True)  57.4 us
    all_to_all x1, waiting for transfers between devices, layer(): arrived = lax.all_to_all(outgoing, ('req', 'z', 'x'), 0, 0, tiled=True)  56.4 us
    pallas_call x1, Pallas kernels, attention_kernel(): pl.pallas_call(_attn_kernel, grid_spec=grid_spec, out_shape=jax.ShapeDtyp...  14.2 us
    all_to_all x1, starting transfers between devices, layer(): arrived = lax.all_to_all(outgoing, ('req', 'z', 'x'), 0, 0, tiled=True)  11.1 us
    all_to_all x1, waiting for transfers between devices, layer(): partial = lax.all_to_all(partial, 'z', 0, 0, tiled=True)  9.56 us
    reshape x1, local copies, waits for them, and re-layouts, layer(): back = half_out.reshape(sources, capacity * folds, lanes)  8.93 us
    dot_general x1, matrix products, layer(): jnp.einsum('tkd,kdf->tf', rows, w_in, preferred_element_type=jnp.float32)  8.19 us
    all_to_all x1, starting transfers between devices, layer(): returned = lax.all_to_all(back, ('req', 'z', 'x'), 0, 0, tiled=True)  7.33 us
  transfers between devices with their start and end apart: 7, of which 4 were waited for; matrix products, arithmetic and copies ran while one was open for 7% of the time, Pallas kernels for 6%

profile of v15, /device:TPU:37, one launch (start us, length us, event | category | flops | bytes accessed | tf_op | source)
XLA Modules:
  0.0 225.7 jit_solution(4712408113454159026)
XLA Ops:
  1.0 2.5 %collective-permute-start.1 = (bf16[128,2048]{1,0:T(8,128)(2,1)}, bf16[128,2048]{1,0:T(8,128)(2,1)}, u32[]{:S(2)}, u32[]{:S(2)}) collective-permute-start(bf16[128,2048]{1,0:T(8,128)(2,1)} %param.15), channel_id=1, source_target_pairs={{0,2},{1,3},{2,0},{3,1},{4,6},{5,7},{6,4},{7,5},{8,10},{9,11},{10,... | collective-permute-start | bytes 1572872 | tf_op jit(solution)/shard_map/ppermute | solution.py:91
  3.4 14.2 %shard_map.122 = bf16[2,512,128]{2,1,0:T(8,128)(2,1)} custom-call(s32[2]{0:T(128)} %len_ref.1, bf16[2,512,128]{2,1,0:T(8,128)(2,1)} %q_ref.1, bf16[2,2,4096,128]{3,2,1,0:T(8,128)(2,1)} %cv_ref.1, bf16[2,2,4096,128]{3,2,1,0:T(8,128)(2,1)} %cv_ref.1, bf16[2,2,512,128]{3,2,1,0:T(8,128)(2,1)} %nv_ref.1, bf16[2,2,512,128]{3,2,1,0:T(8,128)(2,1)} %nv_ref.1), custom_call_target="tpu_custom_call" | custom-call | tf_op jit(solution)/shard_map/pallas_call | solution.py:57
  17.7 1.7 copy.71
  19.4 4.5 %all-to-all-start = ((bf16[4,4,64,128]{3,2,1,0:T(8,128)(2,1)}), bf16[4,4,64,128]{3,2,1,0:T(8,128)(2,1)S(1)}, u32[]{:S(2)}, u32[]{:S(2)}) async-start(bf16[4,4,64,128]{3,2,1,0:T(8,128)(2,1)} %bitcast.58), calls=%async_computation | async-start | bytes 524288 | tf_op jit(solution)/shard_map/all_to_all | solution.py:96
  24.2 1.2 reduce-window.6
  25.9 4.0 %all-to-all-done = bf16[4,4,64,128]{3,2,1,0:T(8,128)(2,1)S(1)} async-done(((bf16[4,4,64,128]{3,2,1,0:T(8,128)(2,1)}), bf16[4,4,64,128]{3,2,1,0:T(8,128)(2,1)S(1)}, u32[]{:S(2)}, u32[]{:S(2)}) %all-to-all-start) | async-done | bytes 262176 | tf_op jit(solution)/shard_map/all_to_all | solution.py:96
  30.7 1.6 pad_maximum_fusion
  32.4 1.7 convolution_convert_fusion.1
  34.1 5.0 %all-to-all-start.1 = ((bf16[4,64,2048]{2,1,0:T(8,128)(2,1)}), bf16[4,64,2048]{2,1,0:T(8,128)(2,1)S(1)}, u32[]{:S(2)}, u32[]{:S(2)}) async-start(bf16[4,64,2048]{2,1,0:T(8,128)(2,1)} %bitcast.61), calls=%async_computation.1 | async-start | bytes 2097152 | tf_op jit(solution)/shard_map/all_to_all | solution.py:104
  39.2 2.4 %scatter_custom_fusion = s32[640]{0:T(1024)S(1)} fusion(s32[512]{0:T(512)S(1)} %bitcast.71, s32[512]{0:T(512)S(1)} %add_select_fusion, s32[]{:T(128)} %constant.60.clone.1), kind=kCustom, calls=%fused_computation.55 | custom fusion | bytes 2564 | tf_op jit(solution)/shard_map/scatter | solution.py:123
  42.0 9.6 %all-to-all-done.1 = bf16[4,64,2048]{2,1,0:T(8,128)(2,1)S(1)} async-done(((bf16[4,64,2048]{2,1,0:T(8,128)(2,1)}), bf16[4,64,2048]{2,1,0:T(8,128)(2,1)S(1)}, u32[]{:S(2)}, u32[]{:S(2)}) %all-to-all-start.1) | async-done | bytes 1048608 | tf_op jit(solution)/shard_map/all_to_all | solution.py:104
  52.8 5.0 %gather_fusion.1 = bf16[1280,16,128]{2,1,0:T(8,128)(2,1)} fusion(bf16[65,16,128]{2,1,0:T(8,128)(2,1)S(1)} %concatenate.11, s32[2048]{0:T(1024)S(1)} %pad_clamp_fusion), kind=kCustom, calls=%fused_computation.1 | custom fusion | bytes 10490880 | tf_op jit(solution)/shard_map/gather | solution.py:128
  57.8 11.1 %all-to-all-start.2 = ((bf16[128,160,128]{2,1,0:T(8,128)(2,1)}), bf16[128,160,128]{2,1,0:T(8,128)(2,1)}, u32[]{:S(2)}, u32[]{:S(2)}) async-start(bf16[128,160,128]{2,1,0:T(8,128)(2,1)} %bitcast.59), calls=%async_computation.2 | async-start | bytes 10485760 | tf_op jit(solution)/shard_map/all_to_all | solution.py:130
  68.9 4.6 %fusion.38 = (bf16[1,2048,512]{2,1,0:T(8,128)(2,1)}, bf16[1,2048,512]{2,1,0:T(8,128)(2,1)}) fusion(bf16[2,2048,512]{2,1,0:T(8,128)(2,1)} %param.20), kind=kLoop, calls=%fused_computation.66 | loop fusion | bytes 8388608 | tf_op jit(solution)/shard_map/slice | solution.py:133
  73.4 56.4 %all-to-all-done.2 = bf16[128,160,128]{2,1,0:T(8,128)(2,1)} async-done(((bf16[128,160,128]{2,1,0:T(8,128)(2,1)}), bf16[128,160,128]{2,1,0:T(8,128)(2,1)}, u32[]{:S(2)}, u32[]{:S(2)}) %all-to-all-start.2) | async-done | bytes 5242912 | tf_op jit(solution)/shard_map/all_to_all | solution.py:130
  129.9 8.2 %fusion.4 = f32[1280,1024]{1,0:T(8,128)S(1)} fusion(bf16[1280,16,128]{2,1,0:T(8,128)(2,1)} %bitcast.15, bf16[16,128,512]{2,1,0:T(8,128)(2,1)} %bitcast.63, bf16[16,128,512]{2,1,0:T(8,128)(2,1)} %bitcast.62), kind=kOutput, calls=%fused_computation.8 | convolution fusion | flops 5377097728 | bytes 14680064 | tf_op jit(solution)/shard_map/tkd,kdf->tf/dot_general | solution.py:135
  138.1 4.7 %convolution_convert_fusion = bf16[1280,2048]{1,0:T(8,128)(2,1)} fusion(bf16[512,2048]{1,0:T(8,128)(2,1)S(1)} %copy-done, f32[1280,1024]{1,0:T(8,128)S(1)} %fusion.4), kind=kOutput, calls=%fused_computation.3 | convolution fusion | flops 2690908160 | bytes 12582912 | tf_op jit(solution)/shard_map/dot_general | solution.py:139
  142.8 8.9 %reshape.202 = bf16[128,160,128]{2,1,0:T(8,128)(2,1)} reshape(bf16[1280,2048]{1,0:T(8,128)(2,1)} %convolution_convert_fusion) | data formatting | bytes 10485760 | tf_op jit(solution)/shard_map/reshape | solution.py:140
  151.7 7.3 %all-to-all-start.3 = ((bf16[128,160,128]{2,1,0:T(8,128)(2,1)}), bf16[128,160,128]{2,1,0:T(8,128)(2,1)}, u32[]{:S(2)}, u32[]{:S(2)}) async-start(bf16[128,160,128]{2,1,0:T(8,128)(2,1)} %reshape.202), calls=%async_computation.3 | async-start | bytes 10485760 | tf_op jit(solution)/shard_map/all_to_all | solution.py:141
  159.8 0.9 broadcast_in_dim.40
  160.7 1.1 broadcast_in_dim.41
  161.8 0.9 reshape.197
  162.7 57.4 %all-to-all-done.3 = bf16[128,160,128]{2,1,0:T(8,128)(2,1)} async-done(((bf16[128,160,128]{2,1,0:T(8,128)(2,1)}), bf16[128,160,128]{2,1,0:T(8,128)(2,1)}, u32[]{:S(2)}, u32[]{:S(2)}) %all-to-all-start.3) | async-done | bytes 5242912 | tf_op jit(solution)/shard_map/all_to_all | solution.py:141
  220.1 4.8 %fusion.16 = bf16[16,8,8,128]{3,2,1,0:T(8,128)(2,1)S(1)} fusion(bf16[1280,16,128]{2,1,0:T(8,128)(2,1)} %bitcast.19, f32[64,1280]{0,1:T(8,128)} %reshape.197), kind=kOutput, calls=%fused_computation.21 | convolution fusion | flops 1006764032 | bytes 5832704 | tf_op jit(solution)/shard_map/ts,skd->tkd/dot_general | solution.py:151
  (50 shorter events, 5.0 us)
Async XLA Ops:
  0.6 137.4 %copy-start = (bf16[512,2048]{1,0:T(8,128)(2,1)S(1)}, bf16[512,2048]{1,0:T(8,128)(2,1)}, u32[]{:S(2)}) copy-start(bf16[512,2048]{1,0:T(8,128)(2,1)} %param.21) | copy-start | bytes 6291460
  0.6 23.2 %copy-start.4 = (s32[64,8]{0,1:T(8,128)S(1)}, s32[64,8]{0,1:T(8,128)}, u32[]{:S(2)}) copy-start(s32[64,8]{0,1:T(8,128)} %param.18) | copy-start | bytes 6148
  0.7 30.0 %collective-permute-start.2 = (bf16[128,2048]{1,0:T(8,128)(2,1)}, bf16[128,2048]{1,0:T(8,128)(2,1)}, u32[]{:S(2)}, u32[]{:S(2)}) collective-permute-start(bf16[128,2048]{1,0:T(8,128)(2,1)} %param.15), channel_id=1, source_target_pairs={{0,3},{1,0},{2,1},{3,2},{4,7},{5,4},{6,5},{7,6},{8,11},{9,8},{10,9... | collective-permute-start | bytes 1572872 | tf_op jit(solution)/shard_map/ppermute | solution.py:91
  1.0 29.7 %collective-permute-start.1 = (bf16[128,2048]{1,0:T(8,128)(2,1)}, bf16[128,2048]{1,0:T(8,128)(2,1)}, u32[]{:S(2)}, u32[]{:S(2)}) collective-permute-start(bf16[128,2048]{1,0:T(8,128)(2,1)} %param.15), channel_id=1, source_target_pairs={{0,2},{1,3},{2,0},{3,1},{4,6},{5,7},{6,4},{7,5},{8,10},{9,11},{10,... | collective-permute-start | bytes 1572872 | tf_op jit(solution)/shard_map/ppermute | solution.py:91
  3.4 27.3 %collective-permute-start = (bf16[128,2048]{1,0:T(8,128)(2,1)}, bf16[128,2048]{1,0:T(8,128)(2,1)}, u32[]{:S(2)}, u32[]{:S(2)}) collective-permute-start(bf16[128,2048]{1,0:T(8,128)(2,1)} %param.15), channel_id=1, source_target_pairs={{0,1},{1,2},{2,3},{3,0},{4,5},{5,6},{6,7},{7,4},{8,9},{9,10},{10,1... | collective-permute-start | bytes 1572872 | tf_op jit(solution)/shard_map/ppermute | solution.py:91
  17.7 13.1 %copy-start.2 = (bf16[128,2048]{1,0:T(8,128)(2,1)S(1)}, bf16[128,2048]{1,0:T(8,128)(2,1)}, u32[]{:S(2)}) copy-start(bf16[128,2048]{1,0:T(8,128)(2,1)} %param.15) | copy-start | bytes 1572868
  19.4 10.5 %all-to-all-start = ((bf16[4,4,64,128]{3,2,1,0:T(8,128)(2,1)}), bf16[4,4,64,128]{3,2,1,0:T(8,128)(2,1)S(1)}, u32[]{:S(2)}, u32[]{:S(2)}) async-start(bf16[4,4,64,128]{3,2,1,0:T(8,128)(2,1)} %bitcast.58), calls=%async_computation | async-start | bytes 524288 | tf_op jit(solution)/shard_map/all_to_all | solution.py:96
  34.1 17.6 %copy-start.1 = (bf16[64,2048]{1,0:T(8,128)(2,1)S(1)}, bf16[64,2048]{1,0:T(8,128)(2,1)}, u32[]{:S(2)}) copy-start(bf16[64,2048]{1,0:T(8,128)(2,1)} %param.16) | copy-start | bytes 786436
  34.1 17.8 %copy-start.3 = (f32[2048]{0:T(1024)S(1)}, f32[2048]{0:T(1024)}, u32[]{:S(2)}) copy-start(f32[2048]{0:T(1024)} %param.17) | copy-start | bytes 24580
  34.1 17.5 %all-to-all-start.1 = ((bf16[4,64,2048]{2,1,0:T(8,128)(2,1)}), bf16[4,64,2048]{2,1,0:T(8,128)(2,1)S(1)}, u32[]{:S(2)}, u32[]{:S(2)}) async-start(bf16[4,64,2048]{2,1,0:T(8,128)(2,1)} %bitcast.61), calls=%async_computation.1 | async-start | bytes 2097152 | tf_op jit(solution)/shard_map/all_to_all | solution.py:104
  57.8 72.1 %all-to-all-start.2 = ((bf16[128,160,128]{2,1,0:T(8,128)(2,1)}), bf16[128,160,128]{2,1,0:T(8,128)(2,1)}, u32[]{:S(2)}, u32[]{:S(2)}) async-start(bf16[128,160,128]{2,1,0:T(8,128)(2,1)} %bitcast.59), calls=%async_computation.2 | async-start | bytes 10485760 | tf_op jit(solution)/shard_map/all_to_all | solution.py:130
  151.7 7.3 %copy-start.5 = (f32[64,8]{0,1:T(8,128)S(1)}, f32[64,8]{0,1:T(8,128)}, u32[]{:S(2)}) copy-start(f32[64,8]{0,1:T(8,128)} %param.19) | copy-start | bytes 6148
  151.7 68.4 %all-to-all-start.3 = ((bf16[128,160,128]{2,1,0:T(8,128)(2,1)}), bf16[128,160,128]{2,1,0:T(8,128)(2,1)}, u32[]{:S(2)}, u32[]{:S(2)}) async-start(bf16[128,160,128]{2,1,0:T(8,128)(2,1)} %reshape.202), calls=%async_computation.3 | async-start | bytes 10485760 | tf_op jit(solution)/shard_map/all_to_all | solution.py:141
